TPU v7x, 128 devices: a whole 4x4x4 slice. The times are simulated.
128 devices in a mesh: tok: 8 (over z, core), wid: 16 (over y, x).
Axes of the slice: x: 4, y: 4, z: 4, core: 2. Of those that a mesh axis runs over, the one named last changes fastest.
Arguments:
- tokens: bfloat16 [8192, 3072], P('tok', 'wid'), may hold values from -6 to 6
- defect_mask: int32 [8192], P('tok'), may hold values 0 or 1
- timestep: int32 [1], replicated, may hold values from 0 to 999
- mask_embed: bfloat16 [3072], P('wid'), may hold values from -6 to 6
- mod_weight: bfloat16 [256, 3, 3072], P(None, None, 'wid'), may hold values from -0.375 to 0.375
- w_qkv: bfloat16 [3072, 3, 2048], P('tok', None, 'wid'), may hold values from -1.4614179 to 1.4614179, as said below
- w_out: bfloat16 [2048, 3072], P('wid'), may hold values from -0.125 to 0.125
Outputs:
- block_out: bfloat16 [8192, 3072], P('tok', 'wid')
Inputs may be any that keep to these rules, and one draw needn't show every extreme that they name: `w_qkv`: entries are at most 81 / sqrt(3072) in magnitude.
All inputs are finite; a program needn't handle non-finite values. No bound on the sum of `defect_mask` on one device may be relied on, other than what follows from the above.
Results may differ from a plain program's by a relative error of at most 0.011.
Values may be sent and summed in bfloat16 or wider, within the bound.
No kernel may reach another device: no remote copies, remote signals or barrier semaphores. Data moves between devices by JAX's collectives and lax.ppermute only.
A program may use at most 128 MiB of HBM per device.

v0:
```python
import math

import jax
import jax.numpy as jnp
from jax import lax
from jax.sharding import PartitionSpec as P

D = 3072
DH = 128
TEMB = 256


def finish_rows(values, row_mean, row_var, shift_row, scale_row):
    normal = (values - row_mean) * lax.rsqrt(row_var + 1e-06)
    return (normal * (1.0 + scale_row.astype(jnp.float32)) + shift_row.astype(jnp.float32)).astype(
        jnp.bfloat16
    )


def body(tokens, defect_mask, timestep, mask_embed, mod_weight, w_qkv, w_out):
    tok_rows = tokens.shape[0]
    residual_in = (
        tokens.astype(jnp.float32)
        + defect_mask.astype(jnp.float32)[:, None] * mask_embed.astype(jnp.float32)[None, :]
    ).astype(jnp.bfloat16)
    half_width = TEMB // 2
    frequency = jnp.exp(-math.log(10000.0) * jnp.arange(half_width, dtype=jnp.float32) / half_width)
    angles = timestep.astype(jnp.float32)[0] * frequency
    embedding = jnp.concatenate([jnp.cos(angles), jnp.sin(angles)])
    modulation = jnp.einsum(
        "e,ecf->cf",
        jax.nn.silu(embedding),
        mod_weight.astype(jnp.float32),
        precision=lax.Precision.HIGHEST,
    ).astype(jnp.bfloat16)
    values = residual_in.astype(jnp.float32)
    row_total, square_total = lax.psum(
        (jnp.sum(values, axis=1), jnp.sum(values * values, axis=1)), "wid"
    )
    row_mean = (row_total / D)[:, None]
    row_var = (square_total / D)[:, None] - row_mean * row_mean
    normed_part = finish_rows(
        values, row_mean, row_var, modulation[0][None, :], modulation[1][None, :]
    )
    normed = lax.all_gather(normed_part, "wid", axis=1, tiled=True)
    local_width = w_qkv.shape[2]
    heads_here = local_width // DH
    qkv = jnp.einsum(
        "td,dcf->tcf",
        normed,
        lax.all_gather(w_qkv, "tok", axis=0, tiled=True),
        preferred_element_type=jnp.float32,
    ).astype(jnp.bfloat16)
    queries = qkv[:, 0].reshape(tok_rows, heads_here, DH)
    key_values = (qkv[:, 1], qkv[:, 2])
    score_scale = DH ** (-0.5)
    run_max = jnp.full((heads_here, tok_rows), -1e30, jnp.float32)
    accumulated = jnp.zeros((tok_rows, heads_here, DH), jnp.float32)
    key_part = lax.all_gather(key_values[0], "tok", axis=0, tiled=True)
    value_part = lax.all_gather(key_values[1], "tok", axis=0, tiled=True)
    count = key_part.shape[0]
    key_heads = key_part.reshape(count, heads_here, DH)
    value_heads = value_part.reshape(count, heads_here, DH)
    scores = (
        jnp.einsum("qhd,khd->hqk", queries, key_heads, preferred_element_type=jnp.float32)
        * score_scale
    )
    new_max = jnp.maximum(run_max, jnp.max(scores, axis=2))
    correction = jnp.exp(run_max - new_max)
    shifted = jnp.exp(scores - new_max[:, :, None])
    new_sum = jnp.sum(shifted, axis=2)
    update = jnp.einsum(
        "hqk,khd->qhd",
        shifted.astype(jnp.bfloat16),
        value_heads,
        preferred_element_type=jnp.float32,
    )
    new_acc = accumulated * correction.T[:, :, None] + update
    attended = (new_acc / new_sum.T[:, :, None]).reshape(tok_rows, local_width).astype(jnp.bfloat16)
    partial_terms = jnp.dot(attended, w_out, preferred_element_type=jnp.float32)
    projected = lax.psum_scatter(
        partial_terms.astype(jnp.bfloat16), "wid", scatter_dimension=1, tiled=True
    ).astype(jnp.float32)
    return (
        residual_in.astype(jnp.float32) + modulation[2].astype(jnp.float32)[None, :] * projected
    ).astype(jnp.bfloat16)


def solution(mesh):
    return jax.shard_map(
        body,
        mesh=mesh,
        in_specs=(
            P("tok", "wid"),
            P("tok"),
            P(),
            P("wid"),
            P(None, None, "wid"),
            P("tok", None, "wid"),
            P("wid", None),
        ),
        out_specs=P("tok", "wid"),
        check_vma=False,
    )
```

profile of v0, /device:TPU:1, one launch (start us, length us, event | category | flops | bytes accessed | tf_op | source)
XLA Modules:
  0.0 284.9 jit_solution(1973260607449243496)
XLA Ops:
  6.5 0.7 all-gather.9.cloned.1.call-update
  7.3 0.0 all-gather.7.cloned.1.call-start
  7.3 0.7 convert_element_type.58
  8.0 0.7 convert_element_type.59
  9.4 1.3 fusion.48
  10.7 1.3 convert_reduce_fusion
  12.0 34.8 %all-reduce = (f32[1024]{0:T(1024)S(1)}, f32[1024]{0:T(1024)S(1)}) all-reduce(f32[1024]{0:T(1024)S(1)} %get-tuple-element.6, f32[1024]{0:T(1024)S(1)} %get-tuple-element.5), channel_id=1, replica_groups=mesh['tok'=8,'wid'=16] {'wid'}, use_global_device_ids=true, to_apply=%region_3.4 | all-reduce | flops 2048 | bytes 16384 | tf_op jit(solution)/shard_map/psum | solution.py:37
  46.8 2.0 fusion.40
  48.8 0.0 all-gather.11.cloned.1.call-start
  48.9 0.0 all-gather.9.cloned.1.call-done
  48.9 65.6 %all-gather.7.cloned.1.call-done = bf16[1024,3072]{0,1:T(8,128)(2,1)} async-done(((bf16[1024,192]{0,1:T(8,128)(2,1)}), bf16[1024,3072]{0,1:T(8,128)(2,1)}) %all-gather.7.cloned.1.call-update) | async-done | bytes 6291472 | tf_op jit(solution)/shard_map/all_gather | solution.py:45
  114.5 6.9 %fusion.9 = bf16[1024,3,128]{2,0,1:T(8,128)(2,1)S(1)} fusion(bf16[3072,3,128]{2,0,1:T(8,128)(2,1)} %all-gather.9.cloned.1.call-done, bf16[1024,3072]{0,1:T(8,128)(2,1)} %all-gather.7.cloned.1.call-done), kind=kOutput, calls=%fused_computation.11 | convolution fusion | flops 2416312320 | bytes 9437184 | tf_op jit(solution)/shard_map/td,dcf->tcf/dot_general | solution.py:48
  121.4 0.8 fusion.47
  122.2 0.0 all-gather.13.cloned.1.call-start
  122.3 0.5 all-gather.13.cloned.1.call-update
  122.8 0.2 reduce-scatter.2.cloned.1.call-start
  123.1 25.1 %all-gather.11.cloned.1.call-done = bf16[8192,1,128]{2,0,1:T(8,128)(2,1)} async-done(((bf16[1024,1,128]{2,0,1:T(8,128)(2,1)}), bf16[8192,1,128]{2,0,1:T(8,128)(2,1)}) %all-gather.11.cloned.1.call-update) | async-done | bytes 2097168 | tf_op jit(solution)/shard_map/all_gather | solution.py:59
  148.2 15.1 %multiply_reduce_fusion = (f32[1024]{0:T(1024)S(1)}, f32[1024,8192]{1,0:T(8,128)}) fusion(bf16[8192,1,128]{2,0,1:T(8,128)(2,1)} %all-gather.11.cloned.1.call-done, bf16[1024,3,128]{2,0,1:T(8,128)(2,1)S(1)} %fusion.9), kind=kOutput, calls=%fused_computation.1 | convolution fusion | flops 2164259840 | bytes 35917824 | tf_op jit(solution)/shard_map/qhd,khd->hqk/dot_general | solution.py:65
  163.3 14.3 %fusion = f32[1024]{0:T(1024)S(1)} fusion(f32[1024,8192]{1,0:T(8,128)} %get-tuple-element.18, f32[1024]{0:T(1024)S(1)} %get-tuple-element.12), kind=kLoop, calls=%fused_computation.2 | loop fusion | flops 25164800 | bytes 33562624 | tf_op jit(solution)/shard_map/reduce_sum | solution.py:71
  177.6 0.0 all-gather.13.cloned.1.call-done
  177.6 14.2 %fusion.32 = bf16[1024,128]{0,1:T(8,128)(2,1)S(1)} fusion(f32[1024,8192]{1,0:T(8,128)} %get-tuple-element.18, f32[1024]{0:T(1024)S(1)} %get-tuple-element.12, bf16[8192,1,128]{2,0,1:T(8,128)(2,1)} %all-gather.13.cloned.1.call-done, f32[1024]{0:T(1024)S(1)} %fusion, f32[1024]{0:T(1024)S(1)} %get-tuple-element.11), kind=kOutput, calls=%fused_computation.20 | convolution fusion | flops 2173042688 | bytes 35926016 | tf_op jit(solution)/shard_map/hqk,khd->qhd/dot_general | solution.py:72
  191.9 4.5 %convolution_convert_fusion = bf16[1024,3072]{0,1:T(8,128)(2,1)} fusion(bf16[1024,128]{0,1:T(8,128)(2,1)S(1)} %fusion.32, bf16[128,3072]{1,0:T(8,128)(2,1)S(1)} %copy-done), kind=kOutput, calls=%fused_computation.7 | convolution fusion | flops 808452096 | bytes 7340032 | tf_op jit(solution)/shard_map/dot_general | solution.py:80
  196.4 79.9 %reduce-scatter.2.cloned.1.call-done = bf16[1024,192]{0,1:T(8,128)(2,1)} async-done(((bf16[1024,3072]{0,1:T(8,128)(2,1)}), bf16[1024,192]{0,1:T(8,128)(2,1)}) %reduce-scatter.2.cloned.1.call-update) | async-done | bytes 393232 | tf_op jit(solution)/shard_map/reduce_scatter | solution.py:81
  276.3 2.0 fusion.42
  (15 shorter events, 0.2 us)
Async XLA Ops:
  6.5 185.3 %copy-start = (bf16[128,3072]{1,0:T(8,128)(2,1)S(1)}, bf16[128,3072]{1,0:T(8,128)(2,1)}, u32[]{:S(2)}) copy-start(bf16[128,3072]{1,0:T(8,128)(2,1)} %param.13) | copy-start | bytes 2359300
  6.5 42.4 %all-gather.9.cloned.1.call-start = ((), (), s32[]{:S(2)}) async-start(), calls=%async_computation.2 | async-start | bytes 2654208 | tf_op jit(solution)/shard_map/all_gather | solution.py:51
  7.3 107.2 %all-gather.7.cloned.1.call-start = ((), (), s32[]{:S(2)}) async-start(), calls=%async_computation.1 | async-start | bytes 6684672 | tf_op jit(solution)/shard_map/all_gather | solution.py:45
  48.8 99.4 %all-gather.11.cloned.1.call-start = ((), (), s32[]{:S(2)}) async-start(), calls=%async_computation.4 | async-start | bytes 2359296 | tf_op jit(solution)/shard_map/all_gather | solution.py:59
  122.2 55.3 %all-gather.13.cloned.1.call-start = ((), (), s32[]{:S(2)}) async-start(), calls=%async_computation.5 | async-start | bytes 2359296 | tf_op jit(solution)/shard_map/all_gather | solution.py:60
  122.8 153.5 %reduce-scatter.2.cloned.1.call-start = ((), (), s32[]{:S(2)}) async-start(), calls=%async_computation.3 | async-start | bytes 6684672 | tf_op jit(solution)/shard_map/reduce_scatter | solution.py:81
  191.8 84.4 %copy-start.1 = (bf16[1024,192]{0,1:T(8,128)(2,1)S(1)}, bf16[1024,192]{0,1:T(8,128)(2,1)}, u32[]{:S(2)}) copy-start(bf16[1024,192]{0,1:T(8,128)(2,1)} %param.7) | copy-start | bytes 1179652
Sparse Core Ops, SparseCore 0:
  9.0 29.3 all-gather.8
  48.9 65.4 all-gather.6
  122.4 25.7 all-gather.10
  149.8 25.7 all-gather.12
  196.5 79.7 reduce-scatter.1
where the time goes:
time: 286 us; the launch traced here: 285 us
  waiting for transfers between devices  172 us (60%)
  matrix products  42 us (15%)
  blocking collectives  34.8 us (12%)
  other arithmetic  21.1 us (7%)
  between operations  13.9 us (5%)
    reduce_scatter x1, waiting for transfers between devices, body(): lax.psum_scatter(partial_terms.astype(jnp.bfloat16), 'wid', scatter_dimen...  79.9 us
    all_gather x1, waiting for transfers between devices, body(): normed = lax.all_gather(normed_part, 'wid', axis=1, tiled=True)  65.6 us
    psum x1, blocking collectives, body(): lax.psum((jnp.sum(values, axis=1), jnp.sum(values * values, axis=1)), 'wid')  34.8 us
    all_gather x1, waiting for transfers between devices, body(): key_part = lax.all_gather(key_values[0], 'tok', axis=0, tiled=True)  25.1 us
    dot_general x1, matrix products, body(): jnp.einsum('qhd,khd->hqk', queries, key_heads, preferred_element_type=jnp...  15.1 us
    reduce_sum x1, other arithmetic, body(): new_sum = jnp.sum(shifted, axis=2)  14.3 us
    dot_general x1, matrix products, body(): jnp.einsum('hqk,khd->qhd', shifted.astype(jnp.bfloat16), value_heads, pre...  14.2 us
    dot_general x1, matrix products, body(): jnp.einsum('td,dcf->tcf', normed, lax.all_gather(w_qkv, 'tok', axis=0, ti...  6.92 us
  transfers between devices with their start and end apart: 5, of which 3 were waited for; matrix products, arithmetic and copies ran while one was open for 12% of the time, Pallas kernels for 0%

commit v1 on v0

v1 whole, which is shorter than its diff:
```python
import math

import jax
import jax.numpy as jnp
from jax import lax
from jax.sharding import PartitionSpec as P

D = 3072
DH = 128
TEMB = 256


def finish_rows(values, row_mean, row_var, shift_row, scale_row):
    normal = (values - row_mean) * lax.rsqrt(row_var + 1e-06)
    return (normal * (1.0 + scale_row.astype(jnp.float32)) + shift_row.astype(jnp.float32)).astype(
        jnp.bfloat16
    )


def body(tokens, defect_mask, timestep, mask_embed, mod_weight, w_qkv, w_out):
    tok_rows = tokens.shape[0]
    residual_in = (
        tokens.astype(jnp.float32)
        + defect_mask.astype(jnp.float32)[:, None] * mask_embed.astype(jnp.float32)[None, :]
    ).astype(jnp.bfloat16)
    w_cols = lax.all_to_all(w_out, "wid", split_axis=1, concat_axis=0, tiled=True)
    w_full = lax.all_gather(w_qkv, "tok", axis=0, tiled=True)
    residual_full = lax.all_gather(residual_in, "wid", axis=1, tiled=True)
    half_width = TEMB // 2
    frequency = jnp.exp(-math.log(10000.0) * jnp.arange(half_width, dtype=jnp.float32) / half_width)
    angles = timestep.astype(jnp.float32)[0] * frequency
    embedding = jnp.concatenate([jnp.cos(angles), jnp.sin(angles)])
    modulation = jnp.einsum(
        "e,ecf->cf",
        jax.nn.silu(embedding),
        mod_weight.astype(jnp.float32),
        precision=lax.Precision.HIGHEST,
    ).astype(jnp.bfloat16)
    shift_scale = lax.all_gather(modulation[:2], "wid", axis=1, tiled=True)
    values = residual_full.astype(jnp.float32)
    row_mean = jnp.mean(values, axis=1, keepdims=True)
    row_var = jnp.mean(values * values, axis=1, keepdims=True) - row_mean * row_mean
    normed = finish_rows(values, row_mean, row_var, shift_scale[0][None, :], shift_scale[1][None, :])
    qkv = jnp.einsum(
        "td,dcf->tcf",
        normed,
        w_full,
        preferred_element_type=jnp.float32,
    ).astype(jnp.bfloat16)
    queries = qkv[:, 0]
    key_values = lax.all_gather(qkv[:, 1:3], "tok", axis=0, tiled=True)
    key_part = key_values[:, 0]
    value_part = key_values[:, 1]
    score_scale = DH ** (-0.5)
    scores = jnp.dot(queries, key_part.T, preferred_element_type=jnp.float32) * score_scale
    shifted = jnp.exp(scores - jnp.max(scores, axis=1, keepdims=True))
    row_sum = jnp.sum(shifted, axis=1, keepdims=True)
    numer = jnp.dot(shifted.astype(jnp.bfloat16), value_part, preferred_element_type=jnp.float32)
    attended = (numer / row_sum).astype(jnp.bfloat16)
    attended_full = lax.all_gather(attended, "wid", axis=1, tiled=True)
    projected = jnp.dot(attended_full, w_cols, preferred_element_type=jnp.float32)
    return (
        residual_in.astype(jnp.float32) + modulation[2].astype(jnp.float32)[None, :] * projected
    ).astype(jnp.bfloat16)


def solution(mesh):
    return jax.shard_map(
        body,
        mesh=mesh,
        in_specs=(
            P("tok", "wid"),
            P("tok"),
            P(),
            P("wid"),
            P(None, None, "wid"),
            P("tok", None, "wid"),
            P("wid", None),
        ),
        out_specs=P("tok", "wid"),
        check_vma=False,
    )
```

time: 286 us -> 258 us (0.902)
  waiting for transfers between devices: 172 us -> 152 us
  blocking collectives: 34.8 us -> 19.5 us
  starting transfers between devices: 0.34 us -> 6.83 us
    reduce_scatter x1 -> x0, waiting for transfers between devices: 79.9 us -> none  [body(): lax.psum_scatter(partial_terms.astype(jnp.bfloat16), 'wid', scatter_dimen...]
    all_gather x4, waiting for transfers between devices: 90.8 us -> 135 us  [the longest x1 42.8 us: body(): residual_full = lax.all_gather(residual_in, 'wid', axis=1, tiled=True)]
    psum x1 -> x0, blocking collectives: 34.8 us -> none  [body(): lax.psum((jnp.sum(values, axis=1), jnp.sum(values * values, axis=1)), 'wid')]
    all_gather x0 -> x1, blocking collectives: none -> 19.5 us  [body(): shift_scale = lax.all_gather(modulation[:2], 'wid', axis=1, tiled=True)]
    all_to_all x0 -> x1, waiting for transfers between devices: none -> 15.9 us  [body(): lax.all_to_all(w_out, 'wid', split_axis=1, concat_axis=0, tiled=True)]
    all_to_all x0 -> x1, starting transfers between devices: none -> 6.53 us  [body(): lax.all_to_all(w_out, 'wid', split_axis=1, concat_axis=0, tiled=True)]
    reduce_sum x2, other arithmetic: 15.6 us -> 18.7 us  [the longest x1 14.3 us: body(): row_sum = jnp.sum(shifted, axis=1, keepdims=True)]
  transfers between devices with their start and end apart: 5 -> 5, of which waited for: 3 -> 5; matrix products, arithmetic and copies ran while one was open for 12% -> 2% of each run, Pallas kernels for 0% -> 0%
where the time goes in v1:
time: 258 us; the launch traced here: 257 us
  waiting for transfers between devices  152 us (59%)
  matrix products  40.9 us (16%)
  other arithmetic  22.1 us (9%)
  blocking collectives  19.5 us (8%)
  between operations  13.9 us (5%)
  starting transfers between devices  6.83 us (3%)
    all_gather x1, waiting for transfers between devices, body(): residual_full = lax.all_gather(residual_in, 'wid', axis=1, tiled=True)  42.8 us
    all_gather x1, waiting for transfers between devices, body(): attended_full = lax.all_gather(attended, 'wid', axis=1, tiled=True)  36.2 us
    all_gather x1, waiting for transfers between devices, body(): key_values = lax.all_gather(qkv[:, 1:3], 'tok', axis=0, tiled=True)  32.7 us
    all_gather x1, waiting for transfers between devices, body(): w_full = lax.all_gather(w_qkv, 'tok', axis=0, tiled=True)  23.3 us
    all_gather x1, blocking collectives, body(): shift_scale = lax.all_gather(modulation[:2], 'wid', axis=1, tiled=True)  19.5 us
    all_to_all x1, waiting for transfers between devices, body(): lax.all_to_all(w_out, 'wid', split_axis=1, concat_axis=0, tiled=True)  15.9 us
    dot_general x1, matrix products, body(): jnp.dot(queries, key_part.T, preferred_element_type=jnp.float32)  14.7 us
    reduce_sum x1, other arithmetic, body(): row_sum = jnp.sum(shifted, axis=1, keepdims=True)  14.3 us
  transfers between devices with their start and end apart: 5, of which 5 were waited for; matrix products, arithmetic and copies ran while one was open for 2% of the time, Pallas kernels for 0%

profile of v1, /device:TPU:1, one launch (start us, length us, event | category | flops | bytes accessed | tf_op | source)
XLA Modules:
  0.0 257.0 jit_solution(2055310667974810968)
XLA Ops:
  6.5 0.7 convert_element_type.47
  7.3 0.7 convert_element_type.48
  7.9 1.9 add_convert_fusion
  9.9 0.0 all-gather.8.cloned.1.call-start
  9.9 0.7 all-gather.8.cloned.1.call-update
  10.6 0.0 all-gather.10.cloned.1.call-start
  11.4 0.3 fusion.30
  11.8 19.5 %all-gather = bf16[16,192,2]{1,2,0:T(2,128)(2,1)S(1)} all-gather(bf16[1,192,2]{1,2,0:T(2,128)(2,1)S(1)} %slice_bitcast_fusion.10), channel_id=1, replica_groups=mesh['tok'=8,'wid'=16] {'wid'}, dimensions={0}, use_global_device_ids=true | all-gather | bytes 13056 | tf_op jit(solution)/shard_map/all_gather | solution.py:39
  31.2 0.1 reshape.28
  31.4 42.8 %all-gather.6.cloned.1.call-done = bf16[1024,3072]{0,1:T(8,128)(2,1)} async-done(((bf16[1024,192]{0,1:T(8,128)(2,1)}), bf16[1024,3072]{0,1:T(8,128)(2,1)}) %all-gather.6.cloned.1.call-update) | async-done | bytes 6291472 | tf_op jit(solution)/shard_map/all_gather | solution.py:28
  74.2 4.5 %convert_reduce_fusion = (f32[1024]{0:T(1024)S(1)}, f32[1024]{0:T(1024)S(1)}) fusion(bf16[1024,3072]{0,1:T(8,128)(2,1)} %all-gather.6.cloned.1.call-done), kind=kLoop, calls=%fused_computation.6 | loop fusion | flops 12580864 | bytes 6299648 | tf_op jit(solution)/shard_map/reduce_sum | solution.py:41
  78.7 23.3 %all-gather.8.cloned.1.call-done = bf16[3072,3,128]{2,0,1:T(8,128)(2,1)} async-done(((bf16[384,3,128]{2,0,1:T(8,128)(2,1)}), bf16[3072,3,128]{2,0,1:T(8,128)(2,1)}) %all-gather.8.cloned.1.call-update) | async-done | bytes 2359312 | tf_op jit(solution)/shard_map/all_gather | solution.py:27
  102.0 7.2 %fusion.13 = bf16[1024,3,128]{2,0,1:T(8,128)(2,1)S(1)} fusion(bf16[3072,3,128]{2,0,1:T(8,128)(2,1)} %all-gather.8.cloned.1.call-done, bf16[1024,3072]{0,1:T(8,128)(2,1)} %all-gather.6.cloned.1.call-done, f32[3072]{0:T(1024)S(1)} %bitcast.53, f32[3072]{0:T(1024)S(1)} %bitcast.52, f32[1024]{0:T(1024)S(1)} %get-tuple-element.8, f32[1024]{0:T(1024)S(1)} %get-tuple-element.7), kind=kOutput, calls=%fused_computation.18 | convolution fusion | flops 2435186688 | bytes 9469952 | tf_op jit(solution)/shard_map/td,dcf->tcf/dot_general | solution.py:44
  109.2 0.8 slice.37
  110.1 0.2 all-gather.12.cloned.1.call-start
  110.3 32.7 %all-gather.10.cloned.1.call-done = bf16[8192,2,128]{2,0,1:T(8,128)(2,1)} async-done(((bf16[1024,2,128]{2,0,1:T(8,128)(2,1)}), bf16[8192,2,128]{2,0,1:T(8,128)(2,1)}) %all-gather.10.cloned.1.call-update) | async-done | bytes 4194320 | tf_op jit(solution)/shard_map/all_gather | solution.py:51
  143.0 14.7 %multiply_reduce_fusion = (f32[1024]{0:T(1024)S(1)}, f32[1024,8192]{1,0:T(8,128)}) fusion(bf16[8192,2,128]{2,0,1:T(8,128)(2,1)} %all-gather.10.cloned.1.call-done, bf16[1024,3,128]{2,0,1:T(8,128)(2,1)S(1)} %fusion.13), kind=kOutput, calls=%fused_computation.1 | convolution fusion | flops 2164259840 | bytes 35917824 | tf_op jit(solution)/shard_map/dot_general | solution.py:55
  157.7 14.3 %fusion = f32[1024]{0:T(1024)S(1)} fusion(f32[1024,8192]{1,0:T(8,128)} %get-tuple-element.10, f32[1024]{0:T(1024)S(1)} %get-tuple-element.9), kind=kLoop, calls=%fused_computation.2 | loop fusion | flops 25164800 | bytes 33562624 | tf_op jit(solution)/shard_map/reduce_sum | solution.py:57
  172.0 14.2 %fusion.21 = bf16[1024,128]{1,0:T(8,128)(2,1)} fusion(bf16[8192,2,128]{2,0,1:T(8,128)(2,1)S(1)} %copy-done.2, f32[1024,8192]{1,0:T(8,128)} %get-tuple-element.10, f32[1024]{0:T(1024)S(1)} %get-tuple-element.9, f32[1024]{0:T(1024)S(1)} %fusion), kind=kOutput, calls=%fused_computation.23 | convolution fusion | flops 2172911616 | bytes 35921920 | tf_op jit(solution)/shard_map/dot_general | solution.py:58
  186.2 1.2 copy.18
  187.3 6.5 %all-to-all-start = ((bf16[128,16,192]{0,2,1:T(8,128)(2,1)}), bf16[128,16,192]{0,2,1:T(8,128)(2,1)S(1)}, u32[]{:S(2)}, u32[]{:S(2)}) async-start(bf16[128,16,192]{0,2,1:T(8,128)(2,1)} %bitcast.13), calls=%async_computation | async-start | bytes 1572864 | tf_op jit(solution)/shard_map/all_to_all | solution.py:26
  193.9 15.9 %all-to-all-done = bf16[128,16,192]{0,2,1:T(8,128)(2,1)S(1)} async-done(((bf16[128,16,192]{0,2,1:T(8,128)(2,1)}), bf16[128,16,192]{0,2,1:T(8,128)(2,1)S(1)}, u32[]{:S(2)}, u32[]{:S(2)}) %all-to-all-start) | async-done | bytes 786464 | tf_op jit(solution)/shard_map/all_to_all | solution.py:26
  209.8 36.2 %all-gather.12.cloned.1.call-done = bf16[1024,2048]{1,0:T(8,128)(2,1)} async-done(((bf16[1024,128]{1,0:T(8,128)(2,1)}), bf16[1024,2048]{1,0:T(8,128)(2,1)}) %all-gather.12.cloned.1.call-update) | async-done | bytes 4194320 | tf_op jit(solution)/shard_map/all_gather | solution.py:60
  246.0 4.5 %fusion.17 = bf16[1024,192]{0,1:T(8,128)(2,1)} fusion(bf16[1024,2048]{1,0:T(8,128)(2,1)} %all-gather.12.cloned.1.call-done, bf16[1024,192]{0,1:T(8,128)(2,1)S(1)} %copy-done.1, f32[192]{0:T(256)S(1)} %bitcast.57, bf16[128,16,192]{0,2,1:T(8,128)(2,1)S(1)} %all-to-all-done), kind=kOutput, calls=%fused_computation.21 | convolution fusion | flops 806092800 | bytes 5767936 | tf_op jit(solution)/shard_map/dot_general | solution.py:61
  (21 shorter events, 0.2 us)
Async XLA Ops:
  6.5 4.8 %copy-start = (bf16[256,3,192]{0,2,1:T(8,128)(2,1)S(1)}, bf16[256,3,192]{0,2,1:T(8,128)(2,1)}, u32[]{:S(2)}) copy-start(bf16[256,3,192]{0,2,1:T(8,128)(2,1)} %param.11) | copy-start | bytes 884740
  6.5 67.7 %all-gather.6.cloned.1.call-start = ((), (), s32[]{:S(2)}) async-start(), calls=%async_computation.1 | async-start | bytes 6684672 | tf_op jit(solution)/shard_map/all_gather | solution.py:28
  9.9 92.2 %all-gather.8.cloned.1.call-start = ((), (), s32[]{:S(2)}) async-start(), calls=%async_computation.2 | async-start | bytes 2654208 | tf_op jit(solution)/shard_map/all_gather | solution.py:27
  10.6 132.4 %all-gather.10.cloned.1.call-start = ((), (), s32[]{:S(2)}) async-start(), calls=%async_computation.3 | async-start | bytes 4718592 | tf_op jit(solution)/shard_map/all_gather | solution.py:51
  110.1 135.9 %all-gather.12.cloned.1.call-start = ((), (), s32[]{:S(2)}) async-start(), calls=%async_computation.4 | async-start | bytes 4456448 | tf_op jit(solution)/shard_map/all_gather | solution.py:60
  157.7 14.3 %copy-start.2 = (bf16[8192,2,128]{2,0,1:T(8,128)(2,1)S(1)}, bf16[8192,2,128]{2,0,1:T(8,128)(2,1)}, u32[]{:S(2)}) copy-start(bf16[8192,2,128]{2,0,1:T(8,128)(2,1)} %all-gather.10.cloned.1.call-done) | copy-start | bytes 12582916
  171.9 14.2 %copy-start.3 = (bf16[128,3072]{1,0:T(8,128)(2,1)S(1)}, bf16[128,3072]{1,0:T(8,128)(2,1)}, u32[]{:S(2)}) copy-start(bf16[128,3072]{1,0:T(8,128)(2,1)} %param.13) | copy-start | bytes 2359300
  171.9 74.1 %copy-start.1 = (bf16[1024,192]{0,1:T(8,128)(2,1)S(1)}, bf16[1024,192]{0,1:T(8,128)(2,1)}, u32[]{:S(2)}) copy-start(bf16[1024,192]{0,1:T(8,128)(2,1)} %add_convert_fusion) | copy-start | bytes 1179652
  187.3 22.5 %all-to-all-start = ((bf16[128,16,192]{0,2,1:T(8,128)(2,1)}), bf16[128,16,192]{0,2,1:T(8,128)(2,1)S(1)}, u32[]{:S(2)}, u32[]{:S(2)}) async-start(bf16[128,16,192]{0,2,1:T(8,128)(2,1)} %bitcast.13), calls=%async_computation | async-start | bytes 1572864 | tf_op jit(solution)/shard_map/all_to_all | solution.py:26
Sparse Core Ops, SparseCore 0:
  10.0 64.1 all-gather.5
  75.9 26.0 all-gather.7
  110.2 32.7 all-gather.9
  186.3 59.6 all-gather.11

commit v2 on v1

--- a/solution.py
+++ b/solution.py
@@ -24,8 +24,10 @@
         + defect_mask.astype(jnp.float32)[:, None] * mask_embed.astype(jnp.float32)[None, :]
     ).astype(jnp.bfloat16)
     w_cols = lax.all_to_all(w_out, "wid", split_axis=1, concat_axis=0, tiled=True)
-    w_full = lax.all_gather(w_qkv, "tok", axis=0, tiled=True)
-    residual_full = lax.all_gather(residual_in, "wid", axis=1, tiled=True)
+    tok_count = lax.axis_size("tok")
+    w_copies = jnp.broadcast_to(w_qkv[None], (tok_count,) + w_qkv.shape)
+    w_full = lax.all_to_all(w_copies, "tok", split_axis=0, concat_axis=0, tiled=True)
+    w_full = w_full.reshape((tok_count * w_qkv.shape[0],) + w_qkv.shape[1:])
     half_width = TEMB // 2
     frequency = jnp.exp(-math.log(10000.0) * jnp.arange(half_width, dtype=jnp.float32) / half_width)
     angles = timestep.astype(jnp.float32)[0] * frequency
@@ -36,7 +38,12 @@
         mod_weight.astype(jnp.float32),
         precision=lax.Precision.HIGHEST,
     ).astype(jnp.bfloat16)
-    shift_scale = lax.all_gather(modulation[:2], "wid", axis=1, tiled=True)
+    extra = jnp.zeros((16, residual_in.shape[1]), jnp.bfloat16).at[:2].set(modulation[:2])
+    packed = lax.all_gather(
+        jnp.concatenate([residual_in, extra], axis=0), "wid", axis=1, tiled=True
+    )
+    residual_full = packed[:tok_rows]
+    shift_scale = packed[tok_rows : tok_rows + 2]
     values = residual_full.astype(jnp.float32)
     row_mean = jnp.mean(values, axis=1, keepdims=True)
     row_var = jnp.mean(values * values, axis=1, keepdims=True) - row_mean * row_mean
@@ -47,6 +54,7 @@
         w_full,
         preferred_element_type=jnp.float32,
     ).astype(jnp.bfloat16)
+    qkv, w_cols = lax.optimization_barrier((qkv, w_cols))
     queries = qkv[:, 0]
     key_values = lax.all_gather(qkv[:, 1:3], "tok", axis=0, tiled=True)
     key_part = key_values[:, 0]

time: 258 us -> 240 us (0.930)
  waiting for transfers between devices: 152 us -> 119 us
  local copies, waits for them, and re-layouts: 2.14 us -> 8.83 us
  blocking collectives: 19.5 us -> 23.2 us
  starting transfers between devices: 6.83 us -> 10.1 us
  other arithmetic: 22.1 us -> 24.9 us
    all_gather x2 -> x1, waiting for transfers between devices: 66.1 us -> 3.36 us  [body(): lax.all_gather(jnp.concatenate([residual_in, extra], axis=0), 'wid', axis...]
    all_to_all x0 -> x1, blocking collectives: none -> 23.2 us  [body(): lax.all_to_all(w_out, 'wid', split_axis=1, concat_axis=0, tiled=True)]
    all_gather x1 -> x0, blocking collectives: 19.5 us -> none  [body(): shift_scale = lax.all_gather(modulation[:2], 'wid', axis=1, tiled=True)]
    all_gather x1, waiting for transfers between devices: 36.2 us -> 54.7 us  [body(): attended_full = lax.all_gather(attended, 'wid', axis=1, tiled=True)]
    all_to_all x1, waiting for transfers between devices: 15.9 us -> 28 us  [body(): lax.all_to_all(w_copies, 'tok', split_axis=0, concat_axis=0, tiled=True)]
    all_to_all x1, starting transfers between devices: 6.53 us -> 9.84 us  [body(): lax.all_to_all(w_copies, 'tok', split_axis=0, concat_axis=0, tiled=True)]
    broadcast_in_dim x0 -> x1, local copies, waits for them, and re-layouts: none -> 2.95 us  [body(): w_copies = jnp.broadcast_to(w_qkv[None], (tok_count,) + w_qkv.shape)]
    all_to_all x0 -> x2, local copies, waits for them, and re-layouts: none -> 2.62 us  [the longest x1 1.61 us: body(): lax.all_to_all(w_copies, 'tok', split_axis=0, concat_axis=0, tiled=True)]
  transfers between devices with their start and end apart: 5 -> 4, of which waited for: 5 -> 4; matrix products, arithmetic and copies ran while one was open for 2% -> 3% of each run, Pallas kernels for 0% -> 0%
where the time goes in v2:
time: 240 us; the launch traced here: 239 us
  waiting for transfers between devices  119 us (50%)
  matrix products  39.2 us (16%)
  other arithmetic  24.9 us (10%)
  blocking collectives  23.2 us (10%)
  between operations  13.9 us (6%)
  starting transfers between devices  10.1 us (4%)
  local copies, waits for them, and re-layouts  8.83 us (4%)
    all_gather x1, waiting for transfers between devices, body(): attended_full = lax.all_gather(attended, 'wid', axis=1, tiled=True)  54.7 us
    all_gather x1, waiting for transfers between devices, body(): key_values = lax.all_gather(qkv[:, 1:3], 'tok', axis=0, tiled=True)  32.5 us
    all_to_all x1, waiting for transfers between devices, body(): lax.all_to_all(w_copies, 'tok', split_axis=0, concat_axis=0, tiled=True)  28 us
    all_to_all x1, blocking collectives, body(): lax.all_to_all(w_out, 'wid', split_axis=1, concat_axis=0, tiled=True)  23.2 us
    dot_general x1, matrix products, body(): jnp.dot(queries, key_part.T, preferred_element_type=jnp.float32)  14.6 us
    reduce_sum x1, other arithmetic, body(): row_sum = jnp.sum(shifted, axis=1, keepdims=True)  14.3 us
    dot_general x1, matrix products, body(): jnp.dot(shifted.astype(jnp.bfloat16), value_part, preferred_element_type=...  14.2 us
    all_to_all x1, starting transfers between devices, body(): lax.all_to_all(w_copies, 'tok', split_axis=0, concat_axis=0, tiled=True)  9.84 us
  transfers between devices with their start and end apart: 4, of which 4 were waited for; matrix products, arithmetic and copies ran while one was open for 3% of the time, Pallas kernels for 0%

profile of v2, /device:TPU:1, one launch (start us, length us, event | category | flops | bytes accessed | tf_op | source)
XLA Modules:
  0.0 238.7 jit_solution(12590052405980159787)
XLA Ops:
  7.3 0.7 convert_element_type.48
  8.0 0.7 convert_element_type.47
  8.7 0.3 fusion.32
  9.2 1.2 add_convert_fusion
  10.4 0.7 copy-done.2
  11.1 0.8 fusion.26
  11.9 1.5 copy.14
  13.4 23.2 %all_to_all.24 = bf16[128,16,192]{0,2,1:T(8,128)(2,1)S(1)} all-to-all(bf16[128,16,192]{0,2,1:T(8,128)(2,1)S(1)} %bitcast.41), channel_id=1, replica_groups=mesh['tok'=8,'wid'=16] {'wid'}, dimensions={1} | all-to-all | bytes 1572864 | tf_op jit(solution)/shard_map/all_to_all | solution.py:26
  36.6 3.0 %broadcast_in_dim.2 = bf16[8,384,3,128]{3,1,2,0:T(8,128)(2,1)} broadcast(bf16[384,3,128]{2,0,1:T(8,128)(2,1)} %param.14), dimensions={1,2,3} | broadcast | bytes 2654208 | tf_op jit(solution)/shard_map/broadcast_in_dim | solution.py:28
  39.6 9.8 %all-to-all-start = ((bf16[8,384,3,128]{3,1,2,0:T(8,128)(2,1)}), bf16[8,384,3,128]{3,1,2,0:T(8,128)(2,1)S(1)}, u32[]{:S(2)}, u32[]{:S(2)}) async-start(bf16[8,384,3,128]{3,1,2,0:T(8,128)(2,1)} %broadcast_in_dim.2), calls=%async_computation | async-start | bytes 4718592 | tf_op jit(solution)/shard_map/all_to_all | solution.py:29
  49.4 1.0 copy_bitcast_fusion
  50.4 28.0 %all-to-all-done = bf16[8,384,3,128]{3,1,2,0:T(8,128)(2,1)S(1)} async-done(((bf16[8,384,3,128]{3,1,2,0:T(8,128)(2,1)}), bf16[8,384,3,128]{3,1,2,0:T(8,128)(2,1)S(1)}, u32[]{:S(2)}, u32[]{:S(2)}) %all-to-all-start) | async-done | bytes 2359328 | tf_op jit(solution)/shard_map/all_to_all | solution.py:29
  78.4 1.6 copy.12
  80.0 3.4 %all-gather.4.cloned.1.call-done = bf16[1040,3072]{0,1:T(8,128)(2,1)} async-done(((bf16[1040,192]{0,1:T(8,128)(2,1)}), bf16[1040,3072]{0,1:T(8,128)(2,1)}) %all-gather.4.cloned.1.call-update) | async-done | bytes 6389776 | tf_op jit(solution)/shard_map/all_gather | solution.py:42
  83.4 4.6 %convert_reduce_fusion = (f32[1024]{0:T(1024)S(1)}, f32[1024]{0:T(1024)S(1)}) fusion(bf16[1040,3072]{0,1:T(8,128)(2,1)} %all-gather.4.cloned.1.call-done), kind=kLoop, calls=%fused_computation.6 | loop fusion | flops 12580864 | bytes 6299648 | tf_op jit(solution)/shard_map/reduce_sum | solution.py:48
  88.0 2.5 %add_reduce_fusion = (f32[3072]{0:T(1024)S(1)}, f32[3072]{0:T(1024)S(1)}) fusion(bf16[1040,3072]{0,1:T(8,128)(2,1)} %all-gather.4.cloned.1.call-done), kind=kLoop, calls=%fused_computation.20 | loop fusion | flops 9216 | bytes 36864 | tf_op jit(solution)/shard_map/add | solution.py:15
  90.5 5.6 %fusion.14 = bf16[1024,3,128]{2,0,1:T(8,128)(2,1)S(1)} fusion(bf16[3072,3,128]{2,0,1:T(8,128)(2,1)} %bitcast.42, f32[3072]{0:T(1024)S(1)} %get-tuple-element.24, f32[3072]{0:T(1024)S(1)} %get-tuple-element.23, f32[1024]{0:T(1024)S(1)} %get-tuple-element.26, f32[1024]{0:T(1024)S(1)} %get-tuple-element.25, bf16[1040,3072]{0,1:T(8,128)(2,1)S(1)} %copy-done.1), kind=kOutput, calls=%fused_computation.21 | convolution fusion | flops 2435186688 | bytes 9469952 | tf_op jit(solution)/shard_map/td,dcf->tcf/dot_general | solution.py:51
  96.1 0.8 slice.52
  97.2 32.5 %all-gather.6.cloned.1.call-done = bf16[8192,2,128]{2,0,1:T(8,128)(2,1)} async-done(((bf16[1024,2,128]{2,0,1:T(8,128)(2,1)}), bf16[8192,2,128]{2,0,1:T(8,128)(2,1)}) %all-gather.6.cloned.1.call-update) | async-done | bytes 4194320 | tf_op jit(solution)/shard_map/all_gather | solution.py:59
  129.7 14.6 %multiply_reduce_fusion = (f32[1024]{0:T(1024)S(1)}, f32[1024,8192]{1,0:T(8,128)}) fusion(bf16[8192,2,128]{2,0,1:T(8,128)(2,1)} %all-gather.6.cloned.1.call-done, bf16[1024,3,128]{2,0,1:T(8,128)(2,1)S(1)} %fusion.14), kind=kOutput, calls=%fused_computation.1 | convolution fusion | flops 2164259840 | bytes 35917824 | tf_op jit(solution)/shard_map/dot_general | solution.py:63
  144.3 14.3 %fusion = f32[1024]{0:T(1024)S(1)} fusion(f32[1024,8192]{1,0:T(8,128)} %get-tuple-element.28, f32[1024]{0:T(1024)S(1)} %get-tuple-element.27), kind=kLoop, calls=%fused_computation.2 | loop fusion | flops 25164800 | bytes 33562624 | tf_op jit(solution)/shard_map/reduce_sum | solution.py:65
  158.6 14.2 %fusion.22 = bf16[1024,128]{1,0:T(8,128)(2,1)} fusion(bf16[8192,2,128]{2,0,1:T(8,128)(2,1)S(1)} %copy-done.4, f32[1024,8192]{1,0:T(8,128)} %get-tuple-element.28, f32[1024]{0:T(1024)S(1)} %get-tuple-element.27, f32[1024]{0:T(1024)S(1)} %fusion), kind=kOutput, calls=%fused_computation.26 | convolution fusion | flops 2172911616 | bytes 35921920 | tf_op jit(solution)/shard_map/dot_general | solution.py:66
  173.0 54.7 %all-gather.8.cloned.1.call-done = bf16[1024,2048]{1,0:T(8,128)(2,1)} async-done(((bf16[1024,128]{1,0:T(8,128)(2,1)}), bf16[1024,2048]{1,0:T(8,128)(2,1)}) %all-gather.8.cloned.1.call-update) | async-done | bytes 4194320 | tf_op jit(solution)/shard_map/all_gather | solution.py:68
  227.7 4.5 %fusion.18 = bf16[1024,192]{0,1:T(8,128)(2,1)} fusion(bf16[1024,2048]{1,0:T(8,128)(2,1)} %all-gather.8.cloned.1.call-done, bf16[2048,192]{0,1:T(8,128)(2,1)S(1)} %copy-done.5, bf16[1024,192]{0,1:T(8,128)(2,1)S(1)} %copy-done.3, f32[192]{0:T(256)S(1)} %convert_reduce_fusion.2), kind=kOutput, calls=%fused_computation.24 | convolution fusion | flops 806092800 | bytes 5767936 | tf_op jit(solution)/shard_map/dot_general | solution.py:69
  (22 shorter events, 0.7 us)
Async XLA Ops:
  6.5 2.1 copy-start
  6.5 76.9 %all-gather.4.cloned.1.call-start = ((), (), s32[]{:S(2)}) async-start(), calls=%async_computation.2 | async-start | bytes 7520256 | tf_op jit(solution)/shard_map/all_gather | solution.py:42
  10.4 0.7 copy-start.2
  39.6 38.9 %all-to-all-start = ((bf16[8,384,3,128]{3,1,2,0:T(8,128)(2,1)}), bf16[8,384,3,128]{3,1,2,0:T(8,128)(2,1)S(1)}, u32[]{:S(2)}, u32[]{:S(2)}) async-start(bf16[8,384,3,128]{3,1,2,0:T(8,128)(2,1)} %broadcast_in_dim.2), calls=%async_computation | async-start | bytes 4718592 | tf_op jit(solution)/shard_map/all_to_all | solution.py:29
  49.4 80.3 %all-gather.6.cloned.1.call-start = ((), (), s32[]{:S(2)}) async-start(), calls=%async_computation.3 | async-start | bytes 4718592 | tf_op jit(solution)/shard_map/all_gather | solution.py:59
  83.4 7.1 %copy-start.1 = (bf16[1040,3072]{0,1:T(8,128)(2,1)S(1)}, bf16[1040,3072]{0,1:T(8,128)(2,1)}, u32[]{:S(2)}) copy-start(bf16[1040,3072]{0,1:T(8,128)(2,1)} %all-gather.4.cloned.1.call-done) | copy-start | bytes 19169284
  97.0 130.7 %all-gather.8.cloned.1.call-start = ((), (), s32[]{:S(2)}) async-start(), calls=%async_computation.4 | async-start | bytes 4456448 | tf_op jit(solution)/shard_map/all_gather | solution.py:68
  144.3 14.3 %copy-start.4 = (bf16[8192,2,128]{2,0,1:T(8,128)(2,1)S(1)}, bf16[8192,2,128]{2,0,1:T(8,128)(2,1)}, u32[]{:S(2)}) copy-start(bf16[8192,2,128]{2,0,1:T(8,128)(2,1)} %all-gather.6.cloned.1.call-done) | copy-start | bytes 12582916
  158.6 69.1 %copy-start.3 = (bf16[1024,192]{0,1:T(8,128)(2,1)S(1)}, bf16[1024,192]{0,1:T(8,128)(2,1)}, u32[]{:S(2)}) copy-start(bf16[1024,192]{0,1:T(8,128)(2,1)} %copy-done.2) | copy-start | bytes 1179652
  158.6 69.1 %copy-start.5 = (bf16[2048,192]{0,1:T(8,128)(2,1)S(1)}, bf16[2048,192]{0,1:T(8,128)(2,1)}, u32[]{:S(2)}) copy-start(bf16[2048,192]{0,1:T(8,128)(2,1)} %copy_bitcast_fusion) | copy-start | bytes 2359300
Sparse Core Ops, SparseCore 0:
  12.1 71.2 all-gather.3
  97.1 32.5 all-gather.5
  172.9 54.6 all-gather.7

commit v3 on v2

--- a/solution.py
+++ b/solution.py
@@ -3,6 +3,8 @@
 import jax
 import jax.numpy as jnp
 from jax import lax
+from jax.experimental import pallas as pl
+from jax.experimental.pallas import tpu as pltpu
 from jax.sharding import PartitionSpec as P
 
 D = 3072
@@ -15,6 +17,39 @@
     return (normal * (1.0 + scale_row.astype(jnp.float32)) + shift_row.astype(jnp.float32)).astype(
         jnp.bfloat16
     )
+
+
+def attention_kernel(q_ref, kv_ref, o_ref):
+    keys = kv_ref[:, :DH]
+    values = kv_ref[:, DH:]
+    scores = lax.dot_general(
+        q_ref[...], keys, (((1,), (1,)), ((), ())), preferred_element_type=jnp.float32
+    ) * (DH ** (-0.5))
+    shifted = jnp.exp(scores - jnp.max(scores, axis=1, keepdims=True))
+    row_sum = jnp.sum(shifted, axis=1, keepdims=True)
+    numer = jnp.dot(shifted.astype(jnp.bfloat16), values, preferred_element_type=jnp.float32)
+    o_ref[...] = (numer / row_sum).astype(o_ref.dtype)
+
+
+def attention(queries, key_values, block=256):
+    rows = queries.shape[0]
+    count = key_values.shape[0]
+    return pl.pallas_call(
+        attention_kernel,
+        grid=(rows // block,),
+        in_specs=[
+            pl.BlockSpec((block, DH), lambda i: (i, 0)),
+            pl.BlockSpec((count, 2 * DH), lambda i: (0, 0)),
+        ],
+        out_specs=pl.BlockSpec((block, DH), lambda i: (i, 0)),
+        out_shape=jax.ShapeDtypeStruct((rows, DH), jnp.bfloat16),
+        compiler_params=pltpu.CompilerParams(vmem_limit_bytes=56 * 1024 * 1024),
+        cost_estimate=pl.CostEstimate(
+            flops=4 * rows * count * DH,
+            transcendentals=rows * count,
+            bytes_accessed=4 * rows * DH + 4 * count * DH,
+        ),
+    )(queries, key_values)
 
 
 def body(tokens, defect_mask, timestep, mask_embed, mod_weight, w_qkv, w_out):
@@ -56,15 +91,10 @@
     ).astype(jnp.bfloat16)
     qkv, w_cols = lax.optimization_barrier((qkv, w_cols))
     queries = qkv[:, 0]
-    key_values = lax.all_gather(qkv[:, 1:3], "tok", axis=0, tiled=True)
-    key_part = key_values[:, 0]
-    value_part = key_values[:, 1]
-    score_scale = DH ** (-0.5)
-    scores = jnp.dot(queries, key_part.T, preferred_element_type=jnp.float32) * score_scale
-    shifted = jnp.exp(scores - jnp.max(scores, axis=1, keepdims=True))
-    row_sum = jnp.sum(shifted, axis=1, keepdims=True)
-    numer = jnp.dot(shifted.astype(jnp.bfloat16), value_part, preferred_element_type=jnp.float32)
-    attended = (numer / row_sum).astype(jnp.bfloat16)
+    key_values = lax.all_gather(
+        qkv[:, 1:3].reshape(tok_rows, 2 * DH), "tok", axis=0, tiled=True
+    )
+    attended = attention(queries, key_values)
     attended_full = lax.all_gather(attended, "wid", axis=1, tiled=True)
     projected = jnp.dot(attended_full, w_cols, preferred_element_type=jnp.float32)
     return (

time: 240 us -> 216 us (0.900)
  matrix products: 39.2 us -> 10.4 us
  Pallas kernels: 0 us -> 18.9 us
  other arithmetic: 24.9 us -> 10.6 us
    dot_general x2 -> x0, matrix products: 28.8 us -> none  [the longest x1 14.6 us: body(): jnp.dot(queries, key_part.T, preferred_element_type=jnp.float32)]
    pallas_call x0 -> x1, Pallas kernels: none -> 18.9 us  [attention(): pl.pallas_call(attention_kernel, grid=(rows // block,), in_specs=[pl.Bloc...]
    reduce_sum x1 -> x0, other arithmetic: 14.3 us -> none  [body(): row_sum = jnp.sum(shifted, axis=1, keepdims=True)]
  transfers between devices with their start and end apart: 4 -> 4, of which waited for: 4 -> 4; matrix products, arithmetic and copies ran while one was open for 3% -> 4% of each run, Pallas kernels for 0% -> 0%
where the time goes in v3:
time: 216 us; the launch traced here: 215 us
  waiting for transfers between devices  118 us (55%)
  blocking collectives  23.2 us (11%)
  Pallas kernels  18.9 us (9%)
  between operations  13.9 us (6%)
  other arithmetic  10.6 us (5%)
  matrix products  10.4 us (5%)
  starting transfers between devices  10.1 us (5%)
  local copies, waits for them, and re-layouts  9.79 us (5%)
    all_gather x1, waiting for transfers between devices, body(): attended_full = lax.all_gather(attended, 'wid', axis=1, tiled=True)  54.7 us
    all_gather x1, waiting for transfers between devices, body(): lax.all_gather(qkv[:, 1:3].reshape(tok_rows, 2 * DH), 'tok', axis=0, tile...  31.7 us
    all_to_all x1, waiting for transfers between devices, body(): lax.all_to_all(w_copies, 'tok', split_axis=0, concat_axis=0, tiled=True)  28 us
    all_to_all x1, blocking collectives, body(): lax.all_to_all(w_out, 'wid', split_axis=1, concat_axis=0, tiled=True)  23.2 us
    pallas_call x1, Pallas kernels, attention(): pl.pallas_call(attention_kernel, grid=(rows // block,), in_specs=[pl.Bloc...  18.9 us
    all_to_all x1, starting transfers between devices, body(): lax.all_to_all(w_copies, 'tok', split_axis=0, concat_axis=0, tiled=True)  9.84 us
    dot_general x1, matrix products, body(): jnp.einsum('td,dcf->tcf', normed, w_full, preferred_element_type=jnp.floa...  5.59 us
    reduce_sum x1, other arithmetic, body(): row_mean = jnp.mean(values, axis=1, keepdims=True)  4.62 us
  transfers between devices with their start and end apart: 4, of which 4 were waited for; matrix products, arithmetic and copies ran while one was open for 4% of the time, Pallas kernels for 0%

profile of v3, /device:TPU:1, one launch (start us, length us, event | category | flops | bytes accessed | tf_op | source)
XLA Modules:
  0.0 214.6 jit_solution(9248553826056399918)
XLA Ops:
  7.5 0.3 fusion.18
  8.0 0.7 convert_element_type.42
  8.7 0.7 convert_element_type.41
  9.4 1.2 add_convert_fusion
  10.6 0.7 copy-done.2
  11.3 0.8 fusion.15
  12.2 1.5 copy.16
  13.7 23.2 %all_to_all.24 = bf16[128,16,192]{0,2,1:T(8,128)(2,1)S(1)} all-to-all(bf16[128,16,192]{0,2,1:T(8,128)(2,1)S(1)} %bitcast.31), channel_id=1, replica_groups=mesh['tok'=8,'wid'=16] {'wid'}, dimensions={1} | all-to-all | bytes 1572864 | tf_op jit(solution)/shard_map/all_to_all | solution.py:61
  36.8 3.0 %broadcast_in_dim.2 = bf16[8,384,3,128]{3,1,2,0:T(8,128)(2,1)} broadcast(bf16[384,3,128]{2,0,1:T(8,128)(2,1)} %param.14), dimensions={1,2,3} | broadcast | bytes 2654208 | tf_op jit(solution)/shard_map/broadcast_in_dim | solution.py:63
  39.8 9.8 %all-to-all-start = ((bf16[8,384,3,128]{3,1,2,0:T(8,128)(2,1)}), bf16[8,384,3,128]{3,1,2,0:T(8,128)(2,1)S(1)}, u32[]{:S(2)}, u32[]{:S(2)}) async-start(bf16[8,384,3,128]{3,1,2,0:T(8,128)(2,1)} %broadcast_in_dim.2), calls=%async_computation | async-start | bytes 4718592 | tf_op jit(solution)/shard_map/all_to_all | solution.py:64
  49.6 1.0 copy_bitcast_fusion
  50.6 28.0 %all-to-all-done = bf16[8,384,3,128]{3,1,2,0:T(8,128)(2,1)S(1)} async-done(((bf16[8,384,3,128]{3,1,2,0:T(8,128)(2,1)}), bf16[8,384,3,128]{3,1,2,0:T(8,128)(2,1)S(1)}, u32[]{:S(2)}, u32[]{:S(2)}) %all-to-all-start) | async-done | bytes 2359328 | tf_op jit(solution)/shard_map/all_to_all | solution.py:64
  78.7 1.6 copy.14
  80.3 3.4 %all-gather.4.cloned.1.call-done = bf16[1040,3072]{0,1:T(8,128)(2,1)} async-done(((bf16[1040,192]{0,1:T(8,128)(2,1)}), bf16[1040,3072]{0,1:T(8,128)(2,1)}) %all-gather.4.cloned.1.call-update) | async-done | bytes 6389776 | tf_op jit(solution)/shard_map/all_gather | solution.py:77
  83.6 4.6 %convert_reduce_fusion = (f32[1024]{0:T(1024)S(1)}, f32[1024]{0:T(1024)S(1)}) fusion(bf16[1040,3072]{0,1:T(8,128)(2,1)} %all-gather.4.cloned.1.call-done), kind=kLoop, calls=%fused_computation.2 | loop fusion | flops 12580864 | bytes 6299648 | tf_op jit(solution)/shard_map/reduce_sum | solution.py:83
  88.3 2.3 %add_reduce_fusion = (f32[3072]{0:T(1024)S(1)}, f32[3072]{0:T(1024)S(1)}) fusion(bf16[1040,3072]{0,1:T(8,128)(2,1)} %all-gather.4.cloned.1.call-done), kind=kLoop, calls=%fused_computation.12 | loop fusion | flops 9216 | bytes 36864 | tf_op jit(solution)/shard_map/add | solution.py:17
  90.6 5.6 %fusion.9 = bf16[1024,3,128]{2,0,1:T(8,128)(2,1)S(1)} fusion(bf16[3072,3,128]{2,0,1:T(8,128)(2,1)} %bitcast.32, f32[3072]{0:T(1024)S(1)} %get-tuple-element.24, f32[3072]{0:T(1024)S(1)} %get-tuple-element.23, f32[1024]{0:T(1024)S(1)} %get-tuple-element.26, f32[1024]{0:T(1024)S(1)} %get-tuple-element.25, bf16[1040,3072]{0,1:T(8,128)(2,1)S(1)} %copy-done.1), kind=kOutput, calls=%fused_computation.13 | convolution fusion | flops 2435186688 | bytes 9469952 | tf_op jit(solution)/shard_map/td,dcf->tcf/dot_general | solution.py:86
  96.2 0.9 copy_bitcast_fusion.1
  97.1 0.2 all-gather.8.cloned.1.call-start
  97.3 0.7 slice_bitcast_fusion.1.q_ref
  98.1 31.7 %all-gather.6.cloned.1.call-done.kv_ref = bf16[8192,256]{1,0:T(8,128)(2,1)} async-done(((bf16[1024,256]{1,0:T(8,128)(2,1)}), bf16[8192,256]{1,0:T(8,128)(2,1)}) %all-gather.6.cloned.1.call-update) | async-done | bytes 4194320 | tf_op jit(solution)/shard_map/all_gather | solution.py:94
  129.8 18.9 %shard_map.73 = bf16[1024,128]{1,0:T(8,128)(2,1)} custom-call(bf16[1024,128]{1,0:T(8,128)(2,1)} %slice_bitcast_fusion.1.q_ref, bf16[8192,256]{1,0:T(8,128)(2,1)} %all-gather.6.cloned.1.call-done.kv_ref), custom_call_target="tpu_custom_call" | custom-call | flops 4294967296 | bytes 4718592 | tf_op jit(solution)/shard_map/pallas_call | solution.py:37
  149.0 54.7 %all-gather.8.cloned.1.call-done = bf16[1024,2048]{1,0:T(8,128)(2,1)} async-done(((bf16[1024,128]{1,0:T(8,128)(2,1)}), bf16[1024,2048]{1,0:T(8,128)(2,1)}) %all-gather.8.cloned.1.call-update) | async-done | bytes 4194320 | tf_op jit(solution)/shard_map/all_gather | solution.py:98
  203.6 4.5 %fusion.13 = bf16[1024,192]{0,1:T(8,128)(2,1)} fusion(bf16[1024,2048]{1,0:T(8,128)(2,1)} %all-gather.8.cloned.1.call-done, bf16[2048,192]{0,1:T(8,128)(2,1)S(1)} %copy-done.4, bf16[1024,192]{0,1:T(8,128)(2,1)S(1)} %copy-done.3, f32[192]{0:T(256)S(1)} %convert_reduce_fusion.2), kind=kOutput, calls=%fused_computation.16 | convolution fusion | flops 806092800 | bytes 5767936 | tf_op jit(solution)/shard_map/dot_general | solution.py:99
  (19 shorter events, 0.7 us)
Async XLA Ops:
  6.5 1.0 copy-start
  6.5 77.1 %all-gather.4.cloned.1.call-start = ((), (), s32[]{:S(2)}) async-start(), calls=%async_computation.2 | async-start | bytes 7520256 | tf_op jit(solution)/shard_map/all_gather | solution.py:77
  10.6 0.7 copy-start.2
  39.8 38.9 %all-to-all-start = ((bf16[8,384,3,128]{3,1,2,0:T(8,128)(2,1)}), bf16[8,384,3,128]{3,1,2,0:T(8,128)(2,1)S(1)}, u32[]{:S(2)}, u32[]{:S(2)}) async-start(bf16[8,384,3,128]{3,1,2,0:T(8,128)(2,1)} %broadcast_in_dim.2), calls=%async_computation | async-start | bytes 4718592 | tf_op jit(solution)/shard_map/all_to_all | solution.py:64
  49.6 80.2 %all-gather.6.cloned.1.call-start = ((), (), s32[]{:S(2)}) async-start(), calls=%async_computation.3 | async-start | bytes 4718592 | tf_op jit(solution)/shard_map/all_gather | solution.py:94
  83.6 7.0 %copy-start.1 = (bf16[1040,3072]{0,1:T(8,128)(2,1)S(1)}, bf16[1040,3072]{0,1:T(8,128)(2,1)}, u32[]{:S(2)}) copy-start(bf16[1040,3072]{0,1:T(8,128)(2,1)} %all-gather.4.cloned.1.call-done) | copy-start | bytes 19169284
  97.1 106.5 %all-gather.8.cloned.1.call-start = ((), (), s32[]{:S(2)}) async-start(), calls=%async_computation.4 | async-start | bytes 4456448 | tf_op jit(solution)/shard_map/all_gather | solution.py:98
  98.1 105.6 %copy-start.3 = (bf16[1024,192]{0,1:T(8,128)(2,1)S(1)}, bf16[1024,192]{0,1:T(8,128)(2,1)}, u32[]{:S(2)}) copy-start(bf16[1024,192]{0,1:T(8,128)(2,1)} %copy-done.2) | copy-start | bytes 1179652
  98.1 105.6 %copy-start.4 = (bf16[2048,192]{0,1:T(8,128)(2,1)S(1)}, bf16[2048,192]{0,1:T(8,128)(2,1)}, u32[]{:S(2)}) copy-start(bf16[2048,192]{0,1:T(8,128)(2,1)} %copy_bitcast_fusion) | copy-start | bytes 2359300
Sparse Core Ops, SparseCore 0:
  12.3 71.2 all-gather.3
  97.2 32.5 all-gather.5
  148.9 54.6 all-gather.7

commit v4 on v3

v4 whole, which is shorter than its diff:
```python
import math

import jax
import jax.numpy as jnp
from jax import lax
from jax.experimental import pallas as pl
from jax.experimental.pallas import tpu as pltpu
from jax.sharding import PartitionSpec as P

D = 3072
DH = 128
TEMB = 256


def finish_rows(values, row_mean, row_var, shift_row, scale_row):
    normal = (values - row_mean) * lax.rsqrt(row_var + 1e-06)
    return (normal * (1.0 + scale_row.astype(jnp.float32)) + shift_row.astype(jnp.float32)).astype(
        jnp.bfloat16
    )


def attention_kernel(q_ref, kv0_ref, kv1_ref, o_ref):
    queries = q_ref[...]
    score_parts = [
        lax.dot_general(
            queries, kv_ref[:, :DH], (((1,), (1,)), ((), ())), preferred_element_type=jnp.float32
        )
        * (DH ** (-0.5))
        for kv_ref in (kv0_ref, kv1_ref)
    ]
    row_max = jnp.maximum(
        jnp.max(score_parts[0], axis=1, keepdims=True), jnp.max(score_parts[1], axis=1, keepdims=True)
    )
    shifted = [jnp.exp(part - row_max) for part in score_parts]
    row_sum = jnp.sum(shifted[0], axis=1, keepdims=True) + jnp.sum(shifted[1], axis=1, keepdims=True)
    numer = jnp.dot(
        shifted[0].astype(jnp.bfloat16), kv0_ref[:, DH:], preferred_element_type=jnp.float32
    ) + jnp.dot(shifted[1].astype(jnp.bfloat16), kv1_ref[:, DH:], preferred_element_type=jnp.float32)
    o_ref[...] = (numer / row_sum).astype(o_ref.dtype)


def attention(queries, kv0, kv1, block=256):
    rows = queries.shape[0]
    count = kv0.shape[0]
    return pl.pallas_call(
        attention_kernel,
        grid=(rows // block,),
        in_specs=[
            pl.BlockSpec((block, DH), lambda i: (i, 0)),
            pl.BlockSpec((count, 2 * DH), lambda i: (0, 0)),
            pl.BlockSpec((count, 2 * DH), lambda i: (0, 0)),
        ],
        out_specs=pl.BlockSpec((block, DH), lambda i: (i, 0)),
        out_shape=jax.ShapeDtypeStruct((rows, DH), jnp.bfloat16),
        compiler_params=pltpu.CompilerParams(vmem_limit_bytes=56 * 1024 * 1024),
        cost_estimate=pl.CostEstimate(
            flops=8 * rows * count * DH,
            transcendentals=2 * rows * count,
            bytes_accessed=4 * rows * DH + 8 * count * DH,
        ),
    )(queries, kv0, kv1)


def body(tokens, defect_mask, timestep, mask_embed, mod_weight, w_qkv, w_out):
    tok_rows = tokens.shape[0]
    half = tok_rows // 2
    residual_in = (
        tokens.astype(jnp.float32)
        + defect_mask.astype(jnp.float32)[:, None] * mask_embed.astype(jnp.float32)[None, :]
    ).astype(jnp.bfloat16)
    w_cols = lax.all_to_all(w_out, "wid", split_axis=1, concat_axis=0, tiled=True)
    tok_count = lax.axis_size("tok")
    w_copies = jnp.broadcast_to(w_qkv[None], (tok_count,) + w_qkv.shape)
    w_full = lax.all_to_all(w_copies, "tok", split_axis=0, concat_axis=0, tiled=True)
    w_full = w_full.reshape((tok_count * w_qkv.shape[0],) + w_qkv.shape[1:])
    half_width = TEMB // 2
    frequency = jnp.exp(-math.log(10000.0) * jnp.arange(half_width, dtype=jnp.float32) / half_width)
    angles = timestep.astype(jnp.float32)[0] * frequency
    embedding = jnp.concatenate([jnp.cos(angles), jnp.sin(angles)])
    modulation = jnp.einsum(
        "e,ecf->cf",
        jax.nn.silu(embedding),
        mod_weight.astype(jnp.float32),
        precision=lax.Precision.HIGHEST,
    ).astype(jnp.bfloat16)
    extra = jnp.zeros((16, residual_in.shape[1]), jnp.bfloat16).at[:2].set(modulation[:2])
    gathered = [
        lax.all_gather(
            jnp.concatenate([residual_in[chunk * half : (chunk + 1) * half], extra], axis=0),
            "wid",
            axis=1,
            tiled=True,
        )
        for chunk in range(2)
    ]
    queries = []
    key_values = []
    for packed in gathered:
        shift_scale = packed[half : half + 2]
        values = packed[:half].astype(jnp.float32)
        row_mean = jnp.mean(values, axis=1, keepdims=True)
        row_var = jnp.mean(values * values, axis=1, keepdims=True) - row_mean * row_mean
        normed = finish_rows(
            values, row_mean, row_var, shift_scale[0][None, :], shift_scale[1][None, :]
        )
        qkv = jnp.einsum(
            "td,dcf->tcf",
            normed,
            w_full,
            preferred_element_type=jnp.float32,
        ).astype(jnp.bfloat16)
        queries.append(qkv[:, 0])
        key_values.append(
            lax.all_gather(qkv[:, 1:3].reshape(half, 2 * DH), "tok", axis=0, tiled=True)
        )
    key_values[1], w_cols = lax.optimization_barrier((key_values[1], w_cols))
    gate = modulation[2].astype(jnp.float32)[None, :]
    outputs = []
    for chunk, query_rows in enumerate(queries):
        attended = attention(query_rows, key_values[0], key_values[1])
        attended_full = lax.all_gather(attended, "wid", axis=1, tiled=True)
        projected = jnp.dot(attended_full, w_cols, preferred_element_type=jnp.float32)
        rows = residual_in[chunk * half : (chunk + 1) * half]
        outputs.append((rows.astype(jnp.float32) + gate * projected).astype(jnp.bfloat16))
    return jnp.concatenate(outputs, axis=0)


def solution(mesh):
    return jax.shard_map(
        body,
        mesh=mesh,
        in_specs=(
            P("tok", "wid"),
            P("tok"),
            P(),
            P("wid"),
            P(None, None, "wid"),
            P("tok", None, "wid"),
            P("wid", None),
        ),
        out_specs=P("tok", "wid"),
        check_vma=False,
    )
```

time: 216 us -> 288 us (1.33)
  waiting for transfers between devices: 118 us -> 160 us
  blocking collectives: 23.2 us -> 53.8 us
  starting transfers between devices: 10.1 us -> 0.21 us
  other arithmetic: 10.6 us -> 14.8 us
  Pallas kernels: 18.9 us -> 22.9 us
    all_gather x2 -> x4, waiting for transfers between devices: 35.1 us -> 80.8 us  [the longest x2 56.3 us: body(): lax.all_gather(jnp.concatenate([residual_in[chunk * half:(chunk + 1) * ha...]
    all_to_all x0 -> x1, blocking collectives: none -> 35.6 us  [body(): lax.all_to_all(w_copies, 'tok', split_axis=0, concat_axis=0, tiled=True)]
    all_to_all x1 -> x0, waiting for transfers between devices: 28 us -> none  [body(): lax.all_to_all(w_copies, 'tok', split_axis=0, concat_axis=0, tiled=True)]
    all_gather x1 -> x2, waiting for transfers between devices: 54.7 us -> 78.7 us  [body(): attended_full = lax.all_gather(attended, 'wid', axis=1, tiled=True)]
    all_to_all x1 -> x0, starting transfers between devices: 9.84 us -> none  [body(): lax.all_to_all(w_copies, 'tok', split_axis=0, concat_axis=0, tiled=True)]
    dot_general x1 -> x0, matrix products: 5.59 us -> none  [body(): jnp.einsum('td,dcf->tcf', normed, w_full, preferred_element_type=jnp.floa...]
    unnamed x0 -> x2, matrix products: none -> 4.96 us
    all_to_all x1, blocking collectives: 23.2 us -> 18.2 us  [body(): lax.all_to_all(w_out, 'wid', split_axis=1, concat_axis=0, tiled=True)]
  transfers between devices with their start and end apart: 4 -> 6, of which waited for: 4 -> 5; matrix products, arithmetic and copies ran while one was open for 4% -> 10% of each run, Pallas kernels for 0% -> 4%
where the time goes in v4:
time: 288 us; the launch traced here: 287 us
  waiting for transfers between devices  160 us (56%)
  blocking collectives  53.8 us (19%)
  Pallas kernels  22.9 us (8%)
  other arithmetic  14.8 us (5%)
  between operations  14.3 us (5%)
  matrix products  10.2 us (4%)
  local copies, waits for them, and re-layouts  10 us (3%)
    all_gather x2, waiting for transfers between devices, body(): attended_full = lax.all_gather(attended, 'wid', axis=1, tiled=True)  78.7 us
    all_gather x2, waiting for transfers between devices, body(): lax.all_gather(jnp.concatenate([residual_in[chunk * half:(chunk + 1) * ha...  56.3 us
    all_to_all x1, blocking collectives, body(): lax.all_to_all(w_copies, 'tok', split_axis=0, concat_axis=0, tiled=True)  35.6 us
    all_gather x2, waiting for transfers between devices, body(): lax.all_gather(qkv[:, 1:3].reshape(half, 2 * DH), 'tok', axis=0, tiled=True)  24.5 us
    pallas_call x2, Pallas kernels, attention(): pl.pallas_call(attention_kernel, grid=(rows // block,), in_specs=[pl.Bloc...  22.9 us
    all_to_all x1, blocking collectives, body(): lax.all_to_all(w_out, 'wid', split_axis=1, concat_axis=0, tiled=True)  18.2 us
  transfers between devices with their start and end apart: 6, of which 5 were waited for; matrix products, arithmetic and copies ran while one was open for 10% of the time, Pallas kernels for 4%

profile of v4, /device:TPU:1, one launch (start us, length us, event | category | flops | bytes accessed | tf_op | source)
XLA Modules:
  0.0 286.5 jit_solution(11105328588866828175)
XLA Ops:
  9.4 1.2 add_convert_fusion
  10.6 0.8 fusion.29
  12.8 35.6 %all_to_all.24 = bf16[8,384,3,128]{1,3,2,0:T(8,128)(2,1)S(1)} all-to-all(bf16[8,384,3,128]{1,3,2,0:T(8,128)(2,1)S(1)} %broadcast_in_dim.2), channel_id=1, replica_groups=mesh['tok'=8,'wid'=16] {'tok'}, dimensions={0} | all-to-all | bytes 4718592 | tf_op jit(solution)/shard_map/all_to_all | solution.py:74
  48.4 1.4 copy.25
  50.3 14.3 %all-gather.11.cloned.1.call-done = bf16[528,3072]{0,1:T(8,128)(2,1)} async-done(((bf16[528,192]{0,1:T(8,128)(2,1)}), bf16[528,3072]{0,1:T(8,128)(2,1)}) %all-gather.11.cloned.1.call-update) | async-done | bytes 3244048 | tf_op jit(solution)/shard_map/all_gather | solution.py:88
  64.6 2.5 add_reduce_fusion
  67.1 2.8 convert_reduce_fusion
  69.9 2.5 fusion.10
  72.4 1.4 copy.30
  74.5 42.0 %all-gather.7.cloned.1.call-done = bf16[528,3072]{0,1:T(8,128)(2,1)} async-done(((bf16[528,192]{0,1:T(8,128)(2,1)}), bf16[528,3072]{0,1:T(8,128)(2,1)}) %all-gather.7.cloned.1.call-update) | async-done | bytes 3244048 | tf_op jit(solution)/shard_map/all_gather | solution.py:88
  116.5 2.5 add_reduce_fusion.1
  119.0 2.8 convert_reduce_fusion.1
  121.8 2.5 fusion.12
  124.3 1.4 copy.27
  126.4 1.5 copy.32
  128.0 18.2 %all_to_all.25 = bf16[128,16,192]{0,2,1:T(8,128)(2,1)S(1)} all-to-all(bf16[128,16,192]{0,2,1:T(8,128)(2,1)S(1)} %bitcast.43), channel_id=1, replica_groups=mesh['tok'=8,'wid'=16] {'wid'}, dimensions={1} | all-to-all | bytes 1572864 | tf_op jit(solution)/shard_map/all_to_all | solution.py:71
  147.0 24.5 %all-gather.9.cloned.1.call-done.kv0_ref = bf16[4096,256]{1,0:T(8,128)(2,1)} async-done(((bf16[512,256]{1,0:T(8,128)(2,1)}), bf16[4096,256]{1,0:T(8,128)(2,1)}) %all-gather.9.cloned.1.call-update) | async-done | bytes 2097168 | tf_op jit(solution)/shard_map/all_gather | solution.py:114
  171.4 11.4 %shard_map.74 = bf16[512,128]{1,0:T(8,128)(2,1)} custom-call(bf16[512,128]{1,0:T(8,128)(2,1)} %slice_bitcast_fusion.2.q_ref, bf16[4096,256]{1,0:T(8,128)(2,1)} %all-gather.9.cloned.1.call-done.kv0_ref, bf16[4096,256]{1,0:T(8,128)(2,1)} %all-gather.13.cloned.1.call-done.kv1_ref), custom_call_target="tpu_custom_call" | custom-call | flops 2147483648 | bytes 4456448 | tf_op jit(solution)/shard_map/pallas_call | solution.py:45
  183.6 11.4 %shard_map.73 = bf16[512,128]{1,0:T(8,128)(2,1)} custom-call(bf16[512,128]{1,0:T(8,128)(2,1)} %slice_bitcast_fusion.3.q_ref, bf16[4096,256]{1,0:T(8,128)(2,1)} %all-gather.9.cloned.1.call-done.kv0_ref, bf16[4096,256]{1,0:T(8,128)(2,1)} %all-gather.13.cloned.1.call-done.kv1_ref), custom_call_target="tpu_custom_call" | custom-call | flops 2147483648 | bytes 4456448 | tf_op jit(solution)/shard_map/pallas_call | solution.py:45
  195.3 32.9 %all-gather.17.cloned.1.call-done = bf16[512,2048]{1,0:T(8,128)(2,1)} async-done(((bf16[512,128]{1,0:T(8,128)(2,1)}), bf16[512,2048]{1,0:T(8,128)(2,1)}) %all-gather.17.cloned.1.call-update) | async-done | bytes 2097168 | tf_op jit(solution)/shard_map/all_gather | solution.py:121
  228.2 2.4 fusion.27
  230.6 45.8 %all-gather.15.cloned.1.call-done = bf16[512,2048]{1,0:T(8,128)(2,1)} async-done(((bf16[512,128]{1,0:T(8,128)(2,1)}), bf16[512,2048]{1,0:T(8,128)(2,1)}) %all-gather.15.cloned.1.call-update) | async-done | bytes 2097168 | tf_op jit(solution)/shard_map/all_gather | solution.py:121
  276.4 2.4 fusion.26
  278.9 0.8 pad_maximum_fusion
  (39 shorter events, 7.3 us)
Async XLA Ops:
  6.5 1.0 copy-start
  6.5 5.7 %copy-start.3 = (bf16[384,3,128]{2,0,1:T(8,128)(2,1)S(1)}, bf16[384,3,128]{2,0,1:T(8,128)(2,1)}, u32[]{:S(2)}) copy-start(bf16[384,3,128]{2,0,1:T(8,128)(2,1)} %param.14) | copy-start | bytes 884740
  6.5 58.1 %all-gather.11.cloned.1.call-start = ((), (), s32[]{:S(2)}) async-start(), calls=%async_computation.4 | async-start | bytes 4177920 | tf_op jit(solution)/shard_map/all_gather | solution.py:88
  11.4 105.1 %all-gather.7.cloned.1.call-start = ((), (), s32[]{:S(2)}) async-start(), calls=%async_computation.2 | async-start | bytes 4177920 | tf_op jit(solution)/shard_map/all_gather | solution.py:88
  12.2 134.8 %all-gather.13.cloned.1.call-start = ((), (), s32[]{:S(2)}) async-start(), calls=%async_computation.5 | async-start | bytes 2359296 | tf_op jit(solution)/shard_map/all_gather | solution.py:114
  64.6 5.2 %copy-start.2 = (bf16[528,3072]{0,1:T(8,128)(2,1)S(1)}, bf16[528,3072]{0,1:T(8,128)(2,1)}, u32[]{:S(2)}) copy-start(bf16[528,3072]{0,1:T(8,128)(2,1)} %all-gather.11.cloned.1.call-done) | copy-start | bytes 9732100
  74.5 97.0 %all-gather.9.cloned.1.call-start = ((), (), s32[]{:S(2)}) async-start(), calls=%async_computation.3 | async-start | bytes 2359296 | tf_op jit(solution)/shard_map/all_gather | solution.py:114
  116.5 5.2 %copy-start.1 = (bf16[528,3072]{0,1:T(8,128)(2,1)S(1)}, bf16[528,3072]{0,1:T(8,128)(2,1)}, u32[]{:S(2)}) copy-start(bf16[528,3072]{0,1:T(8,128)(2,1)} %all-gather.7.cloned.1.call-done) | copy-start | bytes 9732100
  126.4 101.8 %all-gather.17.cloned.1.call-start = ((), (), s32[]{:S(2)}) async-start(), calls=%async_computation.7 | async-start | bytes 2228224 | tf_op jit(solution)/shard_map/all_gather | solution.py:121
  182.9 93.5 %all-gather.15.cloned.1.call-start = ((), (), s32[]{:S(2)}) async-start(), calls=%async_computation.6 | async-start | bytes 2228224 | tf_op jit(solution)/shard_map/all_gather | solution.py:121
Sparse Core Ops, SparseCore 0:
  11.6 53.0 all-gather.10
  66.8 49.7 all-gather.6
  118.3 25.7 all-gather.12
  145.7 25.7 all-gather.8
  183.0 45.0 all-gather.16
  230.1 46.2 all-gather.14

commit v5 on v3

--- a/solution.py
+++ b/solution.py
@@ -58,7 +58,6 @@
         tokens.astype(jnp.float32)
         + defect_mask.astype(jnp.float32)[:, None] * mask_embed.astype(jnp.float32)[None, :]
     ).astype(jnp.bfloat16)
-    w_cols = lax.all_to_all(w_out, "wid", split_axis=1, concat_axis=0, tiled=True)
     tok_count = lax.axis_size("tok")
     w_copies = jnp.broadcast_to(w_qkv[None], (tok_count,) + w_qkv.shape)
     w_full = lax.all_to_all(w_copies, "tok", split_axis=0, concat_axis=0, tiled=True)
@@ -89,11 +88,13 @@
         w_full,
         preferred_element_type=jnp.float32,
     ).astype(jnp.bfloat16)
-    qkv, w_cols = lax.optimization_barrier((qkv, w_cols))
+    w_late, qkv = lax.optimization_barrier((w_out, qkv))
+    w_cols = lax.all_to_all(w_late, "wid", split_axis=1, concat_axis=0, tiled=True)
     queries = qkv[:, 0]
     key_values = lax.all_gather(
         qkv[:, 1:3].reshape(tok_rows, 2 * DH), "tok", axis=0, tiled=True
     )
+    w_cols, key_values = lax.optimization_barrier((w_cols, key_values))
     attended = attention(queries, key_values)
     attended_full = lax.all_gather(attended, "wid", axis=1, tiled=True)
     projected = jnp.dot(attended_full, w_cols, preferred_element_type=jnp.float32)

time: 216 us -> 211 us (0.977)
  blocking collectives: 23.2 us -> 35.6 us
  waiting for transfers between devices: 118 us -> 109 us
  starting transfers between devices: 10.1 us -> 5.25 us
    all_gather x1, waiting for transfers between devices: 3.36 us -> 30.6 us  [body(): lax.all_gather(jnp.concatenate([residual_in, extra], axis=0), 'wid', axis...]
    all_gather x1, waiting for transfers between devices: 31.7 us -> 12.2 us  [body(): lax.all_gather(qkv[:, 1:3].reshape(tok_rows, 2 * DH), 'tok', axis=0, tile...]
    all_to_all x1, waiting for transfers between devices: 28 us -> 11.2 us  [body(): lax.all_to_all(w_late, 'wid', split_axis=1, concat_axis=0, tiled=True)]
    all_to_all x1, blocking collectives: 23.2 us -> 35.6 us  [body(): lax.all_to_all(w_copies, 'tok', split_axis=0, concat_axis=0, tiled=True)]
    all_to_all x1, starting transfers between devices: 9.84 us -> 4.98 us  [body(): lax.all_to_all(w_late, 'wid', split_axis=1, concat_axis=0, tiled=True)]
    optimization_barrier x0 -> x1, local copies, waits for them, and re-layouts: none -> 2.31 us  [body(): w_late, qkv = lax.optimization_barrier((w_out, qkv))]
  transfers between devices with their start and end apart: 4 -> 4, of which waited for: 4 -> 4; matrix products, arithmetic and copies ran while one was open for 4% -> 3% of each run, Pallas kernels for 0% -> 0%
where the time goes in v5:
time: 211 us; the launch traced here: 210 us
  waiting for transfers between devices  109 us (52%)
  blocking collectives  35.6 us (17%)
  Pallas kernels  18.9 us (9%)
  between operations  13.9 us (7%)
  other arithmetic  10.7 us (5%)
  matrix products  8.79 us (4%)
  local copies, waits for them, and re-layouts  7.88 us (4%)
  starting transfers between devices  5.25 us (2%)
    all_gather x1, waiting for transfers between devices, body(): attended_full = lax.all_gather(attended, 'wid', axis=1, tiled=True)  54.7 us
    all_to_all x1, blocking collectives, body(): lax.all_to_all(w_copies, 'tok', split_axis=0, concat_axis=0, tiled=True)  35.6 us
    all_gather x1, waiting for transfers between devices, body(): lax.all_gather(jnp.concatenate([residual_in, extra], axis=0), 'wid', axis...  30.6 us
    pallas_call x1, Pallas kernels, attention(): pl.pallas_call(attention_kernel, grid=(rows // block,), in_specs=[pl.Bloc...  18.9 us
    all_gather x1, waiting for transfers between devices, body(): lax.all_gather(qkv[:, 1:3].reshape(tok_rows, 2 * DH), 'tok', axis=0, tile...  12.2 us
    all_to_all x1, waiting for transfers between devices, body(): lax.all_to_all(w_late, 'wid', split_axis=1, concat_axis=0, tiled=True)  11.2 us
    all_to_all x1, starting transfers between devices, body(): lax.all_to_all(w_late, 'wid', split_axis=1, concat_axis=0, tiled=True)  4.98 us
    reduce_sum x1, other arithmetic, body(): row_mean = jnp.mean(values, axis=1, keepdims=True)  4.62 us
  transfers between devices with their start and end apart: 4, of which 4 were waited for; matrix products, arithmetic and copies ran while one was open for 3% of the time, Pallas kernels for 0%

profile of v5, /device:TPU:1, one launch (start us, length us, event | category | flops | bytes accessed | tf_op | source)
XLA Modules:
  0.0 209.8 jit_solution(6175677398591329781)
XLA Ops:
  7.3 0.2 copy-done
  7.5 0.3 fusion.18
  8.0 0.7 convert_element_type.42
  8.7 0.7 convert_element_type.41
  9.4 1.2 add_convert_fusion
  10.6 0.8 fusion.15
  11.4 1.5 broadcast_in_dim.2
  12.9 35.6 %all_to_all.24 = bf16[8,384,3,128]{3,1,2,0:T(8,128)(2,1)S(1)} all-to-all(bf16[8,384,3,128]{3,1,2,0:T(8,128)(2,1)S(1)} %broadcast_in_dim.2), channel_id=1, replica_groups=mesh['tok'=8,'wid'=16] {'tok'}, dimensions={0} | all-to-all | bytes 4718592 | tf_op jit(solution)/shard_map/all_to_all | solution.py:63
  48.5 0.2 copy.14
  48.7 30.6 %all-gather.4.cloned.1.call-done = bf16[1040,3072]{0,1:T(8,128)(2,1)} async-done(((bf16[1040,192]{0,1:T(8,128)(2,1)}), bf16[1040,3072]{0,1:T(8,128)(2,1)}) %all-gather.4.cloned.1.call-update) | async-done | bytes 6389776 | tf_op jit(solution)/shard_map/all_gather | solution.py:76
  79.3 4.6 %convert_reduce_fusion = (f32[1024]{0:T(1024)S(1)}, f32[1024]{0:T(1024)S(1)}) fusion(bf16[1040,3072]{0,1:T(8,128)(2,1)} %all-gather.4.cloned.1.call-done), kind=kLoop, calls=%fused_computation.2 | loop fusion | flops 12580864 | bytes 6299648 | tf_op jit(solution)/shard_map/reduce_sum | solution.py:82
  83.9 2.5 %add_reduce_fusion = (f32[3072]{0:T(1024)S(1)}, f32[3072]{0:T(1024)S(1)}) fusion(bf16[1040,3072]{0,1:T(8,128)(2,1)} %all-gather.4.cloned.1.call-done), kind=kLoop, calls=%fused_computation.12 | loop fusion | flops 9216 | bytes 36864 | tf_op jit(solution)/shard_map/add | solution.py:17
  86.5 4.0 %fusion.9 = bf16[1024,3,128]{2,0,1:T(8,128)(2,1)S(1)} fusion(bf16[3072,3,128]{2,0,1:T(8,128)(2,1)S(1)} %bitcast.31, f32[3072]{0:T(1024)S(1)} %get-tuple-element.28, f32[3072]{0:T(1024)S(1)} %get-tuple-element.27, f32[1024]{0:T(1024)S(1)} %get-tuple-element.30, f32[1024]{0:T(1024)S(1)} %get-tuple-element.29, bf16[1040,3072]{0,1:T(8,128)(2,1)S(1)} %copy-done.1), kind=kOutput, calls=%fused_computation.13 | convolution fusion | flops 2435186688 | bytes 9469952 | tf_op jit(solution)/shard_map/td,dcf->tcf/dot_general | solution.py:85
  90.5 0.9 copy-done.2
  91.4 0.8 copy_bitcast_fusion.1
  92.2 2.3 %copy.16 = bf16[128,3072]{0,1:T(8,128)(2,1)} copy(bf16[128,3072]{1,0:T(8,128)(2,1)} %param.15) | data formatting | bytes 1572864 | tf_op jit(solution)/shard_map/optimization_barrier | solution.py:91
  94.6 5.0 %all-to-all-start.1 = ((bf16[128,16,192]{0,2,1:T(8,128)(2,1)}), bf16[128,16,192]{0,2,1:T(8,128)(2,1)S(1)}, u32[]{:S(2)}, u32[]{:S(2)}) async-start(bf16[128,16,192]{0,2,1:T(8,128)(2,1)} %bitcast.6), calls=%async_computation.1 | async-start | bytes 1572864 | tf_op jit(solution)/shard_map/all_to_all | solution.py:92
  99.5 0.2 all-gather.8.cloned.1.call-start
  99.8 1.7 slice_bitcast_fusion.1.q_ref
  101.4 11.2 %all-to-all-done.1 = bf16[128,16,192]{0,2,1:T(8,128)(2,1)S(1)} async-done(((bf16[128,16,192]{0,2,1:T(8,128)(2,1)}), bf16[128,16,192]{0,2,1:T(8,128)(2,1)S(1)}, u32[]{:S(2)}, u32[]{:S(2)}) %all-to-all-start.1) | async-done | bytes 786464 | tf_op jit(solution)/shard_map/all_to_all | solution.py:92
  112.8 12.2 %all-gather.6.cloned.1.call-done.kv_ref = bf16[8192,256]{1,0:T(8,128)(2,1)} async-done(((bf16[1024,256]{1,0:T(8,128)(2,1)}), bf16[8192,256]{1,0:T(8,128)(2,1)}) %all-gather.6.cloned.1.call-update) | async-done | bytes 4194320 | tf_op jit(solution)/shard_map/all_gather | solution.py:94
  125.0 18.9 %shard_map.73 = bf16[1024,128]{1,0:T(8,128)(2,1)} custom-call(bf16[1024,128]{1,0:T(8,128)(2,1)} %slice_bitcast_fusion.1.q_ref, bf16[8192,256]{1,0:T(8,128)(2,1)} %all-gather.6.cloned.1.call-done.kv_ref), custom_call_target="tpu_custom_call" | custom-call | flops 4294967296 | bytes 4718592 | tf_op jit(solution)/shard_map/pallas_call | solution.py:37
  144.1 54.7 %all-gather.8.cloned.1.call-done = bf16[1024,2048]{1,0:T(8,128)(2,1)} async-done(((bf16[1024,128]{1,0:T(8,128)(2,1)}), bf16[1024,2048]{1,0:T(8,128)(2,1)}) %all-gather.8.cloned.1.call-update) | async-done | bytes 4194320 | tf_op jit(solution)/shard_map/all_gather | solution.py:99
  198.8 4.5 %fusion.13 = bf16[1024,192]{0,1:T(8,128)(2,1)} fusion(bf16[1024,2048]{1,0:T(8,128)(2,1)} %all-gather.8.cloned.1.call-done, bf16[2048,192]{0,1:T(8,128)(2,1)S(1)} %copy_bitcast_fusion, bf16[1024,192]{0,1:T(8,128)(2,1)S(1)} %add_convert_fusion, f32[192]{0:T(256)S(1)} %convert_reduce_fusion.2), kind=kOutput, calls=%fused_computation.16 | convolution fusion | flops 806092800 | bytes 5767936 | tf_op jit(solution)/shard_map/dot_general | solution.py:100
  (15 shorter events, 0.6 us)
Async XLA Ops:
  6.5 1.0 copy-start
  6.5 72.8 %all-gather.4.cloned.1.call-start = ((), (), s32[]{:S(2)}) async-start(), calls=%async_computation.2 | async-start | bytes 7520256 | tf_op jit(solution)/shard_map/all_gather | solution.py:76
  11.4 113.6 %all-gather.6.cloned.1.call-start = ((), (), s32[]{:S(2)}) async-start(), calls=%async_computation.3 | async-start | bytes 4718592 | tf_op jit(solution)/shard_map/all_gather | solution.py:94
  79.3 7.2 %copy-start.1 = (bf16[1040,3072]{0,1:T(8,128)(2,1)S(1)}, bf16[1040,3072]{0,1:T(8,128)(2,1)}, u32[]{:S(2)}) copy-start(bf16[1040,3072]{0,1:T(8,128)(2,1)} %all-gather.4.cloned.1.call-done) | copy-start | bytes 19169284
  90.5 0.9 copy-start.2
  94.6 18.1 %all-to-all-start.1 = ((bf16[128,16,192]{0,2,1:T(8,128)(2,1)}), bf16[128,16,192]{0,2,1:T(8,128)(2,1)S(1)}, u32[]{:S(2)}, u32[]{:S(2)}) async-start(bf16[128,16,192]{0,2,1:T(8,128)(2,1)} %bitcast.6), calls=%async_computation.1 | async-start | bytes 1572864 | tf_op jit(solution)/shard_map/all_to_all | solution.py:92
  99.5 99.2 %all-gather.8.cloned.1.call-start = ((), (), s32[]{:S(2)}) async-start(), calls=%async_computation.4 | async-start | bytes 4456448 | tf_op jit(solution)/shard_map/all_gather | solution.py:99
Sparse Core Ops, SparseCore 0:
  11.5 67.7 all-gather.3
  92.4 32.5 all-gather.5
  144.0 54.6 all-gather.7

commit v6 on v5

--- a/solution.py
+++ b/solution.py
@@ -17,6 +17,48 @@
     return (normal * (1.0 + scale_row.astype(jnp.float32)) + shift_row.astype(jnp.float32)).astype(
         jnp.bfloat16
     )
+
+
+def project_kernel(x_ref, mod_ref, w_ref, q_ref, kv_ref):
+    values = x_ref[...].astype(jnp.float32)
+    width = values.shape[1]
+    row_mean = jnp.sum(values, axis=1, keepdims=True) / width
+    row_var = jnp.sum(values * values, axis=1, keepdims=True) / width - row_mean * row_mean
+    shift_row = mod_ref[0:1, :].astype(jnp.float32)
+    scale_row = mod_ref[1:2, :].astype(jnp.float32)
+    normal = (values - row_mean) * lax.rsqrt(row_var + 1e-06)
+    normed = (normal * (1.0 + scale_row) + shift_row).astype(jnp.bfloat16)
+    qkv = jnp.dot(normed, w_ref[...], preferred_element_type=jnp.float32).astype(jnp.bfloat16)
+    q_ref[...] = qkv[:, :DH]
+    kv_ref[...] = qkv[:, DH:]
+
+
+def project(packed, rows, weights, block=256):
+    width = packed.shape[1]
+    extra_block = rows // 16
+    return pl.pallas_call(
+        project_kernel,
+        grid=(rows // block,),
+        in_specs=[
+            pl.BlockSpec((block, width), lambda i: (i, 0)),
+            pl.BlockSpec((16, width), lambda i: (extra_block, 0)),
+            pl.BlockSpec(weights.shape, lambda i: (0, 0)),
+        ],
+        out_specs=[
+            pl.BlockSpec((block, DH), lambda i: (i, 0)),
+            pl.BlockSpec((block, 2 * DH), lambda i: (i, 0)),
+        ],
+        out_shape=[
+            jax.ShapeDtypeStruct((rows, DH), jnp.bfloat16),
+            jax.ShapeDtypeStruct((rows, 2 * DH), jnp.bfloat16),
+        ],
+        compiler_params=pltpu.CompilerParams(vmem_limit_bytes=48 * 1024 * 1024),
+        cost_estimate=pl.CostEstimate(
+            flops=2 * rows * width * weights.shape[1] + 10 * rows * width,
+            transcendentals=rows,
+            bytes_accessed=2 * rows * width + 2 * weights.size + 2 * rows * 3 * DH,
+        ),
+    )(packed, packed, weights)
 
 
 def attention_kernel(q_ref, kv_ref, o_ref):
@@ -76,24 +118,12 @@
     packed = lax.all_gather(
         jnp.concatenate([residual_in, extra], axis=0), "wid", axis=1, tiled=True
     )
-    residual_full = packed[:tok_rows]
-    shift_scale = packed[tok_rows : tok_rows + 2]
-    values = residual_full.astype(jnp.float32)
-    row_mean = jnp.mean(values, axis=1, keepdims=True)
-    row_var = jnp.mean(values * values, axis=1, keepdims=True) - row_mean * row_mean
-    normed = finish_rows(values, row_mean, row_var, shift_scale[0][None, :], shift_scale[1][None, :])
-    qkv = jnp.einsum(
-        "td,dcf->tcf",
-        normed,
-        w_full,
-        preferred_element_type=jnp.float32,
-    ).astype(jnp.bfloat16)
+    queries, key_rows = project(packed, tok_rows, w_full.reshape(w_full.shape[0], 3 * DH))
+    qkv = (queries, key_rows)
     w_late, qkv = lax.optimization_barrier((w_out, qkv))
     w_cols = lax.all_to_all(w_late, "wid", split_axis=1, concat_axis=0, tiled=True)
-    queries = qkv[:, 0]
-    key_values = lax.all_gather(
-        qkv[:, 1:3].reshape(tok_rows, 2 * DH), "tok", axis=0, tiled=True
-    )
+    queries, key_rows = qkv
+    key_values = lax.all_gather(key_rows, "tok", axis=0, tiled=True)
     w_cols, key_values = lax.optimization_barrier((w_cols, key_values))
     attended = attention(queries, key_values)
     attended_full = lax.all_gather(attended, "wid", axis=1, tiled=True)

time: 211 us -> 217 us (1.028)
  blocking collectives: 35.6 us -> 53.8 us
  waiting for transfers between devices: 109 us -> 92.2 us
  local copies, waits for them, and re-layouts: 7.88 us -> 20.3 us
  Pallas kernels: 18.9 us -> 26.9 us
  other arithmetic: 10.7 us -> 3.58 us
  starting transfers between devices: 5.25 us -> 0.09 us
  matrix products: 8.79 us -> 4.8 us
    all_to_all x0 -> x1, blocking collectives: none -> 18.2 us  [body(): lax.all_to_all(w_late, 'wid', split_axis=1, concat_axis=0, tiled=True)]
    all_to_all x1 -> x0, waiting for transfers between devices: 11.2 us -> none  [body(): lax.all_to_all(w_late, 'wid', split_axis=1, concat_axis=0, tiled=True)]
    all_gather x0 -> x1, local copies, waits for them, and re-layouts: none -> 9.98 us  [body(): lax.all_gather(jnp.concatenate([residual_in, extra], axis=0), 'wid', axis...]
    pallas_call x0 -> x1, Pallas kernels: none -> 7.97 us  [project(): pl.pallas_call(project_kernel, grid=(rows // block,), in_specs=[pl.BlockS...]
    all_gather x1, waiting for transfers between devices: 30.6 us -> 24.6 us  [body(): lax.all_gather(jnp.concatenate([residual_in, extra], axis=0), 'wid', axis...]
    all_to_all x1 -> x0, starting transfers between devices: 4.98 us -> none  [body(): lax.all_to_all(w_late, 'wid', split_axis=1, concat_axis=0, tiled=True)]
    reduce_sum x1 -> x0, other arithmetic: 4.62 us -> none  [body(): row_mean = jnp.mean(values, axis=1, keepdims=True)]
    dot_general x1 -> x0, matrix products: 3.99 us -> none  [body(): jnp.einsum('td,dcf->tcf', normed, w_full, preferred_element_type=jnp.floa...]
  transfers between devices with their start and end apart: 4 -> 3, of which waited for: 4 -> 3; matrix products, arithmetic and copies ran while one was open for 3% -> 4% of each run, Pallas kernels for 0% -> 0%
where the time goes in v6:
time: 217 us; the launch traced here: 216 us
  waiting for transfers between devices  92.2 us (42%)
  blocking collectives  53.8 us (25%)
  Pallas kernels  26.9 us (12%)
  local copies, waits for them, and re-layouts  20.3 us (9%)
  between operations  13.9 us (6%)
  matrix products  4.8 us (2%)
  other arithmetic  3.58 us (2%)
    all_gather x1, waiting for transfers between devices, body(): attended_full = lax.all_gather(attended, 'wid', axis=1, tiled=True)  54.7 us
    all_to_all x1, blocking collectives, body(): lax.all_to_all(w_copies, 'tok', split_axis=0, concat_axis=0, tiled=True)  35.6 us
    all_gather x1, waiting for transfers between devices, body(): lax.all_gather(jnp.concatenate([residual_in, extra], axis=0), 'wid', axis...  24.6 us
    pallas_call x1, Pallas kernels, attention(): pl.pallas_call(attention_kernel, grid=(rows // block,), in_specs=[pl.Bloc...  18.9 us
    all_to_all x1, blocking collectives, body(): lax.all_to_all(w_late, 'wid', split_axis=1, concat_axis=0, tiled=True)  18.2 us
    all_gather x1, waiting for transfers between devices, body(): key_values = lax.all_gather(key_rows, 'tok', axis=0, tiled=True)  12.8 us
    all_gather x1, local copies, waits for them, and re-layouts, body(): lax.all_gather(jnp.concatenate([residual_in, extra], axis=0), 'wid', axis...  9.98 us
    pallas_call x1, Pallas kernels, project(): pl.pallas_call(project_kernel, grid=(rows // block,), in_specs=[pl.BlockS...  7.97 us
  transfers between devices with their start and end apart: 3, of which 3 were waited for; matrix products, arithmetic and copies ran while one was open for 4% of the time, Pallas kernels for 0%

profile of v6, /device:TPU:1, one launch (start us, length us, event | category | flops | bytes accessed | tf_op | source)
XLA Modules:
  0.0 215.5 jit_solution(15778831485915220268)
XLA Ops:
  7.3 0.2 copy-done
  7.5 0.3 fusion.6
  7.9 0.2 copy.33
  8.0 0.7 convert_element_type.28
  8.7 0.7 convert_element_type.29
  9.4 1.2 add_convert_fusion
  10.6 0.8 fusion.3
  11.5 1.2 copy.26
  12.6 0.3 broadcast_in_dim.2
  13.0 35.6 %all_to_all.24 = bf16[8,384,3,128]{1,3,2,0:T(8,128)(2,1)S(1)} all-to-all(bf16[8,384,3,128]{1,3,2,0:T(8,128)(2,1)S(1)} %broadcast_in_dim.2), channel_id=1, replica_groups=mesh['tok'=8,'wid'=16] {'tok'}, dimensions={0} | all-to-all | bytes 4718592 | tf_op jit(solution)/shard_map/all_to_all | solution.py:105
  48.6 3.8 %copy.34 = bf16[8,384,3,128]{3,2,1,0:T(4,128)(2,1)} copy(bf16[8,384,3,128]{1,3,2,0:T(8,128)(2,1)S(1)} %all_to_all.24) | data formatting | bytes 4718592 | tf_op jit(solution)/shard_map/reshape;reshape | solution.py:121
  52.4 2.3 %copy.40 = bf16[384,8,3,128]{3,1,2,0:T(8,128)(2,1)S(1)} copy(bf16[384,8,3,128]{3,2,1,0:T(4,128)(2,1)} %bitcast.23) | data formatting | bytes 4718592
  54.7 24.6 %all-gather.4.cloned.1.call-done = bf16[1040,3072]{0,1:T(8,128)(2,1)} async-done(((bf16[1040,192]{0,1:T(8,128)(2,1)}), bf16[1040,3072]{0,1:T(8,128)(2,1)}) %all-gather.4.cloned.1.call-update) | async-done | bytes 6389776 | tf_op jit(solution)/shard_map/all_gather | solution.py:118
  79.3 10.0 %copy.28.x_ref.mod_ref = bf16[1040,3072]{1,0:T(8,128)(2,1)} copy(bf16[1040,3072]{0,1:T(8,128)(2,1)} %all-gather.4.cloned.1.call-done) | data formatting | bytes 12779520 | tf_op jit(solution)/shard_map/all_gather | solution.py:118
  89.3 8.0 %shard_map.73 = (bf16[1024,128]{1,0:T(8,128)(2,1)S(1)}, bf16[1024,256]{1,0:T(8,128)(2,1)}) custom-call(bf16[1040,3072]{1,0:T(8,128)(2,1)} %copy.28.x_ref.mod_ref, bf16[1040,3072]{1,0:T(8,128)(2,1)} %copy.28.x_ref.mod_ref, bf16[3072,384]{1,0:T(8,128)(2,1)S(1)} %bitcast.22), custom_call_target="tpu_custom_call" | custom-call | flops 2447376384 | bytes 9437184 | tf_op jit(solution)/shard_map/pallas_call | solution.py:39
  97.3 0.7 copy-done.1
  98.1 1.5 copy.31
  99.6 18.2 %all_to_all.25 = bf16[128,16,192]{0,2,1:T(8,128)(2,1)S(1)} all-to-all(bf16[128,16,192]{0,2,1:T(8,128)(2,1)S(1)} %bitcast.24), channel_id=1, replica_groups=mesh['tok'=8,'wid'=16] {'wid'}, dimensions={1} | all-to-all | bytes 1572864 | tf_op jit(solution)/shard_map/all_to_all | solution.py:124
  117.8 0.1 copy_bitcast_fusion.1
  117.9 12.8 %all-gather.6.cloned.1.call-done.kv_ref = bf16[8192,256]{1,0:T(8,128)(2,1)} async-done(((bf16[1024,256]{1,0:T(8,128)(2,1)}), bf16[8192,256]{1,0:T(8,128)(2,1)}) %all-gather.6.cloned.1.call-update) | async-done | bytes 4194320 | tf_op jit(solution)/shard_map/all_gather | solution.py:126
  130.7 18.9 %shard_map.74 = bf16[1024,128]{1,0:T(8,128)(2,1)} custom-call(bf16[1024,128]{1,0:T(8,128)(2,1)} %copy-done.1, bf16[8192,256]{1,0:T(8,128)(2,1)} %all-gather.6.cloned.1.call-done.kv_ref), custom_call_target="tpu_custom_call" | custom-call | flops 4294967296 | bytes 4718592 | tf_op jit(solution)/shard_map/pallas_call | solution.py:79
  149.7 0.2 convert_reduce_fusion
  149.9 54.7 %all-gather.8.cloned.1.call-done = bf16[1024,2048]{1,0:T(8,128)(2,1)} async-done(((bf16[1024,128]{1,0:T(8,128)(2,1)}), bf16[1024,2048]{1,0:T(8,128)(2,1)}) %all-gather.8.cloned.1.call-update) | async-done | bytes 4194320 | tf_op jit(solution)/shard_map/all_gather | solution.py:129
  204.5 4.5 %fusion.1 = bf16[1024,192]{0,1:T(8,128)(2,1)} fusion(bf16[1024,2048]{1,0:T(8,128)(2,1)} %all-gather.8.cloned.1.call-done, bf16[2048,192]{0,1:T(8,128)(2,1)S(1)} %copy_bitcast_fusion.1, bf16[1024,192]{0,1:T(8,128)(2,1)S(1)} %add_convert_fusion, f32[192]{0:T(256)S(1)} %convert_reduce_fusion), kind=kOutput, calls=%fused_computation.3 | convolution fusion | flops 806092800 | bytes 5767936 | tf_op jit(solution)/shard_map/dot_general | solution.py:130
  (10 shorter events, 0.2 us)
Async XLA Ops:
  6.5 1.0 copy-start
  6.5 72.8 %all-gather.4.cloned.1.call-start = ((), (), s32[]{:S(2)}) async-start(), calls=%async_computation.2 | async-start | bytes 7520256 | tf_op jit(solution)/shard_map/all_gather | solution.py:118
  11.4 119.3 %all-gather.6.cloned.1.call-start = ((), (), s32[]{:S(2)}) async-start(), calls=%async_computation.3 | async-start | bytes 4718592 | tf_op jit(solution)/shard_map/all_gather | solution.py:126
  97.3 0.7 copy-start.1
  98.0 106.5 %all-gather.8.cloned.1.call-start = ((), (), s32[]{:S(2)}) async-start(), calls=%async_computation.4 | async-start | bytes 4456448 | tf_op jit(solution)/shard_map/all_gather | solution.py:129
Sparse Core Ops, SparseCore 0:
  11.5 67.7 all-gather.3
  98.1 32.5 all-gather.5
  149.8 54.6 all-gather.7

commit v7 on v5

--- a/solution.py
+++ b/solution.py
@@ -96,8 +96,13 @@
     )
     w_cols, key_values = lax.optimization_barrier((w_cols, key_values))
     attended = attention(queries, key_values)
-    attended_full = lax.all_gather(attended, "wid", axis=1, tiled=True)
-    projected = jnp.dot(attended_full, w_cols, preferred_element_type=jnp.float32)
+    heads = lax.all_gather(attended, "wid", axis=0, tiled=False)
+    projected = jnp.einsum(
+        "htd,hdc->tc",
+        heads,
+        w_cols.reshape(heads.shape[0], DH, w_cols.shape[1]),
+        preferred_element_type=jnp.float32,
+    )
     return (
         residual_in.astype(jnp.float32) + modulation[2].astype(jnp.float32)[None, :] * projected
     ).astype(jnp.bfloat16)

time: 211 us -> 206 us (0.976)
  waiting for transfers between devices: 109 us -> 104 us
    all_gather x1, waiting for transfers between devices: 54.7 us -> 50.5 us  [body(): heads = lax.all_gather(attended, 'wid', axis=0, tiled=False)]
where the time goes in v7:
time: 206 us
  waiting for transfers between devices  104 us (50%)
  blocking collectives  35.6 us (17%)
  Pallas kernels  18.9 us (9%)
  between operations  13.9 us (7%)
  other arithmetic  10.7 us (5%)
  matrix products  8.78 us (4%)
  local copies, waits for them, and re-layouts  7.88 us (4%)
  starting transfers between devices  5.25 us (3%)
    all_gather x1, waiting for transfers between devices, body(): heads = lax.all_gather(attended, 'wid', axis=0, tiled=False)  50.5 us
    all_to_all x1, blocking collectives, body(): lax.all_to_all(w_copies, 'tok', split_axis=0, concat_axis=0, tiled=True)  35.6 us
    all_gather x1, waiting for transfers between devices, body(): lax.all_gather(jnp.concatenate([residual_in, extra], axis=0), 'wid', axis...  30.6 us
    pallas_call x1, Pallas kernels, attention(): pl.pallas_call(attention_kernel, grid=(rows // block,), in_specs=[pl.Bloc...  18.9 us
    all_gather x1, waiting for transfers between devices, body(): lax.all_gather(qkv[:, 1:3].reshape(tok_rows, 2 * DH), 'tok', axis=0, tile...  12.2 us
    all_to_all x1, waiting for transfers between devices, body(): lax.all_to_all(w_late, 'wid', split_axis=1, concat_axis=0, tiled=True)  11.2 us
    all_to_all x1, starting transfers between devices, body(): lax.all_to_all(w_late, 'wid', split_axis=1, concat_axis=0, tiled=True)  4.98 us
    reduce_sum x1, other arithmetic, body(): row_mean = jnp.mean(values, axis=1, keepdims=True)  4.62 us
  transfers between devices with their start and end apart: 4, of which 4 were waited for; matrix products, arithmetic and copies ran while one was open for 3% of the time, Pallas kernels for 0%

profile of v7, /device:TPU:1, one launch (start us, length us, event | category | flops | bytes accessed | tf_op | source)
XLA Modules:
  0.0 205.5 jit_solution(4487322172887043224)
XLA Ops:
  7.3 0.2 copy-done
  7.5 0.3 fusion.21
  8.0 0.7 convert_element_type.42
  8.7 0.7 convert_element_type.41
  9.4 1.2 add_convert_fusion
  10.6 0.8 fusion.18
  11.4 1.5 broadcast_in_dim.2
  12.9 35.6 %all_to_all.24 = bf16[8,384,3,128]{3,1,2,0:T(8,128)(2,1)S(1)} all-to-all(bf16[8,384,3,128]{3,1,2,0:T(8,128)(2,1)S(1)} %broadcast_in_dim.2), channel_id=1, replica_groups=mesh['tok'=8,'wid'=16] {'tok'}, dimensions={0} | all-to-all | bytes 4718592 | tf_op jit(solution)/shard_map/all_to_all | solution.py:63
  48.5 0.2 copy.15
  48.7 30.6 %all-gather.5.cloned.1.call-done = bf16[1040,3072]{0,1:T(8,128)(2,1)} async-done(((bf16[1040,192]{0,1:T(8,128)(2,1)}), bf16[1040,3072]{0,1:T(8,128)(2,1)}) %all-gather.5.cloned.1.call-update) | async-done | bytes 6389776 | tf_op jit(solution)/shard_map/all_gather | solution.py:76
  79.3 4.6 %convert_reduce_fusion = (f32[1024]{0:T(1024)S(1)}, f32[1024]{0:T(1024)S(1)}) fusion(bf16[1040,3072]{0,1:T(8,128)(2,1)} %all-gather.5.cloned.1.call-done), kind=kLoop, calls=%fused_computation.2 | loop fusion | flops 12580864 | bytes 6299648 | tf_op jit(solution)/shard_map/reduce_sum | solution.py:82
  83.9 2.5 %add_reduce_fusion = (f32[3072]{0:T(1024)S(1)}, f32[3072]{0:T(1024)S(1)}) fusion(bf16[1040,3072]{0,1:T(8,128)(2,1)} %all-gather.5.cloned.1.call-done), kind=kLoop, calls=%fused_computation.12 | loop fusion | flops 9216 | bytes 36864 | tf_op jit(solution)/shard_map/add | solution.py:17
  86.5 4.0 %fusion.9 = bf16[1024,3,128]{2,0,1:T(8,128)(2,1)S(1)} fusion(bf16[3072,3,128]{2,0,1:T(8,128)(2,1)S(1)} %bitcast.46, f32[3072]{0:T(1024)S(1)} %get-tuple-element.28, f32[3072]{0:T(1024)S(1)} %get-tuple-element.27, f32[1024]{0:T(1024)S(1)} %get-tuple-element.30, f32[1024]{0:T(1024)S(1)} %get-tuple-element.29, bf16[1040,3072]{0,1:T(8,128)(2,1)S(1)} %copy-done.1), kind=kOutput, calls=%fused_computation.13 | convolution fusion | flops 2435186688 | bytes 9469952 | tf_op jit(solution)/shard_map/td,dcf->tcf/dot_general | solution.py:85
  90.5 0.9 copy-done.2
  91.4 0.8 copy_bitcast_fusion.1
  92.2 2.3 %copy.17 = bf16[128,3072]{0,1:T(8,128)(2,1)} copy(bf16[128,3072]{1,0:T(8,128)(2,1)} %param.15) | data formatting | bytes 1572864 | tf_op jit(solution)/shard_map/optimization_barrier | solution.py:91
  94.6 5.0 %all-to-all-start.1 = ((bf16[128,16,192]{0,2,1:T(8,128)(2,1)}), bf16[128,16,192]{0,2,1:T(8,128)(2,1)S(1)}, u32[]{:S(2)}, u32[]{:S(2)}) async-start(bf16[128,16,192]{0,2,1:T(8,128)(2,1)} %bitcast.6), calls=%async_computation.1 | async-start | bytes 1572864 | tf_op jit(solution)/shard_map/all_to_all | solution.py:92
  99.5 0.2 all-gather.9.cloned.1.call-start
  99.8 1.7 slice_bitcast_fusion.1.q_ref
  101.4 11.2 %all-to-all-done.1 = bf16[128,16,192]{0,2,1:T(8,128)(2,1)S(1)} async-done(((bf16[128,16,192]{0,2,1:T(8,128)(2,1)}), bf16[128,16,192]{0,2,1:T(8,128)(2,1)S(1)}, u32[]{:S(2)}, u32[]{:S(2)}) %all-to-all-start.1) | async-done | bytes 786464 | tf_op jit(solution)/shard_map/all_to_all | solution.py:92
  112.8 12.2 %all-gather.7.cloned.1.call-done.kv_ref = bf16[8192,256]{1,0:T(8,128)(2,1)} async-done(((bf16[1024,256]{1,0:T(8,128)(2,1)}), bf16[8192,256]{1,0:T(8,128)(2,1)}) %all-gather.7.cloned.1.call-update) | async-done | bytes 4194320 | tf_op jit(solution)/shard_map/all_gather | solution.py:94
  125.0 18.9 %shard_map.73 = bf16[1024,128]{1,0:T(8,128)(2,1)} custom-call(bf16[1024,128]{1,0:T(8,128)(2,1)} %slice_bitcast_fusion.1.q_ref, bf16[8192,256]{1,0:T(8,128)(2,1)} %all-gather.7.cloned.1.call-done.kv_ref), custom_call_target="tpu_custom_call" | custom-call | flops 4294967296 | bytes 4718592 | tf_op jit(solution)/shard_map/pallas_call | solution.py:37
  144.1 50.5 %all-gather.9.cloned.1.call-done = bf16[16384,128]{1,0:T(8,128)(2,1)} async-done(((bf16[1024,128]{1,0:T(8,128)(2,1)}), bf16[16384,128]{1,0:T(8,128)(2,1)}) %all-gather.9.cloned.1.call-update) | async-done | bytes 4194320 | tf_op jit(solution)/shard_map/all_gather | solution.py:99
  194.6 4.5 %fusion.14 = bf16[1024,192]{0,1:T(8,128)(2,1)} fusion(bf16[16,1024,128]{2,1,0:T(8,128)(2,1)} %bitcast.50, bf16[1024,192]{0,1:T(8,128)(2,1)S(1)} %add_convert_fusion, f32[192]{0:T(256)S(1)} %convert_reduce_fusion.2, bf16[2048,192]{0,1:T(8,128)(2,1)S(1)} %copy_bitcast_fusion), kind=kOutput, calls=%fused_computation.17 | convolution fusion | flops 806092800 | bytes 5767936 | tf_op jit(solution)/shard_map/htd,hdc->tc/dot_general | solution.py:100
  (15 shorter events, 0.6 us)
Async XLA Ops:
  6.5 1.0 copy-start
  6.5 72.8 %all-gather.5.cloned.1.call-start = ((), (), s32[]{:S(2)}) async-start(), calls=%async_computation.2 | async-start | bytes 7520256 | tf_op jit(solution)/shard_map/all_gather | solution.py:76
  11.4 113.6 %all-gather.7.cloned.1.call-start = ((), (), s32[]{:S(2)}) async-start(), calls=%async_computation.3 | async-start | bytes 4718592 | tf_op jit(solution)/shard_map/all_gather | solution.py:94
  79.3 7.2 %copy-start.1 = (bf16[1040,3072]{0,1:T(8,128)(2,1)S(1)}, bf16[1040,3072]{0,1:T(8,128)(2,1)}, u32[]{:S(2)}) copy-start(bf16[1040,3072]{0,1:T(8,128)(2,1)} %all-gather.5.cloned.1.call-done) | copy-start | bytes 19169284
  90.5 0.9 copy-start.2
  94.6 18.1 %all-to-all-start.1 = ((bf16[128,16,192]{0,2,1:T(8,128)(2,1)}), bf16[128,16,192]{0,2,1:T(8,128)(2,1)S(1)}, u32[]{:S(2)}, u32[]{:S(2)}) async-start(bf16[128,16,192]{0,2,1:T(8,128)(2,1)} %bitcast.6), calls=%async_computation.1 | async-start | bytes 1572864 | tf_op jit(solution)/shard_map/all_to_all | solution.py:92
  99.5 95.0 %all-gather.9.cloned.1.call-start = ((), (), s32[]{:S(2)}) async-start(), calls=%async_computation.4 | async-start | bytes 4456448 | tf_op jit(solution)/shard_map/all_gather | solution.py:99
Sparse Core Ops, SparseCore 0:
  11.5 67.7 all-gather.4
  92.4 32.5 all-gather.6
  144.0 50.4 all-gather.8

commit v8 on v7

--- a/solution.py
+++ b/solution.py
@@ -73,27 +73,25 @@
         precision=lax.Precision.HIGHEST,
     ).astype(jnp.bfloat16)
     extra = jnp.zeros((16, residual_in.shape[1]), jnp.bfloat16).at[:2].set(modulation[:2])
-    packed = lax.all_gather(
-        jnp.concatenate([residual_in, extra], axis=0), "wid", axis=1, tiled=True
+    stacked = lax.all_gather(
+        jnp.concatenate([residual_in, extra], axis=0), "wid", axis=0, tiled=False
     )
-    residual_full = packed[:tok_rows]
-    shift_scale = packed[tok_rows : tok_rows + 2]
-    values = residual_full.astype(jnp.float32)
-    row_mean = jnp.mean(values, axis=1, keepdims=True)
-    row_var = jnp.mean(values * values, axis=1, keepdims=True) - row_mean * row_mean
-    normed = finish_rows(values, row_mean, row_var, shift_scale[0][None, :], shift_scale[1][None, :])
+    values = stacked[:, :tok_rows, :].astype(jnp.float32)
+    shift_rows = stacked[:, tok_rows : tok_rows + 1, :]
+    scale_rows = stacked[:, tok_rows + 1 : tok_rows + 2, :]
+    row_mean = jnp.sum(values, axis=(0, 2), keepdims=True) / D
+    row_var = jnp.sum(values * values, axis=(0, 2), keepdims=True) / D - row_mean * row_mean
+    normed = finish_rows(values, row_mean, row_var, shift_rows, scale_rows)
     qkv = jnp.einsum(
-        "td,dcf->tcf",
+        "jtc,jcf->tf",
         normed,
-        w_full,
+        w_full.reshape(stacked.shape[0], stacked.shape[2], 3 * DH),
         preferred_element_type=jnp.float32,
     ).astype(jnp.bfloat16)
     w_late, qkv = lax.optimization_barrier((w_out, qkv))
     w_cols = lax.all_to_all(w_late, "wid", split_axis=1, concat_axis=0, tiled=True)
-    queries = qkv[:, 0]
-    key_values = lax.all_gather(
-        qkv[:, 1:3].reshape(tok_rows, 2 * DH), "tok", axis=0, tiled=True
-    )
+    queries = qkv[:, :DH]
+    key_values = lax.all_gather(qkv[:, DH:], "tok", axis=0, tiled=True)
     w_cols, key_values = lax.optimization_barrier((w_cols, key_values))
     attended = attention(queries, key_values)
     heads = lax.all_gather(attended, "wid", axis=0, tiled=False)

time: 206 us -> 210 us (1.019)
  local copies, waits for them, and re-layouts: 7.88 us -> 18.5 us
  waiting for transfers between devices: 104 us -> 97.1 us
  matrix products: 8.78 us -> 11.4 us
  other arithmetic: 10.7 us -> 8.26 us
    another operation x0 -> x2, local copies, waits for them, and re-layouts: none -> 8.51 us  [body(): w_full.reshape(stacked.shape[0], stacked.shape[2], 3 * DH)]
    all_gather x1, waiting for transfers between devices: 30.6 us -> 22.1 us  [body(): lax.all_gather(jnp.concatenate([residual_in, extra], axis=0), 'wid', axis...]
    slice x0 -> x3, local copies, waits for them, and re-layouts: none -> 4.41 us  [the longest x1 1.91 us: body(): scale_rows = stacked[:, tok_rows + 1:tok_rows + 2, :]]
    unnamed x6 -> x15, local copies, waits for them, and re-layouts: 1.08 us -> 3.78 us
    dot_general x1, matrix products: 3.99 us -> 6.59 us  [body(): jnp.einsum('jtc,jcf->tf', normed, w_full.reshape(stacked.shape[0], stacke...]
    add x1, other arithmetic: 2.55 us -> 0.01 us  [finish_rows(): normal * (1.0 + scale_row.astype(jnp.float32))]
  transfers between devices with their start and end apart: 4 -> 4, of which waited for: 4 -> 4; matrix products, arithmetic and copies ran while one was open for 3% -> 6% of each run, Pallas kernels for 0% -> 0%
where the time goes in v8:
time: 210 us; the launch traced here: 209 us
  waiting for transfers between devices  97.1 us (46%)
  blocking collectives  35.7 us (17%)
  Pallas kernels  18.9 us (9%)
  local copies, waits for them, and re-layouts  18.5 us (9%)
  between operations  13.9 us (7%)
  matrix products  11.4 us (5%)
  other arithmetic  8.26 us (4%)
  starting transfers between devices  5.24 us (2%)
    all_gather x1, waiting for transfers between devices, body(): heads = lax.all_gather(attended, 'wid', axis=0, tiled=False)  50.5 us
    all_to_all x1, blocking collectives, body(): lax.all_to_all(w_copies, 'tok', split_axis=0, concat_axis=0, tiled=True)  35.7 us
    all_gather x1, waiting for transfers between devices, body(): lax.all_gather(jnp.concatenate([residual_in, extra], axis=0), 'wid', axis...  22.1 us
    pallas_call x1, Pallas kernels, attention(): pl.pallas_call(attention_kernel, grid=(rows // block,), in_specs=[pl.Bloc...  18.9 us
    all_gather x1, waiting for transfers between devices, body(): key_values = lax.all_gather(qkv[:, DH:], 'tok', axis=0, tiled=True)  13.3 us
    all_to_all x1, waiting for transfers between devices, body(): lax.all_to_all(w_late, 'wid', split_axis=1, concat_axis=0, tiled=True)  11.2 us
    another operation x2, local copies, waits for them, and re-layouts, body(): w_full.reshape(stacked.shape[0], stacked.shape[2], 3 * DH)  8.51 us
    dot_general x1, matrix products, body(): jnp.einsum('jtc,jcf->tf', normed, w_full.reshape(stacked.shape[0], stacke...  6.59 us
  transfers between devices with their start and end apart: 4, of which 4 were waited for; matrix products, arithmetic and copies ran while one was open for 6% of the time, Pallas kernels for 0%

profile of v8, /device:TPU:1, one launch (start us, length us, event | category | flops | bytes accessed | tf_op | source)
XLA Modules:
  0.0 209.1 jit_solution(13370923707970916167)
XLA Ops:
  8.0 0.7 convert_element_type.42
  8.7 0.7 convert_element_type.41
  9.4 1.2 add_convert_fusion
  10.6 0.7 copy-done.2
  11.3 0.8 fusion.17
  12.2 1.2 copy.16
  13.7 35.7 %all_to_all.24 = bf16[8,384,3,128]{1,3,2,0:T(8,128)(2,1)} all-to-all(bf16[8,384,3,128]{1,3,2,0:T(8,128)(2,1)S(1)} %broadcast_in_dim.2), channel_id=1, replica_groups=mesh['tok'=8,'wid'=16] {'tok'}, dimensions={0} | all-to-all | bytes 4718592 | tf_op jit(solution)/shard_map/all_to_all | solution.py:63
  49.4 4.3 %copy.23 = bf16[8,384,3,128]{3,2,1,0:T(4,128)(2,1)S(1)} copy(bf16[8,384,3,128]{1,3,2,0:T(8,128)(2,1)} %all_to_all.24) | data formatting | bytes 4718592 | tf_op jit(solution)/shard_map/reshape;reshape | solution.py:88
  53.7 4.2 %reshape.65 = bf16[16,192,384]{2,1,0:T(8,128)(2,1)} reshape(bf16[8,384,3,128]{3,2,1,0:T(4,128)(2,1)S(1)} %copy.23) | data formatting | bytes 4718592 | tf_op jit(solution)/shard_map/reshape;reshape | solution.py:88
  57.9 22.1 %all-gather.11.cloned.1.call-done = bf16[16,1040,192]{1,2,0:T(8,128)(2,1)} async-done(((bf16[1,1040,192]{1,2,0:T(8,128)(2,1)}), bf16[16,1040,192]{1,2,0:T(8,128)(2,1)}) %all-gather.11.cloned.1.call-update) | async-done | bytes 6389776 | tf_op jit(solution)/shard_map/all_gather | solution.py:76
  80.0 1.9 fusion.20
  82.3 0.4 copy.25
  82.7 4.7 %convert_reduce_fusion = (f32[1024]{0:T(1024)S(1)}, f32[1024]{0:T(1024)S(1)}) fusion(bf16[16,1040,192]{1,2,0:T(8,128)(2,1)} %all-gather.11.cloned.1.call-done), kind=kLoop, calls=%fused_computation.2 | loop fusion | flops 12580864 | bytes 6299648 | tf_op jit(solution)/shard_map/reduce_sum | solution.py:82
  87.4 6.6 %bitcast_convert_fusion = bf16[1024,384]{1,0:T(8,128)(2,1)S(1)} fusion(bf16[16,192,384]{2,1,0:T(8,128)(2,1)S(1)} %copy-done.1, f32[16,192]{1,0:T(8,128)S(1)} %bitcast_convert_fusion.2, f32[16,192]{1,0:T(8,128)S(1)} %add_bitcast_fusion, f32[1024]{0:T(1024)S(1)} %get-tuple-element.30, f32[1024]{0:T(1024)S(1)} %get-tuple-element.29, ...), kind=kOutput, calls=%fused_computation.10 | convolution fusion | flops 2435186688 | bytes 9469952 | tf_op jit(solution)/shard_map/jtc,jcf->tf/dot_general | solution.py:85
  94.0 0.9 copy-done.5
  94.9 0.8 slice.43
  95.8 1.2 copy.19
  97.0 5.0 %all-to-all-start.1 = ((bf16[128,16,192]{0,2,1:T(8,128)(2,1)}), bf16[128,16,192]{0,2,1:T(8,128)(2,1)S(1)}, u32[]{:S(2)}, u32[]{:S(2)}) async-start(bf16[128,16,192]{0,2,1:T(8,128)(2,1)} %bitcast.7), calls=%async_computation.1 | async-start | bytes 1572864 | tf_op jit(solution)/shard_map/all_to_all | solution.py:92
  102.2 1.7 slice.42.q_ref
  103.9 11.2 %all-to-all-done.1 = bf16[128,16,192]{0,2,1:T(8,128)(2,1)S(1)} async-done(((bf16[128,16,192]{0,2,1:T(8,128)(2,1)}), bf16[128,16,192]{0,2,1:T(8,128)(2,1)S(1)}, u32[]{:S(2)}, u32[]{:S(2)}) %all-to-all-start.1) | async-done | bytes 786464 | tf_op jit(solution)/shard_map/all_to_all | solution.py:92
  115.2 13.3 %all-gather.7.cloned.1.call-done.kv_ref = bf16[8192,256]{1,0:T(8,128)(2,1)} async-done(((bf16[1024,256]{1,0:T(8,128)(2,1)}), bf16[8192,256]{1,0:T(8,128)(2,1)}) %all-gather.7.cloned.1.call-update) | async-done | bytes 4194320 | tf_op jit(solution)/shard_map/all_gather | solution.py:94
  128.5 18.9 %shard_map.73 = bf16[1024,128]{1,0:T(8,128)(2,1)} custom-call(bf16[1024,128]{1,0:T(8,128)(2,1)} %slice.42.q_ref, bf16[8192,256]{1,0:T(8,128)(2,1)} %all-gather.7.cloned.1.call-done.kv_ref), custom_call_target="tpu_custom_call" | custom-call | flops 4294967296 | bytes 4718592 | tf_op jit(solution)/shard_map/pallas_call | solution.py:37
  147.6 50.5 %all-gather.9.cloned.1.call-done = bf16[16384,128]{1,0:T(8,128)(2,1)} async-done(((bf16[1024,128]{1,0:T(8,128)(2,1)}), bf16[16384,128]{1,0:T(8,128)(2,1)}) %all-gather.9.cloned.1.call-update) | async-done | bytes 4194320 | tf_op jit(solution)/shard_map/all_gather | solution.py:97
  198.1 4.5 %fusion.12 = bf16[1024,192]{0,1:T(8,128)(2,1)} fusion(bf16[16,1024,128]{2,1,0:T(8,128)(2,1)} %bitcast.45, bf16[1024,192]{0,1:T(8,128)(2,1)S(1)} %copy-done.3, f32[192]{0:T(256)S(1)} %convert_reduce_fusion.1, bf16[2048,192]{0,1:T(8,128)(2,1)S(1)} %copy_bitcast_fusion), kind=kOutput, calls=%fused_computation.14 | convolution fusion | flops 806092800 | bytes 5767936 | tf_op jit(solution)/shard_map/htd,hdc->tc/dot_general | solution.py:98
  (27 shorter events, 2.1 us)
Async XLA Ops:
  6.5 1.0 copy-start
  6.5 73.5 %all-gather.11.cloned.1.call-start = ((), (), s32[]{:S(2)}) async-start(), calls=%async_computation.4 | async-start | bytes 7520256 | tf_op jit(solution)/shard_map/all_gather | solution.py:76
  10.6 0.7 copy-start.2
  12.1 116.3 %all-gather.7.cloned.1.call-start = ((), (), s32[]{:S(2)}) async-start(), calls=%async_computation.2 | async-start | bytes 4718592 | tf_op jit(solution)/shard_map/all_gather | solution.py:94
  82.3 5.1 %copy-start.1 = (bf16[16,192,384]{2,1,0:T(8,128)(2,1)S(1)}, bf16[16,192,384]{2,1,0:T(8,128)(2,1)}, u32[]{:S(2)}) copy-start(bf16[16,192,384]{2,1,0:T(8,128)(2,1)} %reshape.65) | copy-start | bytes 7077892
  87.4 8.4 %copy-start.4 = (bf16[128,3072]{1,0:T(8,128)(2,1)S(1)}, bf16[128,3072]{1,0:T(8,128)(2,1)}, u32[]{:S(2)}) copy-start(bf16[128,3072]{1,0:T(8,128)(2,1)} %param.15) | copy-start | bytes 2359300
  94.0 0.9 copy-start.5
  97.0 18.1 %all-to-all-start.1 = ((bf16[128,16,192]{0,2,1:T(8,128)(2,1)}), bf16[128,16,192]{0,2,1:T(8,128)(2,1)S(1)}, u32[]{:S(2)}, u32[]{:S(2)}) async-start(bf16[128,16,192]{0,2,1:T(8,128)(2,1)} %bitcast.7), calls=%async_computation.1 | async-start | bytes 1572864 | tf_op jit(solution)/shard_map/all_to_all | solution.py:92
  102.0 96.1 %all-gather.9.cloned.1.call-start = ((), (), s32[]{:S(2)}) async-start(), calls=%async_computation.3 | async-start | bytes 4456448 | tf_op jit(solution)/shard_map/all_gather | solution.py:97
  115.1 83.0 %copy-start.3 = (bf16[1024,192]{0,1:T(8,128)(2,1)S(1)}, bf16[1024,192]{0,1:T(8,128)(2,1)}, u32[]{:S(2)}) copy-start(bf16[1024,192]{0,1:T(8,128)(2,1)} %copy-done.2) | copy-start | bytes 1179652
Sparse Core Ops, SparseCore 0:
  12.2 67.7 all-gather.10
  95.9 32.5 all-gather.6
  147.6 50.4 all-gather.8

commit v9 on v7

--- a/solution.py
+++ b/solution.py
@@ -72,12 +72,11 @@
         mod_weight.astype(jnp.float32),
         precision=lax.Precision.HIGHEST,
     ).astype(jnp.bfloat16)
-    extra = jnp.zeros((16, residual_in.shape[1]), jnp.bfloat16).at[:2].set(modulation[:2])
-    packed = lax.all_gather(
-        jnp.concatenate([residual_in, extra], axis=0), "wid", axis=1, tiled=True
-    )
-    residual_full = packed[:tok_rows]
-    shift_scale = packed[tok_rows : tok_rows + 2]
+    residual_full = lax.all_gather(residual_in, "wid", axis=1, tiled=True)
+    wid_count = lax.axis_size("wid")
+    mod_copies = jnp.broadcast_to(modulation[None, :2], (wid_count, 2, modulation.shape[1]))
+    mod_parts = lax.all_to_all(mod_copies, "wid", split_axis=0, concat_axis=0, tiled=True)
+    shift_scale = jnp.transpose(mod_parts, (1, 0, 2)).reshape(2, wid_count * modulation.shape[1])
     values = residual_full.astype(jnp.float32)
     row_mean = jnp.mean(values, axis=1, keepdims=True)
     row_var = jnp.mean(values * values, axis=1, keepdims=True) - row_mean * row_mean

time: 206 us -> 199 us (0.966)
  blocking collectives: 35.6 us -> 13.8 us
  waiting for transfers between devices: 104 us -> 113 us
  starting transfers between devices: 5.25 us -> 12.6 us
  other arithmetic: 10.7 us -> 8.08 us
    all_to_all x0 -> x1, waiting for transfers between devices: none -> 28.8 us  [body(): lax.all_to_all(w_copies, 'tok', split_axis=0, concat_axis=0, tiled=True)]
    all_gather x1, waiting for transfers between devices: 30.6 us -> 8.37 us  [body(): residual_full = lax.all_gather(residual_in, 'wid', axis=1, tiled=True)]
    all_to_all x1, blocking collectives: 35.6 us -> 13.8 us  [body(): lax.all_to_all(mod_copies, 'wid', split_axis=0, concat_axis=0, tiled=True)]
    all_to_all x0 -> x1, starting transfers between devices: none -> 7.41 us  [body(): lax.all_to_all(w_copies, 'tok', split_axis=0, concat_axis=0, tiled=True)]
    add x1, other arithmetic: 2.55 us -> 0.09 us  [finish_rows(): 1.0 + scale_row.astype(jnp.float32)]
  transfers between devices with their start and end apart: 4 -> 5, of which waited for: 4 -> 5; matrix products, arithmetic and copies ran while one was open for 3% -> 4% of each run, Pallas kernels for 0% -> 0%
where the time goes in v9:
time: 199 us
  waiting for transfers between devices  113 us (57%)
  Pallas kernels  18.9 us (9%)
  between operations  13.9 us (7%)
  blocking collectives  13.8 us (7%)
  starting transfers between devices  12.6 us (6%)
  matrix products  10.8 us (5%)
  other arithmetic  8.08 us (4%)
  local copies, waits for them, and re-layouts  7.64 us (4%)
    all_gather x1, waiting for transfers between devices, body(): heads = lax.all_gather(attended, 'wid', axis=0, tiled=False)  50.7 us
    all_to_all x1, waiting for transfers between devices, body(): lax.all_to_all(w_copies, 'tok', split_axis=0, concat_axis=0, tiled=True)  28.8 us
    pallas_call x1, Pallas kernels, attention(): pl.pallas_call(attention_kernel, grid=(rows // block,), in_specs=[pl.Bloc...  18.9 us
    all_to_all x1, blocking collectives, body(): lax.all_to_all(mod_copies, 'wid', split_axis=0, concat_axis=0, tiled=True)  13.8 us
    all_gather x1, waiting for transfers between devices, body(): lax.all_gather(qkv[:, 1:3].reshape(tok_rows, 2 * DH), 'tok', axis=0, tile...  13.3 us
    all_to_all x1, waiting for transfers between devices, body(): lax.all_to_all(w_late, 'wid', split_axis=1, concat_axis=0, tiled=True)  12.1 us
    all_gather x1, waiting for transfers between devices, body(): residual_full = lax.all_gather(residual_in, 'wid', axis=1, tiled=True)  8.37 us
    all_to_all x1, starting transfers between devices, body(): lax.all_to_all(w_copies, 'tok', split_axis=0, concat_axis=0, tiled=True)  7.41 us
  transfers between devices with their start and end apart: 5, of which 5 were waited for; matrix products, arithmetic and copies ran while one was open for 4% of the time, Pallas kernels for 0%

profile of v9, /device:TPU:1, one launch (start us, length us, event | category | flops | bytes accessed | tf_op | source)
XLA Modules:
  0.0 199.0 jit_solution(7769547231045001845)
XLA Ops:
  6.5 0.7 convert_element_type.58
  7.2 0.7 convert_element_type.57
  7.9 1.9 add_convert_fusion
  10.6 0.3 fusion.21
  11.0 13.8 %all_to_all.29 = bf16[16,2,192]{2,1,0:T(2,128)(2,1)S(1)} all-to-all(bf16[16,2,192]{2,1,0:T(2,128)(2,1)S(1)} %broadcast_in_dim.4), channel_id=1, replica_groups=mesh['tok'=8,'wid'=16] {'wid'}, dimensions={0} | all-to-all | bytes 24576 | tf_op jit(solution)/shard_map/all_to_all | solution.py:78
  24.8 3.0 %broadcast_in_dim.5 = bf16[8,384,3,128]{3,1,2,0:T(8,128)(2,1)} broadcast(bf16[384,3,128]{2,0,1:T(8,128)(2,1)} %param.12), dimensions={1,2,3} | broadcast | bytes 2654208 | tf_op jit(solution)/shard_map/broadcast_in_dim | solution.py:62
  27.8 7.4 %all-to-all-start.1 = ((bf16[8,384,3,128]{3,1,2,0:T(8,128)(2,1)}), bf16[8,384,3,128]{3,1,2,0:T(8,128)(2,1)S(1)}, u32[]{:S(2)}, u32[]{:S(2)}) async-start(bf16[8,384,3,128]{3,1,2,0:T(8,128)(2,1)} %broadcast_in_dim.5), calls=%async_computation.1 | async-start | bytes 4718592 | tf_op jit(solution)/shard_map/all_to_all | solution.py:63
  35.2 0.1 fusion.18
  35.4 28.8 %all-to-all-done.1 = bf16[8,384,3,128]{3,1,2,0:T(8,128)(2,1)S(1)} async-done(((bf16[8,384,3,128]{3,1,2,0:T(8,128)(2,1)}), bf16[8,384,3,128]{3,1,2,0:T(8,128)(2,1)S(1)}, u32[]{:S(2)}, u32[]{:S(2)}) %all-to-all-start.1) | async-done | bytes 2359328 | tf_op jit(solution)/shard_map/all_to_all | solution.py:63
  64.2 1.6 copy.15
  65.8 8.4 %all-gather.5.cloned.1.call-done = bf16[1024,3072]{0,1:T(8,128)(2,1)} async-done(((bf16[1024,192]{0,1:T(8,128)(2,1)}), bf16[1024,3072]{0,1:T(8,128)(2,1)}) %all-gather.5.cloned.1.call-update) | async-done | bytes 6291472 | tf_op jit(solution)/shard_map/all_gather | solution.py:75
  74.2 4.6 %convert_reduce_fusion = (f32[1024]{0:T(1024)S(1)}, f32[1024]{0:T(1024)S(1)}) fusion(bf16[1024,3072]{0,1:T(8,128)(2,1)} %all-gather.5.cloned.1.call-done), kind=kLoop, calls=%fused_computation.2 | loop fusion | flops 12580864 | bytes 6299648 | tf_op jit(solution)/shard_map/reduce_sum | solution.py:81
  78.9 6.0 %fusion.8 = bf16[1024,3,128]{2,0,1:T(8,128)(2,1)S(1)} fusion(bf16[3072,3,128]{2,0,1:T(8,128)(2,1)} %bitcast.47, bf16[1024,3072]{0,1:T(8,128)(2,1)S(1)} %copy-done.1, f32[3072]{0:T(1024)S(1)} %reshape.62, f32[3072]{0:T(1024)S(1)} %add.49, f32[1024]{0:T(1024)S(1)} %get-tuple-element.18, f32[1024]{0:T(1024)S(1)} %get-tuple-element.17), kind=kOutput, calls=%fused_computation.10 | convolution fusion | flops 2435186688 | bytes 9469952 | tf_op jit(solution)/shard_map/td,dcf->tcf/dot_general | solution.py:84
  84.8 0.9 copy_bitcast_fusion.1
  85.7 1.2 copy.17
  86.9 5.0 %all-to-all-start.2 = ((bf16[128,16,192]{0,2,1:T(8,128)(2,1)}), bf16[128,16,192]{0,2,1:T(8,128)(2,1)S(1)}, u32[]{:S(2)}, u32[]{:S(2)}) async-start(bf16[128,16,192]{0,2,1:T(8,128)(2,1)} %bitcast.8), calls=%async_computation.2 | async-start | bytes 1572864 | tf_op jit(solution)/shard_map/all_to_all | solution.py:91
  91.9 0.2 all-gather.9.cloned.1.call-start
  92.1 0.7 slice_bitcast_fusion.1.q_ref
  92.8 12.1 %all-to-all-done.2 = bf16[128,16,192]{0,2,1:T(8,128)(2,1)S(1)} async-done(((bf16[128,16,192]{0,2,1:T(8,128)(2,1)}), bf16[128,16,192]{0,2,1:T(8,128)(2,1)S(1)}, u32[]{:S(2)}, u32[]{:S(2)}) %all-to-all-start.2) | async-done | bytes 786464 | tf_op jit(solution)/shard_map/all_to_all | solution.py:91
  104.9 0.1 copy_bitcast_fusion
  105.1 13.3 %all-gather.7.cloned.1.call-done.kv_ref = bf16[8192,256]{1,0:T(8,128)(2,1)} async-done(((bf16[1024,256]{1,0:T(8,128)(2,1)}), bf16[8192,256]{1,0:T(8,128)(2,1)}) %all-gather.7.cloned.1.call-update) | async-done | bytes 4194320 | tf_op jit(solution)/shard_map/all_gather | solution.py:93
  118.4 18.9 %shard_map.73 = bf16[1024,128]{1,0:T(8,128)(2,1)} custom-call(bf16[1024,128]{1,0:T(8,128)(2,1)} %slice_bitcast_fusion.1.q_ref, bf16[8192,256]{1,0:T(8,128)(2,1)} %all-gather.7.cloned.1.call-done.kv_ref), custom_call_target="tpu_custom_call" | custom-call | flops 4294967296 | bytes 4718592 | tf_op jit(solution)/shard_map/pallas_call | solution.py:37
  137.3 50.7 %all-gather.9.cloned.1.call-done = bf16[16384,128]{1,0:T(8,128)(2,1)} async-done(((bf16[1024,128]{1,0:T(8,128)(2,1)}), bf16[16384,128]{1,0:T(8,128)(2,1)}) %all-gather.9.cloned.1.call-update) | async-done | bytes 4194320 | tf_op jit(solution)/shard_map/all_gather | solution.py:98
  188.0 4.5 %fusion.13 = bf16[1024,192]{0,1:T(8,128)(2,1)} fusion(bf16[16,1024,128]{2,1,0:T(8,128)(2,1)} %bitcast.53, bf16[1024,192]{0,1:T(8,128)(2,1)S(1)} %copy-done.2, f32[192]{0:T(256)S(1)} %bitcast.52, bf16[2048,192]{0,1:T(8,128)(2,1)S(1)} %copy_bitcast_fusion), kind=kOutput, calls=%fused_computation.14 | convolution fusion | flops 806092800 | bytes 5767936 | tf_op jit(solution)/shard_map/htd,hdc->tc/dot_general | solution.py:99
  (22 shorter events, 0.3 us)
Async XLA Ops:
  6.5 4.0 %copy-start = (bf16[256,3,192]{0,2,1:T(8,128)(2,1)S(1)}, bf16[256,3,192]{0,2,1:T(8,128)(2,1)}, u32[]{:S(2)}) copy-start(bf16[256,3,192]{0,2,1:T(8,128)(2,1)} %param.11) | copy-start | bytes 884740
  6.5 67.6 %all-gather.5.cloned.1.call-start = ((), (), s32[]{:S(2)}) async-start(), calls=%async_computation.3 | async-start | bytes 6684672 | tf_op jit(solution)/shard_map/all_gather | solution.py:75
  27.8 36.4 %all-to-all-start.1 = ((bf16[8,384,3,128]{3,1,2,0:T(8,128)(2,1)}), bf16[8,384,3,128]{3,1,2,0:T(8,128)(2,1)S(1)}, u32[]{:S(2)}, u32[]{:S(2)}) async-start(bf16[8,384,3,128]{3,1,2,0:T(8,128)(2,1)} %broadcast_in_dim.5), calls=%async_computation.1 | async-start | bytes 4718592 | tf_op jit(solution)/shard_map/all_to_all | solution.py:63
  35.2 83.2 %all-gather.7.cloned.1.call-start = ((), (), s32[]{:S(2)}) async-start(), calls=%async_computation.4 | async-start | bytes 4718592 | tf_op jit(solution)/shard_map/all_gather | solution.py:93
  74.2 4.6 %copy-start.1 = (bf16[1024,3072]{0,1:T(8,128)(2,1)S(1)}, bf16[1024,3072]{0,1:T(8,128)(2,1)}, u32[]{:S(2)}) copy-start(bf16[1024,3072]{0,1:T(8,128)(2,1)} %all-gather.5.cloned.1.call-done) | copy-start | bytes 18874372
  78.8 6.9 %copy-start.3 = (bf16[128,3072]{1,0:T(8,128)(2,1)S(1)}, bf16[128,3072]{1,0:T(8,128)(2,1)}, u32[]{:S(2)}) copy-start(bf16[128,3072]{1,0:T(8,128)(2,1)} %param.13) | copy-start | bytes 2359300
  86.9 18.1 %all-to-all-start.2 = ((bf16[128,16,192]{0,2,1:T(8,128)(2,1)}), bf16[128,16,192]{0,2,1:T(8,128)(2,1)S(1)}, u32[]{:S(2)}, u32[]{:S(2)}) async-start(bf16[128,16,192]{0,2,1:T(8,128)(2,1)} %bitcast.8), calls=%async_computation.2 | async-start | bytes 1572864 | tf_op jit(solution)/shard_map/all_to_all | solution.py:91
  91.9 96.1 %all-gather.9.cloned.1.call-start = ((), (), s32[]{:S(2)}) async-start(), calls=%async_computation.5 | async-start | bytes 4456448 | tf_op jit(solution)/shard_map/all_gather | solution.py:98
  105.1 82.9 %copy-start.2 = (bf16[1024,192]{0,1:T(8,128)(2,1)S(1)}, bf16[1024,192]{0,1:T(8,128)(2,1)}, u32[]{:S(2)}) copy-start(bf16[1024,192]{0,1:T(8,128)(2,1)} %add_convert_fusion) | copy-start | bytes 1179652
Sparse Core Ops, SparseCore 0:
  10.0 64.1 all-gather.4
  85.8 32.5 all-gather.6
  137.5 50.4 all-gather.8

commit v10 on v9

--- a/solution.py
+++ b/solution.py
@@ -17,6 +17,40 @@
     return (normal * (1.0 + scale_row.astype(jnp.float32)) + shift_row.astype(jnp.float32)).astype(
         jnp.bfloat16
     )
+
+
+def project_kernel(x_ref, mod_ref, w_ref, o_ref):
+    values = x_ref[...].astype(jnp.float32)
+    width = values.shape[0]
+    row_mean = jnp.sum(values, axis=0, keepdims=True) / width
+    row_var = jnp.sum(values * values, axis=0, keepdims=True) / width - row_mean * row_mean
+    normal = (values - row_mean) * lax.rsqrt(row_var + 1e-06)
+    shift_col = mod_ref[:, 0:1].astype(jnp.float32)
+    scale_col = mod_ref[:, 1:2].astype(jnp.float32)
+    normed = (normal * (1.0 + scale_col) + shift_col).astype(jnp.bfloat16)
+    o_ref[...] = jnp.dot(w_ref[...], normed, preferred_element_type=jnp.float32).astype(o_ref.dtype)
+
+
+def project(rows_t, mod_cols, weights_t, block=256):
+    width, rows = rows_t.shape
+    outs = weights_t.shape[0]
+    return pl.pallas_call(
+        project_kernel,
+        grid=(rows // block,),
+        in_specs=[
+            pl.BlockSpec((width, block), lambda i: (0, i)),
+            pl.BlockSpec(mod_cols.shape, lambda i: (0, 0)),
+            pl.BlockSpec(weights_t.shape, lambda i: (0, 0)),
+        ],
+        out_specs=pl.BlockSpec((outs, block), lambda i: (0, i)),
+        out_shape=jax.ShapeDtypeStruct((outs, rows), jnp.bfloat16),
+        compiler_params=pltpu.CompilerParams(vmem_limit_bytes=48 * 1024 * 1024),
+        cost_estimate=pl.CostEstimate(
+            flops=2 * rows * width * outs + 10 * rows * width,
+            transcendentals=rows,
+            bytes_accessed=2 * rows * width + 2 * width * outs + 2 * rows * outs,
+        ),
+    )(rows_t, mod_cols, weights_t)
 
 
 def attention_kernel(q_ref, kv_ref, o_ref):
@@ -77,22 +111,13 @@
     mod_copies = jnp.broadcast_to(modulation[None, :2], (wid_count, 2, modulation.shape[1]))
     mod_parts = lax.all_to_all(mod_copies, "wid", split_axis=0, concat_axis=0, tiled=True)
     shift_scale = jnp.transpose(mod_parts, (1, 0, 2)).reshape(2, wid_count * modulation.shape[1])
-    values = residual_full.astype(jnp.float32)
-    row_mean = jnp.mean(values, axis=1, keepdims=True)
-    row_var = jnp.mean(values * values, axis=1, keepdims=True) - row_mean * row_mean
-    normed = finish_rows(values, row_mean, row_var, shift_scale[0][None, :], shift_scale[1][None, :])
-    qkv = jnp.einsum(
-        "td,dcf->tcf",
-        normed,
-        w_full,
-        preferred_element_type=jnp.float32,
-    ).astype(jnp.bfloat16)
+    weights_t = w_full.reshape(w_full.shape[0], 3 * DH).T
+    qkv_t = project(residual_full.T, shift_scale.T, weights_t)
+    qkv = (qkv_t[:DH].T, qkv_t[DH:].T)
     w_late, qkv = lax.optimization_barrier((w_out, qkv))
     w_cols = lax.all_to_all(w_late, "wid", split_axis=1, concat_axis=0, tiled=True)
-    queries = qkv[:, 0]
-    key_values = lax.all_gather(
-        qkv[:, 1:3].reshape(tok_rows, 2 * DH), "tok", axis=0, tiled=True
-    )
+    queries, key_rows = qkv
+    key_values = lax.all_gather(key_rows, "tok", axis=0, tiled=True)
     w_cols, key_values = lax.optimization_barrier((w_cols, key_values))
     attended = attention(queries, key_values)
     heads = lax.all_gather(attended, "wid", axis=0, tiled=False)

time: 199 us -> 199 us (level)
  Pallas kernels: 18.9 us -> 28.4 us
  waiting for transfers between devices: 113 us -> 107 us
  matrix products: 10.8 us -> 4.81 us
  other arithmetic: 8.08 us -> 3.36 us
  blocking collectives: 13.8 us -> 18.3 us
  starting transfers between devices: 12.6 us -> 14.9 us
    pallas_call x0 -> x1, Pallas kernels: none -> 9.49 us  [project(): pl.pallas_call(project_kernel, grid=(rows // block,), in_specs=[pl.BlockS...]
    all_to_all x1, waiting for transfers between devices: 12.1 us -> 5.27 us  [body(): lax.all_to_all(mod_copies, 'wid', split_axis=0, concat_axis=0, tiled=True)]
    dot_general x1 -> x0, matrix products: 5.96 us -> none  [body(): jnp.einsum('td,dcf->tcf', normed, w_full, preferred_element_type=jnp.floa...]
    reduce_sum x1 -> x0, other arithmetic: 4.62 us -> none  [body(): row_mean = jnp.mean(values, axis=1, keepdims=True)]
    all_to_all x1, blocking collectives: 13.8 us -> 18.3 us  [body(): lax.all_to_all(w_late, 'wid', split_axis=1, concat_axis=0, tiled=True)]
    unnamed x8 -> x10, local copies, waits for them, and re-layouts: 0.02 us -> 3.55 us
    all_to_all x1, starting transfers between devices: 4.99 us -> 7.57 us  [body(): lax.all_to_all(mod_copies, 'wid', split_axis=0, concat_axis=0, tiled=True)]
  transfers between devices with their start and end apart: 5 -> 5, of which waited for: 5 -> 5; matrix products, arithmetic and copies ran while one was open for 4% -> 3% of each run, Pallas kernels for 0% -> 0%
where the time goes in v10:
time: 199 us
  waiting for transfers between devices  107 us (54%)
  Pallas kernels  28.4 us (14%)
  blocking collectives  18.3 us (9%)
  starting transfers between devices  14.9 us (7%)
  between operations  13.9 us (7%)
  local copies, waits for them, and re-layouts  8.39 us (4%)
  matrix products  4.81 us (2%)
  other arithmetic  3.36 us (2%)
    all_gather x1, waiting for transfers between devices, body(): heads = lax.all_gather(attended, 'wid', axis=0, tiled=False)  50.7 us
    all_to_all x1, waiting for transfers between devices, body(): lax.all_to_all(w_copies, 'tok', split_axis=0, concat_axis=0, tiled=True)  28.6 us
    pallas_call x1, Pallas kernels, attention(): pl.pallas_call(attention_kernel, grid=(rows // block,), in_specs=[pl.Bloc...  18.9 us
    all_to_all x1, blocking collectives, body(): lax.all_to_all(w_late, 'wid', split_axis=1, concat_axis=0, tiled=True)  18.3 us
    all_gather x1, waiting for transfers between devices, body(): key_values = lax.all_gather(key_rows, 'tok', axis=0, tiled=True)  13.9 us
    pallas_call x1, Pallas kernels, project(): pl.pallas_call(project_kernel, grid=(rows // block,), in_specs=[pl.BlockS...  9.49 us
    all_gather x1, waiting for transfers between devices, body(): residual_full = lax.all_gather(residual_in, 'wid', axis=1, tiled=True)  8.57 us
    all_to_all x1, starting transfers between devices, body(): lax.all_to_all(mod_copies, 'wid', split_axis=0, concat_axis=0, tiled=True)  7.57 us
  transfers between devices with their start and end apart: 5, of which 5 were waited for; matrix products, arithmetic and copies ran while one was open for 3% of the time, Pallas kernels for 0%

profile of v10, /device:TPU:1, one launch (start us, length us, event | category | flops | bytes accessed | tf_op | source)
XLA Modules:
  0.0 199.0 jit_solution(1473004073242893267)
XLA Ops:
  6.5 0.7 convert_element_type.29
  7.2 0.7 convert_element_type.28
  7.9 1.9 add_convert_fusion
  10.6 0.3 fusion.7
  11.0 0.6 broadcast_in_dim.4
  11.6 7.6 %all-to-all-start = ((bf16[16,2,192]{2,1,0:T(2,128)(2,1)}), bf16[16,2,192]{2,1,0:T(2,128)(2,1)S(1)}, u32[]{:S(2)}, u32[]{:S(2)}) async-start(bf16[16,2,192]{2,1,0:T(2,128)(2,1)} %broadcast_in_dim.4), calls=%async_computation | async-start | bytes 32768 | tf_op jit(solution)/shard_map/all_to_all | solution.py:112
  19.2 1.2 copy.19
  20.3 5.3 %all-to-all-done = bf16[16,2,192]{2,1,0:T(2,128)(2,1)S(1)} async-done(((bf16[16,2,192]{2,1,0:T(2,128)(2,1)}), bf16[16,2,192]{2,1,0:T(2,128)(2,1)S(1)}, u32[]{:S(2)}, u32[]{:S(2)}) %all-to-all-start) | async-done | bytes 12320 | tf_op jit(solution)/shard_map/all_to_all | solution.py:112
  25.6 1.8 broadcast_in_dim.5
  27.4 7.3 %all-to-all-start.1 = ((bf16[8,384,3,128]{1,3,2,0:T(8,128)(2,1)}), bf16[8,384,3,128]{1,3,2,0:T(8,128)(2,1)S(1)}, u32[]{:S(2)}, u32[]{:S(2)}) async-start(bf16[8,384,3,128]{1,3,2,0:T(8,128)(2,1)} %broadcast_in_dim.5), calls=%async_computation.1 | async-start | bytes 4718592 | tf_op jit(solution)/shard_map/all_to_all | solution.py:97
  34.7 0.4 copy.18
  35.1 28.6 %all-to-all-done.1 = bf16[8,384,3,128]{1,3,2,0:T(8,128)(2,1)S(1)} async-done(((bf16[8,384,3,128]{1,3,2,0:T(8,128)(2,1)}), bf16[8,384,3,128]{1,3,2,0:T(8,128)(2,1)S(1)}, u32[]{:S(2)}, u32[]{:S(2)}) %all-to-all-start.1) | async-done | bytes 2359328 | tf_op jit(solution)/shard_map/all_to_all | solution.py:97
  63.7 1.4 copy.20
  65.1 0.5 copy.31
  65.6 8.6 %all-gather.5.cloned.1.call-done = bf16[1024,3072]{0,1:T(8,128)(2,1)} async-done(((bf16[1024,192]{0,1:T(8,128)(2,1)}), bf16[1024,3072]{0,1:T(8,128)(2,1)}) %all-gather.5.cloned.1.call-update) | async-done | bytes 6291472 | tf_op jit(solution)/shard_map/all_gather | solution.py:109
  74.2 9.5 %shard_map.73 = bf16[384,1024]{1,0:T(8,128)(2,1)S(1)} custom-call(bf16[3072,1024]{1,0:T(8,128)(2,1)} %bitcast.49, bf16[3072,2]{1,0:T(8,128)(2,1)S(1)} %bitcast.47, bf16[384,3072]{1,0:T(8,128)(2,1)S(1)} %bitcast.46), custom_call_target="tpu_custom_call" | custom-call | flops 2447376384 | bytes 9437184 | tf_op jit(solution)/shard_map/pallas_call | solution.py:37
  83.8 1.0 copy.28
  84.8 0.8 copy.27
  85.7 0.4 copy.23
  86.1 18.3 %all_to_all.29 = bf16[128,16,192]{0,2,1:T(8,128)(2,1)S(1)} all-to-all(bf16[128,16,192]{0,2,1:T(8,128)(2,1)S(1)} %bitcast.50), channel_id=1, replica_groups=mesh['tok'=8,'wid'=16] {'wid'}, dimensions={1} | all-to-all | bytes 1572864 | tf_op jit(solution)/shard_map/all_to_all | solution.py:118
  104.5 13.9 %all-gather.7.cloned.1.call-done.kv_ref = bf16[8192,256]{1,0:T(8,128)(2,1)} async-done(((bf16[1024,256]{1,0:T(8,128)(2,1)}), bf16[8192,256]{1,0:T(8,128)(2,1)}) %all-gather.7.cloned.1.call-update) | async-done | bytes 4194320 | tf_op jit(solution)/shard_map/all_gather | solution.py:120
  118.4 18.9 %shard_map.74 = bf16[1024,128]{1,0:T(8,128)(2,1)} custom-call(bf16[1024,128]{1,0:T(8,128)(2,1)} %bitcast.52, bf16[8192,256]{1,0:T(8,128)(2,1)} %all-gather.7.cloned.1.call-done.kv_ref), custom_call_target="tpu_custom_call" | custom-call | flops 4294967296 | bytes 4718592 | tf_op jit(solution)/shard_map/pallas_call | solution.py:71
  137.3 50.7 %all-gather.9.cloned.1.call-done = bf16[16384,128]{1,0:T(8,128)(2,1)} async-done(((bf16[1024,128]{1,0:T(8,128)(2,1)}), bf16[16384,128]{1,0:T(8,128)(2,1)}) %all-gather.9.cloned.1.call-update) | async-done | bytes 4194320 | tf_op jit(solution)/shard_map/all_gather | solution.py:123
  188.0 4.5 %fusion.2 = bf16[1024,192]{0,1:T(8,128)(2,1)} fusion(bf16[16,1024,128]{2,1,0:T(8,128)(2,1)} %bitcast.58, bf16[1024,192]{0,1:T(8,128)(2,1)S(1)} %copy-done.1, f32[192]{0:T(256)S(1)} %bitcast.57, bf16[2048,192]{0,1:T(8,128)(2,1)S(1)} %copy_bitcast_fusion), kind=kOutput, calls=%fused_computation.3 | convolution fusion | flops 806092800 | bytes 5767936 | tf_op jit(solution)/shard_map/htd,hdc->tc/dot_general | solution.py:124
  (20 shorter events, 0.4 us)
Async XLA Ops:
  6.5 4.0 %copy-start = (bf16[256,3,192]{0,2,1:T(8,128)(2,1)S(1)}, bf16[256,3,192]{0,2,1:T(8,128)(2,1)}, u32[]{:S(2)}) copy-start(bf16[256,3,192]{0,2,1:T(8,128)(2,1)} %param.11) | copy-start | bytes 884740
  6.5 67.6 %all-gather.5.cloned.1.call-start = ((), (), s32[]{:S(2)}) async-start(), calls=%async_computation.3 | async-start | bytes 6684672 | tf_op jit(solution)/shard_map/all_gather | solution.py:109
  11.6 14.0 %all-to-all-start = ((bf16[16,2,192]{2,1,0:T(2,128)(2,1)}), bf16[16,2,192]{2,1,0:T(2,128)(2,1)S(1)}, u32[]{:S(2)}, u32[]{:S(2)}) async-start(bf16[16,2,192]{2,1,0:T(2,128)(2,1)} %broadcast_in_dim.4), calls=%async_computation | async-start | bytes 32768 | tf_op jit(solution)/shard_map/all_to_all | solution.py:112
  27.4 36.3 %all-to-all-start.1 = ((bf16[8,384,3,128]{1,3,2,0:T(8,128)(2,1)}), bf16[8,384,3,128]{1,3,2,0:T(8,128)(2,1)S(1)}, u32[]{:S(2)}, u32[]{:S(2)}) async-start(bf16[8,384,3,128]{1,3,2,0:T(8,128)(2,1)} %broadcast_in_dim.5), calls=%async_computation.1 | async-start | bytes 4718592 | tf_op jit(solution)/shard_map/all_to_all | solution.py:97
  34.7 83.7 %all-gather.7.cloned.1.call-start = ((), (), s32[]{:S(2)}) async-start(), calls=%async_computation.4 | async-start | bytes 4718592 | tf_op jit(solution)/shard_map/all_gather | solution.py:120
  83.7 2.0 %copy-start.2 = (bf16[128,3072]{1,0:T(8,128)(2,1)S(1)}, bf16[128,3072]{1,0:T(8,128)(2,1)}, u32[]{:S(2)}) copy-start(bf16[128,3072]{1,0:T(8,128)(2,1)} %param.13) | copy-start | bytes 2359300
  85.7 102.3 %all-gather.9.cloned.1.call-start = ((), (), s32[]{:S(2)}) async-start(), calls=%async_computation.5 | async-start | bytes 4456448 | tf_op jit(solution)/shard_map/all_gather | solution.py:123
  104.5 83.5 %copy-start.1 = (bf16[1024,192]{0,1:T(8,128)(2,1)S(1)}, bf16[1024,192]{0,1:T(8,128)(2,1)}, u32[]{:S(2)}) copy-start(bf16[1024,192]{0,1:T(8,128)(2,1)} %add_convert_fusion) | copy-start | bytes 1179652
Sparse Core Ops, SparseCore 0:
  10.0 64.1 all-gather.4
  85.8 32.5 all-gather.6
  137.4 50.4 all-gather.8

commit v11 on v10

--- a/solution.py
+++ b/solution.py
@@ -19,7 +19,7 @@
     )
 
 
-def project_kernel(x_ref, mod_ref, w_ref, o_ref):
+def project_kernel(x_ref, mod_ref, w_ref, q_ref, kv_ref):
     values = x_ref[...].astype(jnp.float32)
     width = values.shape[0]
     row_mean = jnp.sum(values, axis=0, keepdims=True) / width
@@ -28,7 +28,10 @@
     shift_col = mod_ref[:, 0:1].astype(jnp.float32)
     scale_col = mod_ref[:, 1:2].astype(jnp.float32)
     normed = (normal * (1.0 + scale_col) + shift_col).astype(jnp.bfloat16)
-    o_ref[...] = jnp.dot(w_ref[...], normed, preferred_element_type=jnp.float32).astype(o_ref.dtype)
+    qkv_t = jnp.dot(w_ref[...], normed, preferred_element_type=jnp.float32)
+    qkv = jnp.transpose(qkv_t).astype(jnp.bfloat16)
+    q_ref[...] = qkv[:, :DH]
+    kv_ref[...] = qkv[:, DH:]
 
 
 def project(rows_t, mod_cols, weights_t, block=256):
@@ -42,8 +45,14 @@
             pl.BlockSpec(mod_cols.shape, lambda i: (0, 0)),
             pl.BlockSpec(weights_t.shape, lambda i: (0, 0)),
         ],
-        out_specs=pl.BlockSpec((outs, block), lambda i: (0, i)),
-        out_shape=jax.ShapeDtypeStruct((outs, rows), jnp.bfloat16),
+        out_specs=[
+            pl.BlockSpec((block, DH), lambda i: (i, 0)),
+            pl.BlockSpec((block, outs - DH), lambda i: (i, 0)),
+        ],
+        out_shape=[
+            jax.ShapeDtypeStruct((rows, DH), jnp.bfloat16),
+            jax.ShapeDtypeStruct((rows, outs - DH), jnp.bfloat16),
+        ],
         compiler_params=pltpu.CompilerParams(vmem_limit_bytes=48 * 1024 * 1024),
         cost_estimate=pl.CostEstimate(
             flops=2 * rows * width * outs + 10 * rows * width,
@@ -112,8 +121,7 @@
     mod_parts = lax.all_to_all(mod_copies, "wid", split_axis=0, concat_axis=0, tiled=True)
     shift_scale = jnp.transpose(mod_parts, (1, 0, 2)).reshape(2, wid_count * modulation.shape[1])
     weights_t = w_full.reshape(w_full.shape[0], 3 * DH).T
-    qkv_t = project(residual_full.T, shift_scale.T, weights_t)
-    qkv = (qkv_t[:DH].T, qkv_t[DH:].T)
+    qkv = tuple(project(residual_full.T, shift_scale.T, weights_t))
     w_late, qkv = lax.optimization_barrier((w_out, qkv))
     w_cols = lax.all_to_all(w_late, "wid", split_axis=1, concat_axis=0, tiled=True)
     queries, key_rows = qkv

time: 199 us -> 199 us (level)
  waiting for transfers between devices: 107 us -> 105 us
  transfers between devices with their start and end apart: 5 -> 5, of which waited for: 5 -> 5; matrix products, arithmetic and copies ran while one was open for 3% -> 4% of each run, Pallas kernels for 0% -> 0%
where the time goes in v11:
time: 199 us; the launch traced here: 198 us
  waiting for transfers between devices  105 us (53%)
  Pallas kernels  28.4 us (14%)
  blocking collectives  18.3 us (9%)
  starting transfers between devices  15.2 us (8%)
  between operations  13.9 us (7%)
  local copies, waits for them, and re-layouts  9.17 us (5%)
  matrix products  4.81 us (2%)
  other arithmetic  3.36 us (2%)
    all_gather x1, waiting for transfers between devices, body(): heads = lax.all_gather(attended, 'wid', axis=0, tiled=False)  50.7 us
    all_to_all x1, waiting for transfers between devices, body(): lax.all_to_all(w_copies, 'tok', split_axis=0, concat_axis=0, tiled=True)  28.5 us
    pallas_call x1, Pallas kernels, attention(): pl.pallas_call(attention_kernel, grid=(rows // block,), in_specs=[pl.Bloc...  18.9 us
    all_to_all x1, blocking collectives, body(): lax.all_to_all(w_late, 'wid', split_axis=1, concat_axis=0, tiled=True)  18.3 us
    all_gather x1, waiting for transfers between devices, body(): key_values = lax.all_gather(key_rows, 'tok', axis=0, tiled=True)  12.7 us
    pallas_call x1, Pallas kernels, project(): pl.pallas_call(project_kernel, grid=(rows // block,), in_specs=[pl.BlockS...  9.43 us
    all_gather x1, waiting for transfers between devices, body(): residual_full = lax.all_gather(residual_in, 'wid', axis=1, tiled=True)  8.41 us
    all_to_all x1, starting transfers between devices, body(): lax.all_to_all(w_copies, 'tok', split_axis=0, concat_axis=0, tiled=True)  7.57 us
  transfers between devices with their start and end apart: 5, of which 5 were waited for; matrix products, arithmetic and copies ran while one was open for 4% of the time, Pallas kernels for 0%

profile of v11, /device:TPU:1, one launch (start us, length us, event | category | flops | bytes accessed | tf_op | source)
XLA Modules:
  0.0 198.5 jit_solution(4504494894794171632)
XLA Ops:
  6.5 0.7 convert_element_type.29
  7.2 0.7 convert_element_type.28
  7.9 1.9 add_convert_fusion
  10.6 0.3 fusion.7
  11.0 0.6 broadcast_in_dim.4
  11.6 7.6 %all-to-all-start = ((bf16[16,2,192]{2,1,0:T(2,128)(2,1)}), bf16[16,2,192]{2,1,0:T(2,128)(2,1)S(1)}, u32[]{:S(2)}, u32[]{:S(2)}) async-start(bf16[16,2,192]{2,1,0:T(2,128)(2,1)} %broadcast_in_dim.4), calls=%async_computation | async-start | bytes 32768 | tf_op jit(solution)/shard_map/all_to_all | solution.py:121
  19.2 1.2 copy.15
  20.3 5.1 %all-to-all-done = bf16[16,2,192]{2,1,0:T(2,128)(2,1)S(1)} async-done(((bf16[16,2,192]{2,1,0:T(2,128)(2,1)}), bf16[16,2,192]{2,1,0:T(2,128)(2,1)S(1)}, u32[]{:S(2)}, u32[]{:S(2)}) %all-to-all-start) | async-done | bytes 12320 | tf_op jit(solution)/shard_map/all_to_all | solution.py:121
  25.5 1.8 broadcast_in_dim.5
  27.3 7.6 %all-to-all-start.1 = ((bf16[8,384,3,128]{1,3,2,0:T(8,128)(2,1)}), bf16[8,384,3,128]{1,3,2,0:T(8,128)(2,1)S(1)}, u32[]{:S(2)}, u32[]{:S(2)}) async-start(bf16[8,384,3,128]{1,3,2,0:T(8,128)(2,1)} %broadcast_in_dim.5), calls=%async_computation.1 | async-start | bytes 4718592 | tf_op jit(solution)/shard_map/all_to_all | solution.py:106
  34.9 0.5 copy.14
  35.3 28.5 %all-to-all-done.1 = bf16[8,384,3,128]{1,3,2,0:T(8,128)(2,1)S(1)} async-done(((bf16[8,384,3,128]{1,3,2,0:T(8,128)(2,1)}), bf16[8,384,3,128]{1,3,2,0:T(8,128)(2,1)S(1)}, u32[]{:S(2)}, u32[]{:S(2)}) %all-to-all-start.1) | async-done | bytes 2359328 | tf_op jit(solution)/shard_map/all_to_all | solution.py:106
  63.9 1.4 copy.16
  65.3 0.5 copy.23
  65.8 8.4 %all-gather.5.cloned.1.call-done = bf16[1024,3072]{0,1:T(8,128)(2,1)} async-done(((bf16[1024,192]{0,1:T(8,128)(2,1)}), bf16[1024,3072]{0,1:T(8,128)(2,1)}) %all-gather.5.cloned.1.call-update) | async-done | bytes 6291472 | tf_op jit(solution)/shard_map/all_gather | solution.py:118
  74.2 9.4 %shard_map.73 = (bf16[1024,128]{1,0:T(8,128)(2,1)S(1)}, bf16[1024,256]{1,0:T(8,128)(2,1)S(1)}) custom-call(bf16[3072,1024]{1,0:T(8,128)(2,1)} %bitcast.47, bf16[3072,2]{1,0:T(8,128)(2,1)S(1)} %bitcast.45, bf16[384,3072]{1,0:T(8,128)(2,1)S(1)} %bitcast.44), custom_call_target="tpu_custom_call" | custom-call | flops 2447376384 | bytes 9437184 | tf_op jit(solution)/shard_map/pallas_call | solution.py:40
  83.6 0.8 copy-done.1
  84.4 0.7 copy-done.2
  85.2 1.5 copy.17
  86.7 18.3 %all_to_all.29 = bf16[128,16,192]{0,2,1:T(8,128)(2,1)S(1)} all-to-all(bf16[128,16,192]{0,2,1:T(8,128)(2,1)S(1)} %bitcast.48), channel_id=1, replica_groups=mesh['tok'=8,'wid'=16] {'wid'}, dimensions={1} | all-to-all | bytes 1572864 | tf_op jit(solution)/shard_map/all_to_all | solution.py:126
  105.1 12.7 %all-gather.7.cloned.1.call-done.kv_ref = bf16[8192,256]{1,0:T(8,128)(2,1)} async-done(((bf16[1024,256]{1,0:T(8,128)(2,1)}), bf16[8192,256]{1,0:T(8,128)(2,1)}) %all-gather.7.cloned.1.call-update) | async-done | bytes 4194320 | tf_op jit(solution)/shard_map/all_gather | solution.py:128
  117.9 18.9 %shard_map.74 = bf16[1024,128]{1,0:T(8,128)(2,1)} custom-call(bf16[1024,128]{1,0:T(8,128)(2,1)} %copy-done.2, bf16[8192,256]{1,0:T(8,128)(2,1)} %all-gather.7.cloned.1.call-done.kv_ref), custom_call_target="tpu_custom_call" | custom-call | flops 4294967296 | bytes 4718592 | tf_op jit(solution)/shard_map/pallas_call | solution.py:80
  136.8 50.7 %all-gather.9.cloned.1.call-done = bf16[16384,128]{1,0:T(8,128)(2,1)} async-done(((bf16[1024,128]{1,0:T(8,128)(2,1)}), bf16[16384,128]{1,0:T(8,128)(2,1)}) %all-gather.9.cloned.1.call-update) | async-done | bytes 4194320 | tf_op jit(solution)/shard_map/all_gather | solution.py:131
  187.5 4.5 %fusion.2 = bf16[1024,192]{0,1:T(8,128)(2,1)} fusion(bf16[16,1024,128]{2,1,0:T(8,128)(2,1)} %bitcast.54, bf16[1024,192]{0,1:T(8,128)(2,1)S(1)} %copy-done.3, f32[192]{0:T(256)S(1)} %bitcast.53, bf16[2048,192]{0,1:T(8,128)(2,1)S(1)} %copy_bitcast_fusion), kind=kOutput, calls=%fused_computation.3 | convolution fusion | flops 806092800 | bytes 5767936 | tf_op jit(solution)/shard_map/htd,hdc->tc/dot_general | solution.py:132
  (18 shorter events, 0.3 us)
Async XLA Ops:
  6.5 4.0 %copy-start = (bf16[256,3,192]{0,2,1:T(8,128)(2,1)S(1)}, bf16[256,3,192]{0,2,1:T(8,128)(2,1)}, u32[]{:S(2)}) copy-start(bf16[256,3,192]{0,2,1:T(8,128)(2,1)} %param.11) | copy-start | bytes 884740
  6.5 67.6 %all-gather.5.cloned.1.call-start = ((), (), s32[]{:S(2)}) async-start(), calls=%async_computation.3 | async-start | bytes 6684672 | tf_op jit(solution)/shard_map/all_gather | solution.py:118
  11.6 13.9 %all-to-all-start = ((bf16[16,2,192]{2,1,0:T(2,128)(2,1)}), bf16[16,2,192]{2,1,0:T(2,128)(2,1)S(1)}, u32[]{:S(2)}, u32[]{:S(2)}) async-start(bf16[16,2,192]{2,1,0:T(2,128)(2,1)} %broadcast_in_dim.4), calls=%async_computation | async-start | bytes 32768 | tf_op jit(solution)/shard_map/all_to_all | solution.py:121
  27.3 36.6 %all-to-all-start.1 = ((bf16[8,384,3,128]{1,3,2,0:T(8,128)(2,1)}), bf16[8,384,3,128]{1,3,2,0:T(8,128)(2,1)S(1)}, u32[]{:S(2)}, u32[]{:S(2)}) async-start(bf16[8,384,3,128]{1,3,2,0:T(8,128)(2,1)} %broadcast_in_dim.5), calls=%async_computation.1 | async-start | bytes 4718592 | tf_op jit(solution)/shard_map/all_to_all | solution.py:106
  34.8 83.0 %all-gather.7.cloned.1.call-start = ((), (), s32[]{:S(2)}) async-start(), calls=%async_computation.4 | async-start | bytes 4718592 | tf_op jit(solution)/shard_map/all_gather | solution.py:128
  83.6 0.8 copy-start.1
  84.4 0.7 copy-start.2
  85.2 102.3 %all-gather.9.cloned.1.call-start = ((), (), s32[]{:S(2)}) async-start(), calls=%async_computation.5 | async-start | bytes 4456448 | tf_op jit(solution)/shard_map/all_gather | solution.py:131
  105.1 82.4 %copy-start.3 = (bf16[1024,192]{0,1:T(8,128)(2,1)S(1)}, bf16[1024,192]{0,1:T(8,128)(2,1)}, u32[]{:S(2)}) copy-start(bf16[1024,192]{0,1:T(8,128)(2,1)} %add_convert_fusion) | copy-start | bytes 1179652
Sparse Core Ops, SparseCore 0:
  10.0 64.1 all-gather.4
  85.3 32.5 all-gather.6
  136.9 50.4 all-gather.8

commit v12 on v11

--- a/solution.py
+++ b/solution.py
@@ -95,6 +95,35 @@
     )(queries, key_values)
 
 
+def output_kernel(h_ref, w_ref, r_ref, g_ref, o_ref):
+    total = jnp.zeros(o_ref.shape, jnp.float32)
+    for head in range(h_ref.shape[0]):
+        total = total + jnp.dot(h_ref[head], w_ref[head], preferred_element_type=jnp.float32)
+    o_ref[...] = (r_ref[...].astype(jnp.float32) + g_ref[...] * total).astype(o_ref.dtype)
+
+
+def output_projection(heads, w_heads, residual, gate, block=256):
+    count, rows, _ = heads.shape
+    cols = w_heads.shape[2]
+    return pl.pallas_call(
+        output_kernel,
+        grid=(rows // block,),
+        in_specs=[
+            pl.BlockSpec((count, block, DH), lambda i: (0, i, 0)),
+            pl.BlockSpec(w_heads.shape, lambda i: (0, 0, 0)),
+            pl.BlockSpec((block, cols), lambda i: (i, 0)),
+            pl.BlockSpec(gate.shape, lambda i: (0, 0)),
+        ],
+        out_specs=pl.BlockSpec((block, cols), lambda i: (i, 0)),
+        out_shape=jax.ShapeDtypeStruct((rows, cols), jnp.bfloat16),
+        cost_estimate=pl.CostEstimate(
+            flops=2 * count * rows * DH * cols,
+            transcendentals=0,
+            bytes_accessed=2 * heads.size + 2 * w_heads.size + 4 * rows * cols,
+        ),
+    )(heads, w_heads, residual, gate)
+
+
 def body(tokens, defect_mask, timestep, mask_embed, mod_weight, w_qkv, w_out):
     tok_rows = tokens.shape[0]
     residual_in = (
@@ -129,15 +158,12 @@
     w_cols, key_values = lax.optimization_barrier((w_cols, key_values))
     attended = attention(queries, key_values)
     heads = lax.all_gather(attended, "wid", axis=0, tiled=False)
-    projected = jnp.einsum(
-        "htd,hdc->tc",
+    return output_projection(
         heads,
         w_cols.reshape(heads.shape[0], DH, w_cols.shape[1]),
-        preferred_element_type=jnp.float32,
+        residual_in,
+        modulation[2:3].astype(jnp.float32),
     )
-    return (
-        residual_in.astype(jnp.float32) + modulation[2].astype(jnp.float32)[None, :] * projected
-    ).astype(jnp.bfloat16)
 
 
 def solution(mesh):

time: 199 us -> 202 us (1.015)
  Pallas kernels: 28.4 us -> 33.8 us
  matrix products: 4.81 us -> 0.34 us
  local copies, waits for them, and re-layouts: 9.17 us -> 13.5 us
    pallas_call x0 -> x1, Pallas kernels: none -> 5.74 us  [output_projection(): pl.pallas_call(output_kernel, grid=(rows // block,), in_specs=[pl.BlockSp...]
    dot_general x1 -> x0, matrix products: 4.46 us -> none  [body(): jnp.einsum('htd,hdc->tc', heads, w_cols.reshape(heads.shape[0], DH, w_col...]
    convert_element_type x0 -> x2, local copies, waits for them, and re-layouts: none -> 2.15 us  [the longest x1 1.2 us: body(): tokens.astype(jnp.float32)]
where the time goes in v12:
time: 202 us
  waiting for transfers between devices  105 us (52%)
  Pallas kernels  33.8 us (17%)
  blocking collectives  18.3 us (9%)
  starting transfers between devices  15 us (7%)
  between operations  13.9 us (7%)
  local copies, waits for them, and re-layouts  13.5 us (7%)
  other arithmetic  2.24 us (1%)
    all_gather x1, waiting for transfers between devices, body(): heads = lax.all_gather(attended, 'wid', axis=0, tiled=False)  48.8 us
    all_to_all x1, waiting for transfers between devices, body(): lax.all_to_all(w_copies, 'tok', split_axis=0, concat_axis=0, tiled=True)  28.6 us
    pallas_call x1, Pallas kernels, attention(): pl.pallas_call(attention_kernel, grid=(rows // block,), in_specs=[pl.Bloc...  18.9 us
    all_to_all x1, blocking collectives, body(): lax.all_to_all(w_late, 'wid', split_axis=1, concat_axis=0, tiled=True)  18.3 us
    all_gather x1, waiting for transfers between devices, body(): key_values = lax.all_gather(key_rows, 'tok', axis=0, tiled=True)  12.8 us
    pallas_call x1, Pallas kernels, project(): pl.pallas_call(project_kernel, grid=(rows // block,), in_specs=[pl.BlockS...  9.16 us
    all_gather x1, waiting for transfers between devices, body(): residual_full = lax.all_gather(residual_in, 'wid', axis=1, tiled=True)  8.43 us
    all_to_all x1, starting transfers between devices, body(): lax.all_to_all(mod_copies, 'wid', split_axis=0, concat_axis=0, tiled=True)  7.57 us
  transfers between devices with their start and end apart: 5, of which 5 were waited for; matrix products, arithmetic and copies ran while one was open for 4% of the time, Pallas kernels for 0%

profile of v12, /device:TPU:1, one launch (start us, length us, event | category | flops | bytes accessed | tf_op | source)
XLA Modules:
  0.0 201.9 jit_solution(17175505468838386053)
XLA Ops:
  6.5 0.7 convert_element_type.24
  7.3 0.7 convert_element_type.23
  8.0 1.2 copy.37
  9.4 1.0 copy.38
  11.5 0.6 broadcast_in_dim.4
  12.1 7.6 %all-to-all-start = ((bf16[16,2,192]{2,1,0:T(2,128)(2,1)}), bf16[16,2,192]{2,1,0:T(2,128)(2,1)S(1)}, u32[]{:S(2)}, u32[]{:S(2)}) async-start(bf16[16,2,192]{2,1,0:T(2,128)(2,1)} %broadcast_in_dim.4), calls=%async_computation | async-start | bytes 32768 | tf_op jit(solution)/shard_map/all_to_all | solution.py:150
  19.9 6.2 %all-to-all-done = bf16[16,2,192]{2,1,0:T(2,128)(2,1)S(1)} async-done(((bf16[16,2,192]{2,1,0:T(2,128)(2,1)}), bf16[16,2,192]{2,1,0:T(2,128)(2,1)S(1)}, u32[]{:S(2)}, u32[]{:S(2)}) %all-to-all-start) | async-done | bytes 12320 | tf_op jit(solution)/shard_map/all_to_all | solution.py:150
  26.1 1.8 broadcast_in_dim.5
  27.9 7.4 %all-to-all-start.1 = ((bf16[8,384,3,128]{1,3,2,0:T(8,128)(2,1)}), bf16[8,384,3,128]{1,3,2,0:T(8,128)(2,1)S(1)}, u32[]{:S(2)}, u32[]{:S(2)}) async-start(bf16[8,384,3,128]{1,3,2,0:T(8,128)(2,1)} %broadcast_in_dim.5), calls=%async_computation.1 | async-start | bytes 4718592 | tf_op jit(solution)/shard_map/all_to_all | solution.py:135
  35.8 28.6 %all-to-all-done.1 = bf16[8,384,3,128]{1,3,2,0:T(8,128)(2,1)S(1)} async-done(((bf16[8,384,3,128]{1,3,2,0:T(8,128)(2,1)}), bf16[8,384,3,128]{1,3,2,0:T(8,128)(2,1)S(1)}, u32[]{:S(2)}, u32[]{:S(2)}) %all-to-all-start.1) | async-done | bytes 2359328 | tf_op jit(solution)/shard_map/all_to_all | solution.py:135
  64.4 1.4 copy.41
  66.3 8.4 %all-gather.5.cloned.1.call-done = bf16[1024,3072]{0,1:T(8,128)(2,1)} async-done(((bf16[1024,192]{0,1:T(8,128)(2,1)}), bf16[1024,3072]{0,1:T(8,128)(2,1)}) %all-gather.5.cloned.1.call-update) | async-done | bytes 6291472 | tf_op jit(solution)/shard_map/all_gather | solution.py:147
  74.7 9.2 %shard_map.73 = (bf16[1024,128]{1,0:T(8,128)(2,1)S(1)}, bf16[1024,256]{1,0:T(8,128)(2,1)S(1)}) custom-call(bf16[3072,1024]{1,0:T(8,128)(2,1)} %bitcast.31, bf16[3072,2]{1,0:T(8,128)(2,1)S(1)} %bitcast.29, bf16[384,3072]{1,0:T(8,128)(2,1)S(1)} %bitcast.28), custom_call_target="tpu_custom_call" | custom-call | flops 2447376384 | bytes 9437184 | tf_op jit(solution)/shard_map/pallas_call | solution.py:40
  83.9 0.8 copy-done.1
  84.6 0.7 copy-done.2
  85.4 1.5 copy.42
  86.9 18.3 %all_to_all.29 = bf16[128,16,192]{0,2,1:T(8,128)(2,1)S(1)} all-to-all(bf16[128,16,192]{0,2,1:T(8,128)(2,1)S(1)} %bitcast.34), channel_id=1, replica_groups=mesh['tok'=8,'wid'=16] {'wid'}, dimensions={1} | all-to-all | bytes 1572864 | tf_op jit(solution)/shard_map/all_to_all | solution.py:155
  105.3 12.8 %all-gather.7.cloned.1.call-done.kv_ref = bf16[8192,256]{1,0:T(8,128)(2,1)} async-done(((bf16[1024,256]{1,0:T(8,128)(2,1)}), bf16[8192,256]{1,0:T(8,128)(2,1)}) %all-gather.7.cloned.1.call-update) | async-done | bytes 4194320 | tf_op jit(solution)/shard_map/all_gather | solution.py:157
  118.1 18.9 %shard_map.74 = bf16[1024,128]{1,0:T(8,128)(2,1)} custom-call(bf16[1024,128]{1,0:T(8,128)(2,1)} %copy-done.2, bf16[8192,256]{1,0:T(8,128)(2,1)} %all-gather.7.cloned.1.call-done.kv_ref), custom_call_target="tpu_custom_call" | custom-call | flops 4294967296 | bytes 4718592 | tf_op jit(solution)/shard_map/pallas_call | solution.py:80
  137.0 0.6 slice_convert_fusion.g_ref
  137.6 1.3 copy.44
  138.9 48.8 %all-gather.9.cloned.1.call-done = bf16[16384,128]{1,0:T(8,128)(2,1)} async-done(((bf16[1024,128]{1,0:T(8,128)(2,1)}), bf16[16384,128]{1,0:T(8,128)(2,1)}) %all-gather.9.cloned.1.call-update) | async-done | bytes 4194320 | tf_op jit(solution)/shard_map/all_gather | solution.py:160
  187.7 5.7 %shard_map.75 = bf16[1024,192]{1,0:T(8,128)(2,1)} custom-call(bf16[16,1024,128]{2,1,0:T(8,128)(2,1)} %bitcast.32, bf16[16,128,192]{2,1,0:T(8,128)(2,1)} %bitcast.33, bf16[1024,192]{1,0:T(8,128)(2,1)} %copy-done.3, f32[1,192]{1,0:T(1,128)} %slice_convert_fusion.g_ref), custom_call_target="tpu_custom_call" | custom-call | flops 805306368 | bytes 5767168 | tf_op jit(solution)/shard_map/pallas_call | solution.py:108
  193.4 2.0 copy.45
  (24 shorter events, 2.0 us)
Async XLA Ops:
  6.5 4.5 %copy-start = (bf16[256,3,192]{0,2,1:T(8,128)(2,1)S(1)}, bf16[256,3,192]{0,2,1:T(8,128)(2,1)}, u32[]{:S(2)}) copy-start(bf16[256,3,192]{0,2,1:T(8,128)(2,1)} %param.11) | copy-start | bytes 884740
  6.5 13.1 %copy-start.4 = (bf16[384,3,128]{2,0,1:T(8,128)(2,1)S(1)}, bf16[384,3,128]{2,0,1:T(8,128)(2,1)}, u32[]{:S(2)}) copy-start(bf16[384,3,128]{2,0,1:T(8,128)(2,1)} %param.12) | copy-start | bytes 884740
  6.5 68.1 %all-gather.5.cloned.1.call-start = ((), (), s32[]{:S(2)}) async-start(), calls=%async_computation.3 | async-start | bytes 6684672 | tf_op jit(solution)/shard_map/all_gather | solution.py:147
  9.4 18.6 %copy-start.3 = (bf16[1024,192]{1,0:T(8,128)(2,1)}, bf16[1024,192]{1,0:T(8,128)(2,1)S(1)}, u32[]{:S(2)}) copy-start(bf16[1024,192]{1,0:T(8,128)(2,1)S(1)} %add_convert_fusion.r_ref) | copy-start | bytes 1179652
  12.1 14.0 %all-to-all-start = ((bf16[16,2,192]{2,1,0:T(2,128)(2,1)}), bf16[16,2,192]{2,1,0:T(2,128)(2,1)S(1)}, u32[]{:S(2)}, u32[]{:S(2)}) async-start(bf16[16,2,192]{2,1,0:T(2,128)(2,1)} %broadcast_in_dim.4), calls=%async_computation | async-start | bytes 32768 | tf_op jit(solution)/shard_map/all_to_all | solution.py:150
  27.9 36.4 %all-to-all-start.1 = ((bf16[8,384,3,128]{1,3,2,0:T(8,128)(2,1)}), bf16[8,384,3,128]{1,3,2,0:T(8,128)(2,1)S(1)}, u32[]{:S(2)}, u32[]{:S(2)}) async-start(bf16[8,384,3,128]{1,3,2,0:T(8,128)(2,1)} %broadcast_in_dim.5), calls=%async_computation.1 | async-start | bytes 4718592 | tf_op jit(solution)/shard_map/all_to_all | solution.py:135
  35.3 82.7 %all-gather.7.cloned.1.call-start = ((), (), s32[]{:S(2)}) async-start(), calls=%async_computation.4 | async-start | bytes 4718592 | tf_op jit(solution)/shard_map/all_gather | solution.py:157
  83.9 0.8 copy-start.1
  84.6 0.7 copy-start.2
  85.4 102.3 %all-gather.9.cloned.1.call-start = ((), (), s32[]{:S(2)}) async-start(), calls=%async_computation.5 | async-start | bytes 4456448 | tf_op jit(solution)/shard_map/all_gather | solution.py:160
Sparse Core Ops, SparseCore 0:
  10.5 64.1 all-gather.4
  85.5 32.5 all-gather.6
  137.2 50.4 all-gather.8

commit v13 on v11

--- a/solution.py
+++ b/solution.py
@@ -19,7 +19,7 @@
     )
 
 
-def project_kernel(x_ref, mod_ref, w_ref, q_ref, kv_ref):
+def project_kernel(x_ref, mod_ref, w_ref, q_init, kv_init, q_ref, kv_ref):
     values = x_ref[...].astype(jnp.float32)
     width = values.shape[0]
     row_mean = jnp.sum(values, axis=0, keepdims=True) / width
@@ -44,6 +44,8 @@
             pl.BlockSpec((width, block), lambda i: (0, i)),
             pl.BlockSpec(mod_cols.shape, lambda i: (0, 0)),
             pl.BlockSpec(weights_t.shape, lambda i: (0, 0)),
+            pl.BlockSpec(memory_space=pltpu.HBM),
+            pl.BlockSpec(memory_space=pltpu.HBM),
         ],
         out_specs=[
             pl.BlockSpec((block, DH), lambda i: (i, 0)),
@@ -59,7 +61,14 @@
             transcendentals=rows,
             bytes_accessed=2 * rows * width + 2 * width * outs + 2 * rows * outs,
         ),
-    )(rows_t, mod_cols, weights_t)
+        input_output_aliases={3: 0, 4: 1},
+    )(
+        rows_t,
+        mod_cols,
+        weights_t,
+        pltpu.with_memory_space_constraint(jnp.zeros((rows, DH), jnp.bfloat16), pltpu.HBM),
+        pltpu.with_memory_space_constraint(jnp.zeros((rows, outs - DH), jnp.bfloat16), pltpu.HBM),
+    )
 
 
 def attention_kernel(q_ref, kv_ref, o_ref):

time: 199 us -> 200 us (level)
  no operation moved by 1% of the time
where the time goes in v13:
time: 200 us; the launch traced here: 199 us
  waiting for transfers between devices  106 us (53%)
  Pallas kernels  29 us (14%)
  blocking collectives  18.3 us (9%)
  starting transfers between devices  14.9 us (7%)
  between operations  13.8 us (7%)
  local copies, waits for them, and re-layouts  9.25 us (5%)
  matrix products  4.81 us (2%)
  other arithmetic  3.36 us (2%)
    all_gather x1, waiting for transfers between devices, body(): heads = lax.all_gather(attended, 'wid', axis=0, tiled=False)  50.7 us
    all_to_all x1, waiting for transfers between devices, body(): lax.all_to_all(w_copies, 'tok', split_axis=0, concat_axis=0, tiled=True)  28.5 us
    pallas_call x1, Pallas kernels, attention(): pl.pallas_call(attention_kernel, grid=(rows // block,), in_specs=[pl.Bloc...  18.9 us
    all_to_all x1, blocking collectives, body(): lax.all_to_all(w_late, 'wid', split_axis=1, concat_axis=0, tiled=True)  18.3 us
    all_gather x1, waiting for transfers between devices, body(): key_values = lax.all_gather(key_rows, 'tok', axis=0, tiled=True)  12.7 us
    pallas_call x1, Pallas kernels, project(): pl.pallas_call(project_kernel, grid=(rows // block,), in_specs=[pl.BlockS...  10.1 us
    all_gather x1, waiting for transfers between devices, body(): residual_full = lax.all_gather(residual_in, 'wid', axis=1, tiled=True)  8.58 us
    all_to_all x1, starting transfers between devices, body(): lax.all_to_all(mod_copies, 'wid', split_axis=0, concat_axis=0, tiled=True)  7.57 us
  transfers between devices with their start and end apart: 5, of which 5 were waited for; matrix products, arithmetic and copies ran while one was open for 4% of the time, Pallas kernels for 0%

profile of v13, /device:TPU:1, one launch (start us, length us, event | category | flops | bytes accessed | tf_op | source)
XLA Modules:
  0.0 199.2 jit_solution(17759187903165144587)
XLA Ops:
  6.5 0.7 convert_element_type.28
  7.3 0.7 convert_element_type.29
  7.9 1.9 add_convert_fusion
  10.6 0.3 fusion.7
  11.0 0.6 broadcast_in_dim.8
  11.6 7.6 %all-to-all-start = ((bf16[16,2,192]{2,1,0:T(2,128)(2,1)}), bf16[16,2,192]{2,1,0:T(2,128)(2,1)S(1)}, u32[]{:S(2)}, u32[]{:S(2)}) async-start(bf16[16,2,192]{2,1,0:T(2,128)(2,1)} %broadcast_in_dim.8), calls=%async_computation | async-start | bytes 32768 | tf_op jit(solution)/shard_map/all_to_all | solution.py:130
  19.2 1.2 copy.17
  20.3 5.3 %all-to-all-done = bf16[16,2,192]{2,1,0:T(2,128)(2,1)S(1)} async-done(((bf16[16,2,192]{2,1,0:T(2,128)(2,1)}), bf16[16,2,192]{2,1,0:T(2,128)(2,1)S(1)}, u32[]{:S(2)}, u32[]{:S(2)}) %all-to-all-start) | async-done | bytes 12320 | tf_op jit(solution)/shard_map/all_to_all | solution.py:130
  25.6 1.8 broadcast_in_dim.9
  27.4 7.3 %all-to-all-start.1 = ((bf16[8,384,3,128]{1,3,2,0:T(8,128)(2,1)}), bf16[8,384,3,128]{1,3,2,0:T(8,128)(2,1)S(1)}, u32[]{:S(2)}, u32[]{:S(2)}) async-start(bf16[8,384,3,128]{1,3,2,0:T(8,128)(2,1)} %broadcast_in_dim.9), calls=%async_computation.1 | async-start | bytes 4718592 | tf_op jit(solution)/shard_map/all_to_all | solution.py:115
  34.7 0.5 copy.16
  35.2 28.5 %all-to-all-done.1 = bf16[8,384,3,128]{1,3,2,0:T(8,128)(2,1)S(1)} async-done(((bf16[8,384,3,128]{1,3,2,0:T(8,128)(2,1)}), bf16[8,384,3,128]{1,3,2,0:T(8,128)(2,1)S(1)}, u32[]{:S(2)}, u32[]{:S(2)}) %all-to-all-start.1) | async-done | bytes 2359328 | tf_op jit(solution)/shard_map/all_to_all | solution.py:115
  63.7 1.4 copy.18
  65.1 0.5 copy.25
  65.6 8.6 %all-gather.5.cloned.1.call-done = bf16[1024,3072]{0,1:T(8,128)(2,1)} async-done(((bf16[1024,192]{0,1:T(8,128)(2,1)}), bf16[1024,3072]{0,1:T(8,128)(2,1)}) %all-gather.5.cloned.1.call-update) | async-done | bytes 6291472 | tf_op jit(solution)/shard_map/all_gather | solution.py:127
  74.2 0.8 broadcast_in_dim.11.kv_init
  75.0 0.7 broadcast_in_dim.10.q_init
  75.8 10.1 %shard_map.73 = (bf16[1024,128]{1,0:T(8,128)(2,1)}, bf16[1024,256]{1,0:T(8,128)(2,1)}) custom-call(bf16[3072,1024]{1,0:T(8,128)(2,1)} %bitcast.47, bf16[3072,2]{1,0:T(8,128)(2,1)S(1)} %bitcast.45, bf16[384,3072]{1,0:T(8,128)(2,1)S(1)} %bitcast.44, bf16[1024,128]{1,0:T(8,128)(2,1)} %broadcast_in_dim.10.q_init, ...), custom_call_target="tpu_custom_call", output_to_operand_aliasing={{0}: (3, {}), {1}: (4, {})} | custom-call | flops 2447376384 | bytes 9437184 | tf_op jit(solution)/shard_map/pallas_call | solution.py:40
  85.9 1.5 copy.19
  87.5 18.3 %all_to_all.29 = bf16[128,16,192]{0,2,1:T(8,128)(2,1)S(1)} all-to-all(bf16[128,16,192]{0,2,1:T(8,128)(2,1)S(1)} %bitcast.48), channel_id=1, replica_groups=mesh['tok'=8,'wid'=16] {'wid'}, dimensions={1} | all-to-all | bytes 1572864 | tf_op jit(solution)/shard_map/all_to_all | solution.py:135
  105.9 12.7 %all-gather.7.cloned.1.call-done.kv_ref = bf16[8192,256]{1,0:T(8,128)(2,1)} async-done(((bf16[1024,256]{1,0:T(8,128)(2,1)}), bf16[8192,256]{1,0:T(8,128)(2,1)}) %all-gather.7.cloned.1.call-update) | async-done | bytes 4194320 | tf_op jit(solution)/shard_map/all_gather | solution.py:137
  118.6 18.9 %shard_map.74 = bf16[1024,128]{1,0:T(8,128)(2,1)} custom-call(bf16[1024,128]{1,0:T(8,128)(2,1)} %get-tuple-element.14.q_ref, bf16[8192,256]{1,0:T(8,128)(2,1)} %all-gather.7.cloned.1.call-done.kv_ref), custom_call_target="tpu_custom_call" | custom-call | flops 4294967296 | bytes 4718592 | tf_op jit(solution)/shard_map/pallas_call | solution.py:89
  137.6 50.7 %all-gather.9.cloned.1.call-done = bf16[16384,128]{1,0:T(8,128)(2,1)} async-done(((bf16[1024,128]{1,0:T(8,128)(2,1)}), bf16[16384,128]{1,0:T(8,128)(2,1)}) %all-gather.9.cloned.1.call-update) | async-done | bytes 4194320 | tf_op jit(solution)/shard_map/all_gather | solution.py:140
  188.2 4.5 %fusion.2 = bf16[1024,192]{0,1:T(8,128)(2,1)} fusion(bf16[16,1024,128]{2,1,0:T(8,128)(2,1)} %bitcast.54, bf16[1024,192]{0,1:T(8,128)(2,1)S(1)} %copy-done.1, f32[192]{0:T(256)S(1)} %bitcast.53, bf16[2048,192]{0,1:T(8,128)(2,1)S(1)} %copy_bitcast_fusion), kind=kOutput, calls=%fused_computation.3 | convolution fusion | flops 806092800 | bytes 5767936 | tf_op jit(solution)/shard_map/htd,hdc->tc/dot_general | solution.py:141
  (16 shorter events, 0.3 us)
Async XLA Ops:
  6.5 4.0 %copy-start = (bf16[256,3,192]{0,2,1:T(8,128)(2,1)S(1)}, bf16[256,3,192]{0,2,1:T(8,128)(2,1)}, u32[]{:S(2)}) copy-start(bf16[256,3,192]{0,2,1:T(8,128)(2,1)} %param.11) | copy-start | bytes 884740
  6.5 67.6 %all-gather.5.cloned.1.call-start = ((), (), s32[]{:S(2)}) async-start(), calls=%async_computation.3 | async-start | bytes 6684672 | tf_op jit(solution)/shard_map/all_gather | solution.py:127
  11.6 14.0 %all-to-all-start = ((bf16[16,2,192]{2,1,0:T(2,128)(2,1)}), bf16[16,2,192]{2,1,0:T(2,128)(2,1)S(1)}, u32[]{:S(2)}, u32[]{:S(2)}) async-start(bf16[16,2,192]{2,1,0:T(2,128)(2,1)} %broadcast_in_dim.8), calls=%async_computation | async-start | bytes 32768 | tf_op jit(solution)/shard_map/all_to_all | solution.py:130
  27.4 36.3 %all-to-all-start.1 = ((bf16[8,384,3,128]{1,3,2,0:T(8,128)(2,1)}), bf16[8,384,3,128]{1,3,2,0:T(8,128)(2,1)S(1)}, u32[]{:S(2)}, u32[]{:S(2)}) async-start(bf16[8,384,3,128]{1,3,2,0:T(8,128)(2,1)} %broadcast_in_dim.9), calls=%async_computation.1 | async-start | bytes 4718592 | tf_op jit(solution)/shard_map/all_to_all | solution.py:115
  34.7 83.9 %all-gather.7.cloned.1.call-start = ((), (), s32[]{:S(2)}) async-start(), calls=%async_computation.4 | async-start | bytes 4718592 | tf_op jit(solution)/shard_map/all_gather | solution.py:137
  85.9 102.3 %all-gather.9.cloned.1.call-start = ((), (), s32[]{:S(2)}) async-start(), calls=%async_computation.5 | async-start | bytes 4456448 | tf_op jit(solution)/shard_map/all_gather | solution.py:140
  105.8 82.4 %copy-start.1 = (bf16[1024,192]{0,1:T(8,128)(2,1)S(1)}, bf16[1024,192]{0,1:T(8,128)(2,1)}, u32[]{:S(2)}) copy-start(bf16[1024,192]{0,1:T(8,128)(2,1)} %add_convert_fusion) | copy-start | bytes 1179652
Sparse Core Ops, SparseCore 0:
  10.0 64.1 all-gather.4
  86.0 32.5 all-gather.6
  137.7 50.4 all-gather.8

commit v14 on v13

--- a/solution.py
+++ b/solution.py
@@ -34,7 +34,7 @@
     kv_ref[...] = qkv[:, DH:]
 
 
-def project(rows_t, mod_cols, weights_t, block=256):
+def project(rows_t, mod_cols, weights_t, q_init, kv_init, block=256):
     width, rows = rows_t.shape
     outs = weights_t.shape[0]
     return pl.pallas_call(
@@ -66,8 +66,8 @@
         rows_t,
         mod_cols,
         weights_t,
-        pltpu.with_memory_space_constraint(jnp.zeros((rows, DH), jnp.bfloat16), pltpu.HBM),
-        pltpu.with_memory_space_constraint(jnp.zeros((rows, outs - DH), jnp.bfloat16), pltpu.HBM),
+        pltpu.with_memory_space_constraint(q_init, pltpu.HBM),
+        pltpu.with_memory_space_constraint(kv_init, pltpu.HBM),
     )
 
 
@@ -129,8 +129,11 @@
     mod_copies = jnp.broadcast_to(modulation[None, :2], (wid_count, 2, modulation.shape[1]))
     mod_parts = lax.all_to_all(mod_copies, "wid", split_axis=0, concat_axis=0, tiled=True)
     shift_scale = jnp.transpose(mod_parts, (1, 0, 2)).reshape(2, wid_count * modulation.shape[1])
+    q_init = residual_in[:, :DH]
+    kv_init = jnp.concatenate([q_init, q_init], axis=1)
+    q_init, kv_init, w_full = lax.optimization_barrier((q_init, kv_init, w_full))
     weights_t = w_full.reshape(w_full.shape[0], 3 * DH).T
-    qkv = tuple(project(residual_full.T, shift_scale.T, weights_t))
+    qkv = tuple(project(residual_full.T, shift_scale.T, weights_t, q_init, kv_init))
     w_late, qkv = lax.optimization_barrier((w_out, qkv))
     w_cols = lax.all_to_all(w_late, "wid", split_axis=1, concat_axis=0, tiled=True)
     queries, key_rows = qkv

time: 200 us -> 198 us (0.990)
  local copies, waits for them, and re-layouts: 9.25 us -> 14.3 us
  waiting for transfers between devices: 106 us -> 101 us
    all_gather x1, waiting for transfers between devices: 8.58 us -> 4.86 us  [body(): residual_full = lax.all_gather(residual_in, 'wid', axis=1, tiled=True)]
    convert_element_type x0 -> x3, local copies, waits for them, and re-layouts: none -> 3.14 us  [the longest x1 1.26 us: body(): tokens.astype(jnp.float32)]
    optimization_barrier x0 -> x1, local copies, waits for them, and re-layouts: none -> 2.87 us  [body(): lax.optimization_barrier((q_init, kv_init, w_full))]
  transfers between devices with their start and end apart: 5 -> 5, of which waited for: 5 -> 5; matrix products, arithmetic and copies ran while one was open for 4% -> 6% of each run, Pallas kernels for 0% -> 0%
where the time goes in v14:
time: 198 us
  waiting for transfers between devices  101 us (51%)
  Pallas kernels  28.7 us (14%)
  blocking collectives  18.3 us (9%)
  starting transfers between devices  15 us (8%)
  local copies, waits for them, and re-layouts  14.3 us (7%)
  between operations  13.9 us (7%)
  matrix products  3.8 us (2%)
  other arithmetic  2.48 us (1%)
    all_gather x1, waiting for transfers between devices, body(): heads = lax.all_gather(attended, 'wid', axis=0, tiled=False)  50.7 us
    all_to_all x1, waiting for transfers between devices, body(): lax.all_to_all(w_copies, 'tok', split_axis=0, concat_axis=0, tiled=True)  26.7 us
    pallas_call x1, Pallas kernels, attention(): pl.pallas_call(attention_kernel, grid=(rows // block,), in_specs=[pl.Bloc...  18.9 us
    all_to_all x1, blocking collectives, body(): lax.all_to_all(w_late, 'wid', split_axis=1, concat_axis=0, tiled=True)  18.3 us
    all_gather x1, waiting for transfers between devices, body(): key_values = lax.all_gather(key_rows, 'tok', axis=0, tiled=True)  12.8 us
    pallas_call x1, Pallas kernels, project(): pl.pallas_call(project_kernel, grid=(rows // block,), in_specs=[pl.BlockS...  9.81 us
    all_to_all x1, starting transfers between devices, body(): lax.all_to_all(mod_copies, 'wid', split_axis=0, concat_axis=0, tiled=True)  7.57 us
    all_to_all x1, starting transfers between devices, body(): lax.all_to_all(w_copies, 'tok', split_axis=0, concat_axis=0, tiled=True)  7.42 us
  transfers between devices with their start and end apart: 5, of which 5 were waited for; matrix products, arithmetic and copies ran while one was open for 6% of the time, Pallas kernels for 0%

profile of v14, /device:TPU:1, one launch (start us, length us, event | category | flops | bytes accessed | tf_op | source)
XLA Modules:
  0.0 197.8 jit_solution(1201633753604061171)
XLA Ops:
  6.5 1.3 copy.44
  7.8 0.7 convert_element_type.28
  8.5 0.7 convert_element_type.29
  9.4 0.9 copy.45
  11.5 0.6 broadcast_in_dim.4
  12.1 7.6 %all-to-all-start = ((bf16[16,2,192]{2,1,0:T(2,128)(2,1)}), bf16[16,2,192]{2,1,0:T(2,128)(2,1)S(1)}, u32[]{:S(2)}, u32[]{:S(2)}) async-start(bf16[16,2,192]{2,1,0:T(2,128)(2,1)} %broadcast_in_dim.4), calls=%async_computation | async-start | bytes 32768 | tf_op jit(solution)/shard_map/all_to_all | solution.py:130
  19.9 6.2 %all-to-all-done = bf16[16,2,192]{2,1,0:T(2,128)(2,1)S(1)} async-done(((bf16[16,2,192]{2,1,0:T(2,128)(2,1)}), bf16[16,2,192]{2,1,0:T(2,128)(2,1)S(1)}, u32[]{:S(2)}, u32[]{:S(2)}) %all-to-all-start) | async-done | bytes 12320 | tf_op jit(solution)/shard_map/all_to_all | solution.py:130
  26.1 1.8 broadcast_in_dim.5
  27.9 7.4 %all-to-all-start.1 = ((bf16[8,384,3,128]{1,3,2,0:T(8,128)(2,1)}), bf16[8,384,3,128]{1,3,2,0:T(8,128)(2,1)S(1)}, u32[]{:S(2)}, u32[]{:S(2)}) async-start(bf16[8,384,3,128]{1,3,2,0:T(8,128)(2,1)} %broadcast_in_dim.5), calls=%async_computation.1 | async-start | bytes 4718592 | tf_op jit(solution)/shard_map/all_to_all | solution.py:115
  35.3 1.0 slice.14.q_init
  36.3 0.9 pad_maximum_fusion.kv_init
  37.2 0.4 copy.46
  37.6 26.7 %all-to-all-done.1 = bf16[8,384,3,128]{1,3,2,0:T(8,128)(2,1)S(1)} async-done(((bf16[8,384,3,128]{1,3,2,0:T(8,128)(2,1)}), bf16[8,384,3,128]{1,3,2,0:T(8,128)(2,1)S(1)}, u32[]{:S(2)}, u32[]{:S(2)}) %all-to-all-start.1) | async-done | bytes 2359328 | tf_op jit(solution)/shard_map/all_to_all | solution.py:115
  64.3 2.6 %copy.48 = bf16[8,384,3,128]{3,1,0,2:T(8,128)(2,1)} copy(bf16[8,384,3,128]{1,3,2,0:T(8,128)(2,1)S(1)} %all-to-all-done.1) | data formatting | bytes 4718592 | tf_op jit(solution)/shard_map/all_to_all | solution.py:115
  66.9 2.9 %copy.49 = bf16[3072,3,128]{0,2,1:T(8,128)(2,1)S(1)} copy(bf16[3072,3,128]{2,0,1:T(8,128)(2,1)} %bitcast.43) | data formatting | bytes 4718592 | tf_op jit(solution)/shard_map/optimization_barrier | solution.py:134
  69.8 4.9 %all-gather.5.cloned.1.call-done = bf16[1024,3072]{0,1:T(8,128)(2,1)} async-done(((bf16[1024,192]{0,1:T(8,128)(2,1)}), bf16[1024,3072]{0,1:T(8,128)(2,1)}) %all-gather.5.cloned.1.call-update) | async-done | bytes 6291472 | tf_op jit(solution)/shard_map/all_gather | solution.py:127
  74.7 9.8 %shard_map.73 = (bf16[1024,128]{1,0:T(8,128)(2,1)}, bf16[1024,256]{1,0:T(8,128)(2,1)}) custom-call(bf16[3072,1024]{1,0:T(8,128)(2,1)} %bitcast.44, bf16[3072,2]{1,0:T(8,128)(2,1)S(1)} %bitcast.42, bf16[384,3072]{1,0:T(8,128)(2,1)S(1)} %bitcast.41, bf16[1024,128]{1,0:T(8,128)(2,1)} %copy-done.3, ...), custom_call_target="tpu_custom_call", output_to_operand_aliasing={{0}: (3, {}), {1}: (4, {})} | custom-call | flops 2447376384 | bytes 9437184 | tf_op jit(solution)/shard_map/pallas_call | solution.py:40
  84.6 1.5 copy.50
  86.1 18.3 %all_to_all.29 = bf16[128,16,192]{0,2,1:T(8,128)(2,1)S(1)} all-to-all(bf16[128,16,192]{0,2,1:T(8,128)(2,1)S(1)} %bitcast.45), channel_id=1, replica_groups=mesh['tok'=8,'wid'=16] {'wid'}, dimensions={1} | all-to-all | bytes 1572864 | tf_op jit(solution)/shard_map/all_to_all | solution.py:138
  104.5 12.8 %all-gather.7.cloned.1.call-done.kv_ref = bf16[8192,256]{1,0:T(8,128)(2,1)} async-done(((bf16[1024,256]{1,0:T(8,128)(2,1)}), bf16[8192,256]{1,0:T(8,128)(2,1)}) %all-gather.7.cloned.1.call-update) | async-done | bytes 4194320 | tf_op jit(solution)/shard_map/all_gather | solution.py:140
  117.2 18.9 %shard_map.74 = bf16[1024,128]{1,0:T(8,128)(2,1)} custom-call(bf16[1024,128]{1,0:T(8,128)(2,1)} %get-tuple-element.20.q_ref, bf16[8192,256]{1,0:T(8,128)(2,1)} %all-gather.7.cloned.1.call-done.kv_ref), custom_call_target="tpu_custom_call" | custom-call | flops 4294967296 | bytes 4718592 | tf_op jit(solution)/shard_map/pallas_call | solution.py:89
  136.2 50.7 %all-gather.9.cloned.1.call-done = bf16[16384,128]{1,0:T(8,128)(2,1)} async-done(((bf16[1024,128]{1,0:T(8,128)(2,1)}), bf16[16384,128]{1,0:T(8,128)(2,1)}) %all-gather.9.cloned.1.call-update) | async-done | bytes 4194320 | tf_op jit(solution)/shard_map/all_gather | solution.py:143
  186.8 3.5 %fusion.2 = bf16[1024,192]{1,0:T(8,128)(2,1)S(1)} fusion(bf16[16,1024,128]{2,1,0:T(8,128)(2,1)} %bitcast.51, bf16[1024,192]{1,0:T(8,128)(2,1)S(1)} %copy-done.2, f32[192]{0:T(256)S(1)} %bitcast.50, bf16[2048,192]{0,1:T(8,128)(2,1)S(1)} %copy_bitcast_fusion), kind=kOutput, calls=%fused_computation.3 | convolution fusion | flops 806092800 | bytes 5767936 | tf_op jit(solution)/shard_map/htd,hdc->tc/dot_general | solution.py:144
  190.3 0.9 copy.54
  (25 shorter events, 1.1 us)
Async XLA Ops:
  6.5 4.5 %copy-start = (bf16[256,3,192]{0,2,1:T(8,128)(2,1)S(1)}, bf16[256,3,192]{0,2,1:T(8,128)(2,1)}, u32[]{:S(2)}) copy-start(bf16[256,3,192]{0,2,1:T(8,128)(2,1)} %param.11) | copy-start | bytes 884740
  6.5 13.1 %copy-start.4 = (bf16[384,3,128]{2,0,1:T(8,128)(2,1)S(1)}, bf16[384,3,128]{2,0,1:T(8,128)(2,1)}, u32[]{:S(2)}) copy-start(bf16[384,3,128]{2,0,1:T(8,128)(2,1)} %param.12) | copy-start | bytes 884740
  6.5 68.1 %all-gather.5.cloned.1.call-start = ((), (), s32[]{:S(2)}) async-start(), calls=%async_computation.3 | async-start | bytes 6684672 | tf_op jit(solution)/shard_map/all_gather | solution.py:127
  9.4 18.5 %copy-start.1 = (bf16[1024,192]{1,0:T(8,128)(2,1)}, bf16[1024,192]{1,0:T(8,128)(2,1)S(1)}, u32[]{:S(2)}) copy-start(bf16[1024,192]{1,0:T(8,128)(2,1)S(1)} %add_convert_fusion) | copy-start | bytes 1179652
  12.1 14.0 %all-to-all-start = ((bf16[16,2,192]{2,1,0:T(2,128)(2,1)}), bf16[16,2,192]{2,1,0:T(2,128)(2,1)S(1)}, u32[]{:S(2)}, u32[]{:S(2)}) async-start(bf16[16,2,192]{2,1,0:T(2,128)(2,1)} %broadcast_in_dim.4), calls=%async_computation | async-start | bytes 32768 | tf_op jit(solution)/shard_map/all_to_all | solution.py:130
  27.9 36.4 %all-to-all-start.1 = ((bf16[8,384,3,128]{1,3,2,0:T(8,128)(2,1)}), bf16[8,384,3,128]{1,3,2,0:T(8,128)(2,1)S(1)}, u32[]{:S(2)}, u32[]{:S(2)}) async-start(bf16[8,384,3,128]{1,3,2,0:T(8,128)(2,1)} %broadcast_in_dim.5), calls=%async_computation.1 | async-start | bytes 4718592 | tf_op jit(solution)/shard_map/all_to_all | solution.py:115
  35.3 81.9 %all-gather.7.cloned.1.call-start = ((), (), s32[]{:S(2)}) async-start(), calls=%async_computation.4 | async-start | bytes 4718592 | tf_op jit(solution)/shard_map/all_gather | solution.py:140
  36.3 0.9 copy-start.3
  84.5 102.3 %all-gather.9.cloned.1.call-start = ((), (), s32[]{:S(2)}) async-start(), calls=%async_computation.5 | async-start | bytes 4456448 | tf_op jit(solution)/shard_map/all_gather | solution.py:143
  104.4 82.4 %copy-start.2 = (bf16[1024,192]{1,0:T(8,128)(2,1)S(1)}, bf16[1024,192]{1,0:T(8,128)(2,1)}, u32[]{:S(2)}) copy-start(bf16[1024,192]{1,0:T(8,128)(2,1)} %copy-done.1) | copy-start | bytes 1179652
Sparse Core Ops, SparseCore 0:
  10.5 64.1 all-gather.4
  84.6 32.5 all-gather.6
  136.3 50.4 all-gather.8

commit v15 on v14

--- a/solution.py
+++ b/solution.py
@@ -129,8 +129,9 @@
     mod_copies = jnp.broadcast_to(modulation[None, :2], (wid_count, 2, modulation.shape[1]))
     mod_parts = lax.all_to_all(mod_copies, "wid", split_axis=0, concat_axis=0, tiled=True)
     shift_scale = jnp.transpose(mod_parts, (1, 0, 2)).reshape(2, wid_count * modulation.shape[1])
-    q_init = residual_in[:, :DH]
-    kv_init = jnp.concatenate([q_init, q_init], axis=1)
+    w_rows = w_full.reshape(w_full.shape[0], 3 * DH)[:tok_rows]
+    q_init = w_rows[:, :DH]
+    kv_init = w_rows[:, DH:]
     q_init, kv_init, w_full = lax.optimization_barrier((q_init, kv_init, w_full))
     weights_t = w_full.reshape(w_full.shape[0], 3 * DH).T
     qkv = tuple(project(residual_full.T, shift_scale.T, weights_t, q_init, kv_init))

time: 198 us -> 198 us (level)
  local copies, waits for them, and re-layouts: 14.3 us -> 18.9 us
  waiting for transfers between devices: 101 us -> 96.6 us
  blocking collectives: 18.3 us -> 16.2 us
    all_gather x1, waiting for transfers between devices: 4.86 us -> 0.02 us  [body(): residual_full = lax.all_gather(residual_in, 'wid', axis=1, tiled=True)]
    another operation x0 -> x1, local copies, waits for them, and re-layouts: none -> 3.83 us  [body(): w_rows = w_full.reshape(w_full.shape[0], 3 * DH)[:tok_rows]]
    unnamed x11 -> x6, local copies, waits for them, and re-layouts: 0.24 us -> 3.48 us
    convert_element_type x3 -> x0, local copies, waits for them, and re-layouts: 3.14 us -> none  [the longest x1 1.26 us: body(): tokens.astype(jnp.float32)]
    all_to_all x1, blocking collectives: 18.3 us -> 16.2 us  [body(): lax.all_to_all(w_late, 'wid', split_axis=1, concat_axis=0, tiled=True)]
  transfers between devices with their start and end apart: 5 -> 5, of which waited for: 5 -> 4; matrix products, arithmetic and copies ran while one was open for 6% -> 10% of each run, Pallas kernels for 0% -> 0%
where the time goes in v15:
time: 198 us; the launch traced here: 197 us
  waiting for transfers between devices  96.6 us (49%)
  Pallas kernels  28.8 us (15%)
  local copies, waits for them, and re-layouts  18.9 us (10%)
  blocking collectives  16.2 us (8%)
  starting transfers between devices  14.9 us (8%)
  between operations  13.8 us (7%)
  matrix products  4.8 us (2%)
  other arithmetic  3.36 us (2%)
    all_gather x1, waiting for transfers between devices, body(): heads = lax.all_gather(attended, 'wid', axis=0, tiled=False)  50.7 us
    all_to_all x1, waiting for transfers between devices, body(): lax.all_to_all(w_copies, 'tok', split_axis=0, concat_axis=0, tiled=True)  28.6 us
    pallas_call x1, Pallas kernels, attention(): pl.pallas_call(attention_kernel, grid=(rows // block,), in_specs=[pl.Bloc...  18.9 us
    all_to_all x1, blocking collectives, body(): lax.all_to_all(w_late, 'wid', split_axis=1, concat_axis=0, tiled=True)  16.2 us
    all_gather x1, waiting for transfers between devices, body(): key_values = lax.all_gather(key_rows, 'tok', axis=0, tiled=True)  12.1 us
    pallas_call x1, Pallas kernels, project(): pl.pallas_call(project_kernel, grid=(rows // block,), in_specs=[pl.BlockS...  9.83 us
    all_to_all x1, starting transfers between devices, body(): lax.all_to_all(mod_copies, 'wid', split_axis=0, concat_axis=0, tiled=True)  7.57 us
    all_to_all x1, starting transfers between devices, body(): lax.all_to_all(w_copies, 'tok', split_axis=0, concat_axis=0, tiled=True)  7.27 us
  transfers between devices with their start and end apart: 5, of which 4 were waited for; matrix products, arithmetic and copies ran while one was open for 10% of the time, Pallas kernels for 0%

profile of v15, /device:TPU:1, one launch (start us, length us, event | category | flops | bytes accessed | tf_op | source)
XLA Modules:
  0.0 197.3 jit_solution(16515278199816405946)
XLA Ops:
  6.5 0.7 convert_element_type.28
  7.3 0.7 convert_element_type.29
  7.9 1.9 add_convert_fusion
  11.0 0.6 broadcast_in_dim.4
  11.6 7.6 %all-to-all-start = ((bf16[16,2,192]{2,1,0:T(2,128)(2,1)}), bf16[16,2,192]{2,1,0:T(2,128)(2,1)S(1)}, u32[]{:S(2)}, u32[]{:S(2)}) async-start(bf16[16,2,192]{2,1,0:T(2,128)(2,1)} %broadcast_in_dim.4), calls=%async_computation | async-start | bytes 32768 | tf_op jit(solution)/shard_map/all_to_all | solution.py:130
  19.2 1.2 copy.28
  20.3 5.3 %all-to-all-done = bf16[16,2,192]{2,1,0:T(2,128)(2,1)S(1)} async-done(((bf16[16,2,192]{2,1,0:T(2,128)(2,1)}), bf16[16,2,192]{2,1,0:T(2,128)(2,1)S(1)}, u32[]{:S(2)}, u32[]{:S(2)}) %all-to-all-start) | async-done | bytes 12320 | tf_op jit(solution)/shard_map/all_to_all | solution.py:130
  25.6 1.8 broadcast_in_dim.5
  27.4 7.3 %all-to-all-start.1 = ((bf16[8,384,3,128]{1,3,2,0:T(8,128)(2,1)}), bf16[8,384,3,128]{1,3,2,0:T(8,128)(2,1)S(1)}, u32[]{:S(2)}, u32[]{:S(2)}) async-start(bf16[8,384,3,128]{1,3,2,0:T(8,128)(2,1)} %broadcast_in_dim.5), calls=%async_computation.1 | async-start | bytes 4718592 | tf_op jit(solution)/shard_map/all_to_all | solution.py:115
  34.7 0.4 copy.27
  35.1 28.6 %all-to-all-done.1 = bf16[8,384,3,128]{1,3,2,0:T(8,128)(2,1)S(1)} async-done(((bf16[8,384,3,128]{1,3,2,0:T(8,128)(2,1)}), bf16[8,384,3,128]{1,3,2,0:T(8,128)(2,1)S(1)}, u32[]{:S(2)}, u32[]{:S(2)}) %all-to-all-start.1) | async-done | bytes 2359328 | tf_op jit(solution)/shard_map/all_to_all | solution.py:115
  63.7 3.8 %copy.38 = bf16[8,384,3,128]{3,2,1,0:T(4,128)(2,1)} copy(bf16[8,384,3,128]{1,3,2,0:T(8,128)(2,1)S(1)} %all-to-all-done.1) | data formatting | bytes 4718592 | tf_op jit(solution)/shard_map/reshape;reshape | solution.py:132
  67.5 2.3 %copy.50 = bf16[384,8,3,128]{3,1,2,0:T(8,128)(2,1)S(1)} copy(bf16[384,8,3,128]{3,2,1,0:T(4,128)(2,1)} %bitcast.48) | data formatting | bytes 4718592
  69.8 0.9 slice.22.kv_init
  70.7 0.7 slice.21.q_init
  71.5 2.6 %copy.32 = bf16[8,384,3,128]{3,1,0,2:T(8,128)(2,1)} copy(bf16[8,384,3,128]{1,3,2,0:T(8,128)(2,1)S(1)} %all-to-all-done.1) | data formatting | bytes 4718592 | tf_op jit(solution)/shard_map/all_to_all | solution.py:115
  74.0 2.8 %copy.33 = bf16[3072,3,128]{0,2,1:T(8,128)(2,1)S(1)} copy(bf16[3072,3,128]{2,0,1:T(8,128)(2,1)} %bitcast.49) | data formatting | bytes 4718592 | tf_op jit(solution)/shard_map/optimization_barrier | solution.py:135
  76.9 9.8 %shard_map.73 = (bf16[1024,128]{1,0:T(8,128)(2,1)}, bf16[1024,256]{1,0:T(8,128)(2,1)}) custom-call(bf16[3072,1024]{1,0:T(8,128)(2,1)} %bitcast.50, bf16[3072,2]{1,0:T(8,128)(2,1)S(1)} %bitcast.47, bf16[384,3072]{1,0:T(8,128)(2,1)S(1)} %bitcast.46, bf16[1024,128]{1,0:T(8,128)(2,1)} %slice.21.q_init, ...), custom_call_target="tpu_custom_call", output_to_operand_aliasing={{0}: (3, {}), {1}: (4, {})} | custom-call | flops 2447376384 | bytes 9437184 | tf_op jit(solution)/shard_map/pallas_call | solution.py:40
  86.8 1.5 copy.34
  88.3 16.2 %all_to_all.29 = bf16[128,16,192]{0,2,1:T(8,128)(2,1)S(1)} all-to-all(bf16[128,16,192]{0,2,1:T(8,128)(2,1)S(1)} %bitcast.53), channel_id=1, replica_groups=mesh['tok'=8,'wid'=16] {'wid'}, dimensions={1} | all-to-all | bytes 1572864 | tf_op jit(solution)/shard_map/all_to_all | solution.py:139
  104.7 12.1 %all-gather.7.cloned.1.call-done.kv_ref = bf16[8192,256]{1,0:T(8,128)(2,1)} async-done(((bf16[1024,256]{1,0:T(8,128)(2,1)}), bf16[8192,256]{1,0:T(8,128)(2,1)}) %all-gather.7.cloned.1.call-update) | async-done | bytes 4194320 | tf_op jit(solution)/shard_map/all_gather | solution.py:141
  116.7 18.9 %shard_map.74 = bf16[1024,128]{1,0:T(8,128)(2,1)} custom-call(bf16[1024,128]{1,0:T(8,128)(2,1)} %get-tuple-element.20.q_ref, bf16[8192,256]{1,0:T(8,128)(2,1)} %all-gather.7.cloned.1.call-done.kv_ref), custom_call_target="tpu_custom_call" | custom-call | flops 4294967296 | bytes 4718592 | tf_op jit(solution)/shard_map/pallas_call | solution.py:89
  135.7 50.7 %all-gather.9.cloned.1.call-done = bf16[16384,128]{1,0:T(8,128)(2,1)} async-done(((bf16[1024,128]{1,0:T(8,128)(2,1)}), bf16[16384,128]{1,0:T(8,128)(2,1)}) %all-gather.9.cloned.1.call-update) | async-done | bytes 4194320 | tf_op jit(solution)/shard_map/all_gather | solution.py:144
  186.4 4.5 %fusion.2 = bf16[1024,192]{0,1:T(8,128)(2,1)} fusion(bf16[16,1024,128]{2,1,0:T(8,128)(2,1)} %bitcast.59, bf16[1024,192]{0,1:T(8,128)(2,1)S(1)} %copy-done.1, f32[192]{0:T(256)S(1)} %bitcast.58, bf16[2048,192]{0,1:T(8,128)(2,1)S(1)} %copy_bitcast_fusion.1), kind=kOutput, calls=%fused_computation.4 | convolution fusion | flops 806092800 | bytes 5767936 | tf_op jit(solution)/shard_map/htd,hdc->tc/dot_general | solution.py:145
  (18 shorter events, 0.7 us)
Async XLA Ops:
  6.5 4.0 %copy-start = (bf16[256,3,192]{0,2,1:T(8,128)(2,1)S(1)}, bf16[256,3,192]{0,2,1:T(8,128)(2,1)}, u32[]{:S(2)}) copy-start(bf16[256,3,192]{0,2,1:T(8,128)(2,1)} %param.11) | copy-start | bytes 884740
  6.5 70.4 %all-gather.5.cloned.1.call-start = ((), (), s32[]{:S(2)}) async-start(), calls=%async_computation.3 | async-start | bytes 6684672 | tf_op jit(solution)/shard_map/all_gather | solution.py:127
  11.6 14.0 %all-to-all-start = ((bf16[16,2,192]{2,1,0:T(2,128)(2,1)}), bf16[16,2,192]{2,1,0:T(2,128)(2,1)S(1)}, u32[]{:S(2)}, u32[]{:S(2)}) async-start(bf16[16,2,192]{2,1,0:T(2,128)(2,1)} %broadcast_in_dim.4), calls=%async_computation | async-start | bytes 32768 | tf_op jit(solution)/shard_map/all_to_all | solution.py:130
  27.4 36.3 %all-to-all-start.1 = ((bf16[8,384,3,128]{1,3,2,0:T(8,128)(2,1)}), bf16[8,384,3,128]{1,3,2,0:T(8,128)(2,1)S(1)}, u32[]{:S(2)}, u32[]{:S(2)}) async-start(bf16[8,384,3,128]{1,3,2,0:T(8,128)(2,1)} %broadcast_in_dim.5), calls=%async_computation.1 | async-start | bytes 4718592 | tf_op jit(solution)/shard_map/all_to_all | solution.py:115
  34.7 82.0 %all-gather.7.cloned.1.call-start = ((), (), s32[]{:S(2)}) async-start(), calls=%async_computation.4 | async-start | bytes 4718592 | tf_op jit(solution)/shard_map/all_gather | solution.py:141
  86.8 99.6 %all-gather.9.cloned.1.call-start = ((), (), s32[]{:S(2)}) async-start(), calls=%async_computation.5 | async-start | bytes 4456448 | tf_op jit(solution)/shard_map/all_gather | solution.py:144
  104.7 81.7 %copy-start.1 = (bf16[1024,192]{0,1:T(8,128)(2,1)S(1)}, bf16[1024,192]{0,1:T(8,128)(2,1)}, u32[]{:S(2)}) copy-start(bf16[1024,192]{0,1:T(8,128)(2,1)} %add_convert_fusion) | copy-start | bytes 1179652
Sparse Core Ops, SparseCore 0:
  10.0 64.1 all-gather.4
  86.9 29.8 all-gather.6
  135.8 50.4 all-gather.8

commit v16 on v15

--- a/solution.py
+++ b/solution.py
@@ -106,10 +106,7 @@
 
 def body(tokens, defect_mask, timestep, mask_embed, mod_weight, w_qkv, w_out):
     tok_rows = tokens.shape[0]
-    residual_in = (
-        tokens.astype(jnp.float32)
-        + defect_mask.astype(jnp.float32)[:, None] * mask_embed.astype(jnp.float32)[None, :]
-    ).astype(jnp.bfloat16)
+    residual_in = tokens + defect_mask.astype(jnp.bfloat16)[:, None] * mask_embed[None, :]
     tok_count = lax.axis_size("tok")
     w_copies = jnp.broadcast_to(w_qkv[None], (tok_count,) + w_qkv.shape)
     w_full = lax.all_to_all(w_copies, "tok", split_axis=0, concat_axis=0, tiled=True)

time: 198 us -> 197 us (level)
    convert_element_type x3 -> x1, other arithmetic: 3.29 us -> 0.73 us  [body(): defect_mask.astype(jnp.bfloat16)[:, None] * mask_embed[None, :]]
where the time goes in v16:
time: 197 us
  waiting for transfers between devices  96.9 us (49%)
  Pallas kernels  28.8 us (15%)
  local copies, waits for them, and re-layouts  18.9 us (10%)
  blocking collectives  16.1 us (8%)
  starting transfers between devices  14.9 us (8%)
  between operations  13.8 us (7%)
  matrix products  4.8 us (2%)
  other arithmetic  2.65 us (1%)
    all_gather x1, waiting for transfers between devices, body(): heads = lax.all_gather(attended, 'wid', axis=0, tiled=False)  50.7 us
    all_to_all x1, waiting for transfers between devices, body(): lax.all_to_all(w_copies, 'tok', split_axis=0, concat_axis=0, tiled=True)  28.6 us
    pallas_call x1, Pallas kernels, attention(): pl.pallas_call(attention_kernel, grid=(rows // block,), in_specs=[pl.Bloc...  18.9 us
    all_to_all x1, blocking collectives, body(): lax.all_to_all(w_late, 'wid', split_axis=1, concat_axis=0, tiled=True)  16.1 us
    all_gather x1, waiting for transfers between devices, body(): key_values = lax.all_gather(key_rows, 'tok', axis=0, tiled=True)  12.3 us
    pallas_call x1, Pallas kernels, project(): pl.pallas_call(project_kernel, grid=(rows // block,), in_specs=[pl.BlockS...  9.82 us
    all_to_all x1, starting transfers between devices, body(): lax.all_to_all(mod_copies, 'wid', split_axis=0, concat_axis=0, tiled=True)  7.57 us
    all_to_all x1, starting transfers between devices, body(): lax.all_to_all(w_copies, 'tok', split_axis=0, concat_axis=0, tiled=True)  7.31 us
  transfers between devices with their start and end apart: 5, of which 4 were waited for; matrix products, arithmetic and copies ran while one was open for 10% of the time, Pallas kernels for 0%

profile of v16, /device:TPU:1, one launch (start us, length us, event | category | flops | bytes accessed | tf_op | source)
XLA Modules:
  0.0 196.8 jit_solution(2097011154058205010)
XLA Ops:
  6.5 0.7 convert_element_type.18
  7.3 1.8 multiply_add_fusion
  9.9 0.3 fusion.7
  10.3 0.6 broadcast_in_dim.4
  10.9 7.6 %all-to-all-start = ((bf16[16,2,192]{2,1,0:T(2,128)(2,1)}), bf16[16,2,192]{2,1,0:T(2,128)(2,1)S(1)}, u32[]{:S(2)}, u32[]{:S(2)}) async-start(bf16[16,2,192]{2,1,0:T(2,128)(2,1)} %broadcast_in_dim.4), calls=%async_computation | async-start | bytes 32768 | tf_op jit(solution)/shard_map/all_to_all | solution.py:127
  18.5 1.2 copy.28
  19.6 5.3 %all-to-all-done = bf16[16,2,192]{2,1,0:T(2,128)(2,1)S(1)} async-done(((bf16[16,2,192]{2,1,0:T(2,128)(2,1)}), bf16[16,2,192]{2,1,0:T(2,128)(2,1)S(1)}, u32[]{:S(2)}, u32[]{:S(2)}) %all-to-all-start) | async-done | bytes 12320 | tf_op jit(solution)/shard_map/all_to_all | solution.py:127
  24.9 1.8 broadcast_in_dim.5
  26.7 7.3 %all-to-all-start.1 = ((bf16[8,384,3,128]{1,3,2,0:T(8,128)(2,1)}), bf16[8,384,3,128]{1,3,2,0:T(8,128)(2,1)S(1)}, u32[]{:S(2)}, u32[]{:S(2)}) async-start(bf16[8,384,3,128]{1,3,2,0:T(8,128)(2,1)} %broadcast_in_dim.5), calls=%async_computation.1 | async-start | bytes 4718592 | tf_op jit(solution)/shard_map/all_to_all | solution.py:112
  34.0 0.4 copy.27
  34.5 28.6 %all-to-all-done.1 = bf16[8,384,3,128]{1,3,2,0:T(8,128)(2,1)S(1)} async-done(((bf16[8,384,3,128]{1,3,2,0:T(8,128)(2,1)}), bf16[8,384,3,128]{1,3,2,0:T(8,128)(2,1)S(1)}, u32[]{:S(2)}, u32[]{:S(2)}) %all-to-all-start.1) | async-done | bytes 2359328 | tf_op jit(solution)/shard_map/all_to_all | solution.py:112
  63.0 3.8 %copy.38 = bf16[8,384,3,128]{3,2,1,0:T(4,128)(2,1)} copy(bf16[8,384,3,128]{1,3,2,0:T(8,128)(2,1)S(1)} %all-to-all-done.1) | data formatting | bytes 4718592 | tf_op jit(solution)/shard_map/reshape;reshape | solution.py:129
  66.9 2.3 %copy.50 = bf16[384,8,3,128]{3,1,2,0:T(8,128)(2,1)S(1)} copy(bf16[384,8,3,128]{3,2,1,0:T(4,128)(2,1)} %bitcast.48) | data formatting | bytes 4718592
  69.2 0.9 slice.22.kv_init
  70.1 0.7 slice.21.q_init
  70.8 2.6 %copy.32 = bf16[8,384,3,128]{3,1,0,2:T(8,128)(2,1)} copy(bf16[8,384,3,128]{1,3,2,0:T(8,128)(2,1)S(1)} %all-to-all-done.1) | data formatting | bytes 4718592 | tf_op jit(solution)/shard_map/all_to_all | solution.py:112
  73.4 2.8 %copy.33 = bf16[3072,3,128]{0,2,1:T(8,128)(2,1)S(1)} copy(bf16[3072,3,128]{2,0,1:T(8,128)(2,1)} %bitcast.49) | data formatting | bytes 4718592 | tf_op jit(solution)/shard_map/optimization_barrier | solution.py:132
  76.2 9.8 %shard_map.73 = (bf16[1024,128]{1,0:T(8,128)(2,1)}, bf16[1024,256]{1,0:T(8,128)(2,1)}) custom-call(bf16[3072,1024]{1,0:T(8,128)(2,1)} %bitcast.50, bf16[3072,2]{1,0:T(8,128)(2,1)S(1)} %bitcast.47, bf16[384,3072]{1,0:T(8,128)(2,1)S(1)} %bitcast.46, bf16[1024,128]{1,0:T(8,128)(2,1)} %slice.21.q_init, ...), custom_call_target="tpu_custom_call", output_to_operand_aliasing={{0}: (3, {}), {1}: (4, {})} | custom-call | flops 2447376384 | bytes 9437184 | tf_op jit(solution)/shard_map/pallas_call | solution.py:40
  86.1 1.5 copy.34
  87.6 16.1 %all_to_all.29 = bf16[128,16,192]{0,2,1:T(8,128)(2,1)S(1)} all-to-all(bf16[128,16,192]{0,2,1:T(8,128)(2,1)S(1)} %bitcast.53), channel_id=1, replica_groups=mesh['tok'=8,'wid'=16] {'wid'}, dimensions={1} | all-to-all | bytes 1572864 | tf_op jit(solution)/shard_map/all_to_all | solution.py:136
  103.9 12.3 %all-gather.7.cloned.1.call-done.kv_ref = bf16[8192,256]{1,0:T(8,128)(2,1)} async-done(((bf16[1024,256]{1,0:T(8,128)(2,1)}), bf16[8192,256]{1,0:T(8,128)(2,1)}) %all-gather.7.cloned.1.call-update) | async-done | bytes 4194320 | tf_op jit(solution)/shard_map/all_gather | solution.py:138
  116.2 18.9 %shard_map.74 = bf16[1024,128]{1,0:T(8,128)(2,1)} custom-call(bf16[1024,128]{1,0:T(8,128)(2,1)} %get-tuple-element.20.q_ref, bf16[8192,256]{1,0:T(8,128)(2,1)} %all-gather.7.cloned.1.call-done.kv_ref), custom_call_target="tpu_custom_call" | custom-call | flops 4294967296 | bytes 4718592 | tf_op jit(solution)/shard_map/pallas_call | solution.py:89
  135.2 50.7 %all-gather.9.cloned.1.call-done = bf16[16384,128]{1,0:T(8,128)(2,1)} async-done(((bf16[1024,128]{1,0:T(8,128)(2,1)}), bf16[16384,128]{1,0:T(8,128)(2,1)}) %all-gather.9.cloned.1.call-update) | async-done | bytes 4194320 | tf_op jit(solution)/shard_map/all_gather | solution.py:141
  185.8 4.5 %fusion.2 = bf16[1024,192]{0,1:T(8,128)(2,1)} fusion(bf16[16,1024,128]{2,1,0:T(8,128)(2,1)} %bitcast.59, bf16[1024,192]{0,1:T(8,128)(2,1)S(1)} %copy-done.1, f32[192]{0:T(256)S(1)} %bitcast.58, bf16[2048,192]{0,1:T(8,128)(2,1)S(1)} %copy_bitcast_fusion.1), kind=kOutput, calls=%fused_computation.4 | convolution fusion | flops 806092800 | bytes 5767936 | tf_op jit(solution)/shard_map/htd,hdc->tc/dot_general | solution.py:142
  (17 shorter events, 0.3 us)
Async XLA Ops:
  6.5 3.3 %copy-start = (bf16[256,3,192]{0,2,1:T(8,128)(2,1)S(1)}, bf16[256,3,192]{0,2,1:T(8,128)(2,1)}, u32[]{:S(2)}) copy-start(bf16[256,3,192]{0,2,1:T(8,128)(2,1)} %param.11) | copy-start | bytes 884740
  6.5 69.7 %all-gather.5.cloned.1.call-start = ((), (), s32[]{:S(2)}) async-start(), calls=%async_computation.3 | async-start | bytes 6684672 | tf_op jit(solution)/shard_map/all_gather | solution.py:124
  10.9 14.0 %all-to-all-start = ((bf16[16,2,192]{2,1,0:T(2,128)(2,1)}), bf16[16,2,192]{2,1,0:T(2,128)(2,1)S(1)}, u32[]{:S(2)}, u32[]{:S(2)}) async-start(bf16[16,2,192]{2,1,0:T(2,128)(2,1)} %broadcast_in_dim.4), calls=%async_computation | async-start | bytes 32768 | tf_op jit(solution)/shard_map/all_to_all | solution.py:127
  26.7 36.3 %all-to-all-start.1 = ((bf16[8,384,3,128]{1,3,2,0:T(8,128)(2,1)}), bf16[8,384,3,128]{1,3,2,0:T(8,128)(2,1)S(1)}, u32[]{:S(2)}, u32[]{:S(2)}) async-start(bf16[8,384,3,128]{1,3,2,0:T(8,128)(2,1)} %broadcast_in_dim.5), calls=%async_computation.1 | async-start | bytes 4718592 | tf_op jit(solution)/shard_map/all_to_all | solution.py:112
  34.0 82.2 %all-gather.7.cloned.1.call-start = ((), (), s32[]{:S(2)}) async-start(), calls=%async_computation.4 | async-start | bytes 4718592 | tf_op jit(solution)/shard_map/all_gather | solution.py:138
  86.1 99.8 %all-gather.9.cloned.1.call-start = ((), (), s32[]{:S(2)}) async-start(), calls=%async_computation.5 | async-start | bytes 4456448 | tf_op jit(solution)/shard_map/all_gather | solution.py:141
  103.9 81.9 %copy-start.1 = (bf16[1024,192]{0,1:T(8,128)(2,1)S(1)}, bf16[1024,192]{0,1:T(8,128)(2,1)}, u32[]{:S(2)}) copy-start(bf16[1024,192]{0,1:T(8,128)(2,1)} %multiply_add_fusion) | copy-start | bytes 1179652
Sparse Core Ops, SparseCore 0:
  9.5 64.1 all-gather.4
  86.2 29.9 all-gather.6
  135.3 50.4 all-gather.8

commit v17 on v16

--- a/solution.py
+++ b/solution.py
@@ -34,7 +34,7 @@
     kv_ref[...] = qkv[:, DH:]
 
 
-def project(rows_t, mod_cols, weights_t, q_init, kv_init, block=256):
+def project(rows_t, mod_cols, weights_t, q_init, kv_init, block=512):
     width, rows = rows_t.shape
     outs = weights_t.shape[0]
     return pl.pallas_call(

time: 197 us -> 196 us (level)
  no operation moved by 1% of the time
where the time goes in v17:
time: 196 us
  waiting for transfers between devices  96.9 us (49%)
  Pallas kernels  27.9 us (14%)
  local copies, waits for them, and re-layouts  18.9 us (10%)
  blocking collectives  16.1 us (8%)
  starting transfers between devices  14.9 us (8%)
  between operations  13.8 us (7%)
  matrix products  4.8 us (2%)
  other arithmetic  2.65 us (1%)
    all_gather x1, waiting for transfers between devices, body(): heads = lax.all_gather(attended, 'wid', axis=0, tiled=False)  50.7 us
    all_to_all x1, waiting for transfers between devices, body(): lax.all_to_all(w_copies, 'tok', split_axis=0, concat_axis=0, tiled=True)  28.6 us
    pallas_call x1, Pallas kernels, attention(): pl.pallas_call(attention_kernel, grid=(rows // block,), in_specs=[pl.Bloc...  18.9 us
    all_to_all x1, blocking collectives, body(): lax.all_to_all(w_late, 'wid', split_axis=1, concat_axis=0, tiled=True)  16.1 us
    all_gather x1, waiting for transfers between devices, body(): key_values = lax.all_gather(key_rows, 'tok', axis=0, tiled=True)  12.3 us
    pallas_call x1, Pallas kernels, project(): pl.pallas_call(project_kernel, grid=(rows // block,), in_specs=[pl.BlockS...  8.93 us
    all_to_all x1, starting transfers between devices, body(): lax.all_to_all(mod_copies, 'wid', split_axis=0, concat_axis=0, tiled=True)  7.57 us
    all_to_all x1, starting transfers between devices, body(): lax.all_to_all(w_copies, 'tok', split_axis=0, concat_axis=0, tiled=True)  7.31 us
  transfers between devices with their start and end apart: 5, of which 4 were waited for; matrix products, arithmetic and copies ran while one was open for 10% of the time, Pallas kernels for 0%

profile of v17, /device:TPU:1, one launch (start us, length us, event | category | flops | bytes accessed | tf_op | source)
XLA Modules:
  0.0 195.9 jit_solution(5180225196112477401)
XLA Ops:
  6.5 0.7 convert_element_type.18
  7.3 1.8 multiply_add_fusion
  9.9 0.3 fusion.7
  10.3 0.6 broadcast_in_dim.4
  10.9 7.6 %all-to-all-start = ((bf16[16,2,192]{2,1,0:T(2,128)(2,1)}), bf16[16,2,192]{2,1,0:T(2,128)(2,1)S(1)}, u32[]{:S(2)}, u32[]{:S(2)}) async-start(bf16[16,2,192]{2,1,0:T(2,128)(2,1)} %broadcast_in_dim.4), calls=%async_computation | async-start | bytes 32768 | tf_op jit(solution)/shard_map/all_to_all | solution.py:127
  18.5 1.2 copy.28
  19.6 5.3 %all-to-all-done = bf16[16,2,192]{2,1,0:T(2,128)(2,1)S(1)} async-done(((bf16[16,2,192]{2,1,0:T(2,128)(2,1)}), bf16[16,2,192]{2,1,0:T(2,128)(2,1)S(1)}, u32[]{:S(2)}, u32[]{:S(2)}) %all-to-all-start) | async-done | bytes 12320 | tf_op jit(solution)/shard_map/all_to_all | solution.py:127
  24.9 1.8 broadcast_in_dim.5
  26.7 7.3 %all-to-all-start.1 = ((bf16[8,384,3,128]{1,3,2,0:T(8,128)(2,1)}), bf16[8,384,3,128]{1,3,2,0:T(8,128)(2,1)S(1)}, u32[]{:S(2)}, u32[]{:S(2)}) async-start(bf16[8,384,3,128]{1,3,2,0:T(8,128)(2,1)} %broadcast_in_dim.5), calls=%async_computation.1 | async-start | bytes 4718592 | tf_op jit(solution)/shard_map/all_to_all | solution.py:112
  34.0 0.4 copy.27
  34.5 28.6 %all-to-all-done.1 = bf16[8,384,3,128]{1,3,2,0:T(8,128)(2,1)S(1)} async-done(((bf16[8,384,3,128]{1,3,2,0:T(8,128)(2,1)}), bf16[8,384,3,128]{1,3,2,0:T(8,128)(2,1)S(1)}, u32[]{:S(2)}, u32[]{:S(2)}) %all-to-all-start.1) | async-done | bytes 2359328 | tf_op jit(solution)/shard_map/all_to_all | solution.py:112
  63.0 3.8 %copy.38 = bf16[8,384,3,128]{3,2,1,0:T(4,128)(2,1)} copy(bf16[8,384,3,128]{1,3,2,0:T(8,128)(2,1)S(1)} %all-to-all-done.1) | data formatting | bytes 4718592 | tf_op jit(solution)/shard_map/reshape;reshape | solution.py:129
  66.9 2.3 %copy.50 = bf16[384,8,3,128]{3,1,2,0:T(8,128)(2,1)S(1)} copy(bf16[384,8,3,128]{3,2,1,0:T(4,128)(2,1)} %bitcast.48) | data formatting | bytes 4718592
  69.2 0.9 slice.22.kv_init
  70.1 0.7 slice.21.q_init
  70.8 2.6 %copy.32 = bf16[8,384,3,128]{3,1,0,2:T(8,128)(2,1)} copy(bf16[8,384,3,128]{1,3,2,0:T(8,128)(2,1)S(1)} %all-to-all-done.1) | data formatting | bytes 4718592 | tf_op jit(solution)/shard_map/all_to_all | solution.py:112
  73.4 2.8 %copy.33 = bf16[3072,3,128]{0,2,1:T(8,128)(2,1)S(1)} copy(bf16[3072,3,128]{2,0,1:T(8,128)(2,1)} %bitcast.49) | data formatting | bytes 4718592 | tf_op jit(solution)/shard_map/optimization_barrier | solution.py:132
  76.2 8.9 %shard_map.73 = (bf16[1024,128]{1,0:T(8,128)(2,1)}, bf16[1024,256]{1,0:T(8,128)(2,1)}) custom-call(bf16[3072,1024]{1,0:T(8,128)(2,1)} %bitcast.50, bf16[3072,2]{1,0:T(8,128)(2,1)S(1)} %bitcast.47, bf16[384,3072]{1,0:T(8,128)(2,1)S(1)} %bitcast.46, bf16[1024,128]{1,0:T(8,128)(2,1)} %slice.21.q_init, ...), custom_call_target="tpu_custom_call", output_to_operand_aliasing={{0}: (3, {}), {1}: (4, {})} | custom-call | flops 2447376384 | bytes 9437184 | tf_op jit(solution)/shard_map/pallas_call | solution.py:40
  85.2 1.5 copy.34
  86.8 16.1 %all_to_all.29 = bf16[128,16,192]{0,2,1:T(8,128)(2,1)S(1)} all-to-all(bf16[128,16,192]{0,2,1:T(8,128)(2,1)S(1)} %bitcast.53), channel_id=1, replica_groups=mesh['tok'=8,'wid'=16] {'wid'}, dimensions={1} | all-to-all | bytes 1572864 | tf_op jit(solution)/shard_map/all_to_all | solution.py:136
  103.0 12.3 %all-gather.7.cloned.1.call-done.kv_ref = bf16[8192,256]{1,0:T(8,128)(2,1)} async-done(((bf16[1024,256]{1,0:T(8,128)(2,1)}), bf16[8192,256]{1,0:T(8,128)(2,1)}) %all-gather.7.cloned.1.call-update) | async-done | bytes 4194320 | tf_op jit(solution)/shard_map/all_gather | solution.py:138
  115.3 18.9 %shard_map.74 = bf16[1024,128]{1,0:T(8,128)(2,1)} custom-call(bf16[1024,128]{1,0:T(8,128)(2,1)} %get-tuple-element.20.q_ref, bf16[8192,256]{1,0:T(8,128)(2,1)} %all-gather.7.cloned.1.call-done.kv_ref), custom_call_target="tpu_custom_call" | custom-call | flops 4294967296 | bytes 4718592 | tf_op jit(solution)/shard_map/pallas_call | solution.py:89
  134.3 50.7 %all-gather.9.cloned.1.call-done = bf16[16384,128]{1,0:T(8,128)(2,1)} async-done(((bf16[1024,128]{1,0:T(8,128)(2,1)}), bf16[16384,128]{1,0:T(8,128)(2,1)}) %all-gather.9.cloned.1.call-update) | async-done | bytes 4194320 | tf_op jit(solution)/shard_map/all_gather | solution.py:141
  184.9 4.5 %fusion.2 = bf16[1024,192]{0,1:T(8,128)(2,1)} fusion(bf16[16,1024,128]{2,1,0:T(8,128)(2,1)} %bitcast.59, bf16[1024,192]{0,1:T(8,128)(2,1)S(1)} %copy-done.1, f32[192]{0:T(256)S(1)} %bitcast.58, bf16[2048,192]{0,1:T(8,128)(2,1)S(1)} %copy_bitcast_fusion.1), kind=kOutput, calls=%fused_computation.4 | convolution fusion | flops 806092800 | bytes 5767936 | tf_op jit(solution)/shard_map/htd,hdc->tc/dot_general | solution.py:142
  (17 shorter events, 0.3 us)
Async XLA Ops:
  6.5 3.3 %copy-start = (bf16[256,3,192]{0,2,1:T(8,128)(2,1)S(1)}, bf16[256,3,192]{0,2,1:T(8,128)(2,1)}, u32[]{:S(2)}) copy-start(bf16[256,3,192]{0,2,1:T(8,128)(2,1)} %param.11) | copy-start | bytes 884740
  6.5 69.7 %all-gather.5.cloned.1.call-start = ((), (), s32[]{:S(2)}) async-start(), calls=%async_computation.3 | async-start | bytes 6684672 | tf_op jit(solution)/shard_map/all_gather | solution.py:124
  10.9 14.0 %all-to-all-start = ((bf16[16,2,192]{2,1,0:T(2,128)(2,1)}), bf16[16,2,192]{2,1,0:T(2,128)(2,1)S(1)}, u32[]{:S(2)}, u32[]{:S(2)}) async-start(bf16[16,2,192]{2,1,0:T(2,128)(2,1)} %broadcast_in_dim.4), calls=%async_computation | async-start | bytes 32768 | tf_op jit(solution)/shard_map/all_to_all | solution.py:127
  26.7 36.3 %all-to-all-start.1 = ((bf16[8,384,3,128]{1,3,2,0:T(8,128)(2,1)}), bf16[8,384,3,128]{1,3,2,0:T(8,128)(2,1)S(1)}, u32[]{:S(2)}, u32[]{:S(2)}) async-start(bf16[8,384,3,128]{1,3,2,0:T(8,128)(2,1)} %broadcast_in_dim.5), calls=%async_computation.1 | async-start | bytes 4718592 | tf_op jit(solution)/shard_map/all_to_all | solution.py:112
  34.0 81.3 %all-gather.7.cloned.1.call-start = ((), (), s32[]{:S(2)}) async-start(), calls=%async_computation.4 | async-start | bytes 4718592 | tf_op jit(solution)/shard_map/all_gather | solution.py:138
  85.2 99.8 %all-gather.9.cloned.1.call-start = ((), (), s32[]{:S(2)}) async-start(), calls=%async_computation.5 | async-start | bytes 4456448 | tf_op jit(solution)/shard_map/all_gather | solution.py:141
  103.0 81.9 %copy-start.1 = (bf16[1024,192]{0,1:T(8,128)(2,1)S(1)}, bf16[1024,192]{0,1:T(8,128)(2,1)}, u32[]{:S(2)}) copy-start(bf16[1024,192]{0,1:T(8,128)(2,1)} %multiply_add_fusion) | copy-start | bytes 1179652
Sparse Core Ops, SparseCore 0:
  9.5 64.1 all-gather.4
  85.3 29.9 all-gather.6
  134.4 50.4 all-gather.8

commit v18 on v17

--- a/solution.py
+++ b/solution.py
@@ -20,9 +20,11 @@
 
 
 def project_kernel(x_ref, mod_ref, w_ref, q_init, kv_init, q_ref, kv_ref):
-    values = x_ref[...].astype(jnp.float32)
+    rows = x_ref[...]
+    values = rows.astype(jnp.float32)
     width = values.shape[0]
-    row_mean = jnp.sum(values, axis=0, keepdims=True) / width
+    ones = jnp.ones((8, width), jnp.bfloat16)
+    row_mean = jnp.dot(ones, rows, preferred_element_type=jnp.float32)[0:1] / width
     row_var = jnp.sum(values * values, axis=0, keepdims=True) / width - row_mean * row_mean
     normal = (values - row_mean) * lax.rsqrt(row_var + 1e-06)
     shift_col = mod_ref[:, 0:1].astype(jnp.float32)

time: 196 us -> 195 us (level)
  no operation moved by 1% of the time
where the time goes in v18:
time: 195 us
  waiting for transfers between devices  96.8 us (50%)
  Pallas kernels  26.5 us (14%)
  local copies, waits for them, and re-layouts  18.9 us (10%)
  blocking collectives  16.1 us (8%)
  starting transfers between devices  14.9 us (8%)
  between operations  13.8 us (7%)
  matrix products  4.8 us (2%)
  other arithmetic  2.65 us (1%)
    all_gather x1, waiting for transfers between devices, body(): heads = lax.all_gather(attended, 'wid', axis=0, tiled=False)  50.7 us
    all_to_all x1, waiting for transfers between devices, body(): lax.all_to_all(w_copies, 'tok', split_axis=0, concat_axis=0, tiled=True)  28.6 us
    pallas_call x1, Pallas kernels, attention(): pl.pallas_call(attention_kernel, grid=(rows // block,), in_specs=[pl.Bloc...  18.9 us
    all_to_all x1, blocking collectives, body(): lax.all_to_all(w_late, 'wid', split_axis=1, concat_axis=0, tiled=True)  16.1 us
    all_gather x1, waiting for transfers between devices, body(): key_values = lax.all_gather(key_rows, 'tok', axis=0, tiled=True)  12.3 us
    all_to_all x1, starting transfers between devices, body(): lax.all_to_all(mod_copies, 'wid', split_axis=0, concat_axis=0, tiled=True)  7.57 us
    pallas_call x1, Pallas kernels, project(): pl.pallas_call(project_kernel, grid=(rows // block,), in_specs=[pl.BlockS...  7.54 us
    all_to_all x1, starting transfers between devices, body(): lax.all_to_all(w_copies, 'tok', split_axis=0, concat_axis=0, tiled=True)  7.31 us
  transfers between devices with their start and end apart: 5, of which 4 were waited for; matrix products, arithmetic and copies ran while one was open for 10% of the time, Pallas kernels for 0%

profile of v18, /device:TPU:1, one launch (start us, length us, event | category | flops | bytes accessed | tf_op | source)
XLA Modules:
  0.0 194.5 jit_solution(5068966771931262769)
XLA Ops:
  6.5 0.7 convert_element_type.18
  7.3 1.8 multiply_add_fusion
  9.9 0.3 fusion.7
  10.3 0.6 broadcast_in_dim.4
  10.9 7.6 %all-to-all-start = ((bf16[16,2,192]{2,1,0:T(2,128)(2,1)}), bf16[16,2,192]{2,1,0:T(2,128)(2,1)S(1)}, u32[]{:S(2)}, u32[]{:S(2)}) async-start(bf16[16,2,192]{2,1,0:T(2,128)(2,1)} %broadcast_in_dim.4), calls=%async_computation | async-start | bytes 32768 | tf_op jit(solution)/shard_map/all_to_all | solution.py:129
  18.5 1.2 copy.28
  19.6 5.3 %all-to-all-done = bf16[16,2,192]{2,1,0:T(2,128)(2,1)S(1)} async-done(((bf16[16,2,192]{2,1,0:T(2,128)(2,1)}), bf16[16,2,192]{2,1,0:T(2,128)(2,1)S(1)}, u32[]{:S(2)}, u32[]{:S(2)}) %all-to-all-start) | async-done | bytes 12320 | tf_op jit(solution)/shard_map/all_to_all | solution.py:129
  24.9 1.8 broadcast_in_dim.5
  26.7 7.3 %all-to-all-start.1 = ((bf16[8,384,3,128]{1,3,2,0:T(8,128)(2,1)}), bf16[8,384,3,128]{1,3,2,0:T(8,128)(2,1)S(1)}, u32[]{:S(2)}, u32[]{:S(2)}) async-start(bf16[8,384,3,128]{1,3,2,0:T(8,128)(2,1)} %broadcast_in_dim.5), calls=%async_computation.1 | async-start | bytes 4718592 | tf_op jit(solution)/shard_map/all_to_all | solution.py:114
  34.0 0.4 copy.27
  34.5 28.6 %all-to-all-done.1 = bf16[8,384,3,128]{1,3,2,0:T(8,128)(2,1)S(1)} async-done(((bf16[8,384,3,128]{1,3,2,0:T(8,128)(2,1)}), bf16[8,384,3,128]{1,3,2,0:T(8,128)(2,1)S(1)}, u32[]{:S(2)}, u32[]{:S(2)}) %all-to-all-start.1) | async-done | bytes 2359328 | tf_op jit(solution)/shard_map/all_to_all | solution.py:114
  63.0 3.8 %copy.38 = bf16[8,384,3,128]{3,2,1,0:T(4,128)(2,1)} copy(bf16[8,384,3,128]{1,3,2,0:T(8,128)(2,1)S(1)} %all-to-all-done.1) | data formatting | bytes 4718592 | tf_op jit(solution)/shard_map/reshape;reshape | solution.py:131
  66.9 2.3 %copy.50 = bf16[384,8,3,128]{3,1,2,0:T(8,128)(2,1)S(1)} copy(bf16[384,8,3,128]{3,2,1,0:T(4,128)(2,1)} %bitcast.48) | data formatting | bytes 4718592
  69.2 0.9 slice.22.kv_init
  70.1 0.7 slice.21.q_init
  70.8 2.6 %copy.32 = bf16[8,384,3,128]{3,1,0,2:T(8,128)(2,1)} copy(bf16[8,384,3,128]{1,3,2,0:T(8,128)(2,1)S(1)} %all-to-all-done.1) | data formatting | bytes 4718592 | tf_op jit(solution)/shard_map/all_to_all | solution.py:114
  73.4 2.8 %copy.33 = bf16[3072,3,128]{0,2,1:T(8,128)(2,1)S(1)} copy(bf16[3072,3,128]{2,0,1:T(8,128)(2,1)} %bitcast.49) | data formatting | bytes 4718592 | tf_op jit(solution)/shard_map/optimization_barrier | solution.py:134
  76.2 7.5 %shard_map.73 = (bf16[1024,128]{1,0:T(8,128)(2,1)}, bf16[1024,256]{1,0:T(8,128)(2,1)}) custom-call(bf16[3072,1024]{1,0:T(8,128)(2,1)} %bitcast.50, bf16[3072,2]{1,0:T(8,128)(2,1)S(1)} %bitcast.47, bf16[384,3072]{1,0:T(8,128)(2,1)S(1)} %bitcast.46, bf16[1024,128]{1,0:T(8,128)(2,1)} %slice.21.q_init, ...), custom_call_target="tpu_custom_call", output_to_operand_aliasing={{0}: (3, {}), {1}: (4, {})} | custom-call | flops 2447376384 | bytes 9437184 | tf_op jit(solution)/shard_map/pallas_call | solution.py:42
  83.9 1.5 copy.34
  85.4 16.1 %all_to_all.29 = bf16[128,16,192]{0,2,1:T(8,128)(2,1)S(1)} all-to-all(bf16[128,16,192]{0,2,1:T(8,128)(2,1)S(1)} %bitcast.53), channel_id=1, replica_groups=mesh['tok'=8,'wid'=16] {'wid'}, dimensions={1} | all-to-all | bytes 1572864 | tf_op jit(solution)/shard_map/all_to_all | solution.py:138
  101.6 12.3 %all-gather.7.cloned.1.call-done.kv_ref = bf16[8192,256]{1,0:T(8,128)(2,1)} async-done(((bf16[1024,256]{1,0:T(8,128)(2,1)}), bf16[8192,256]{1,0:T(8,128)(2,1)}) %all-gather.7.cloned.1.call-update) | async-done | bytes 4194320 | tf_op jit(solution)/shard_map/all_gather | solution.py:140
  113.9 18.9 %shard_map.74 = bf16[1024,128]{1,0:T(8,128)(2,1)} custom-call(bf16[1024,128]{1,0:T(8,128)(2,1)} %get-tuple-element.20.q_ref, bf16[8192,256]{1,0:T(8,128)(2,1)} %all-gather.7.cloned.1.call-done.kv_ref), custom_call_target="tpu_custom_call" | custom-call | flops 4294967296 | bytes 4718592 | tf_op jit(solution)/shard_map/pallas_call | solution.py:91
  132.9 50.7 %all-gather.9.cloned.1.call-done = bf16[16384,128]{1,0:T(8,128)(2,1)} async-done(((bf16[1024,128]{1,0:T(8,128)(2,1)}), bf16[16384,128]{1,0:T(8,128)(2,1)}) %all-gather.9.cloned.1.call-update) | async-done | bytes 4194320 | tf_op jit(solution)/shard_map/all_gather | solution.py:143
  183.6 4.5 %fusion.2 = bf16[1024,192]{0,1:T(8,128)(2,1)} fusion(bf16[16,1024,128]{2,1,0:T(8,128)(2,1)} %bitcast.59, bf16[1024,192]{0,1:T(8,128)(2,1)S(1)} %copy-done.1, f32[192]{0:T(256)S(1)} %bitcast.58, bf16[2048,192]{0,1:T(8,128)(2,1)S(1)} %copy_bitcast_fusion.1), kind=kOutput, calls=%fused_computation.4 | convolution fusion | flops 806092800 | bytes 5767936 | tf_op jit(solution)/shard_map/htd,hdc->tc/dot_general | solution.py:144
  (17 shorter events, 0.3 us)
Async XLA Ops:
  6.5 3.3 %copy-start = (bf16[256,3,192]{0,2,1:T(8,128)(2,1)S(1)}, bf16[256,3,192]{0,2,1:T(8,128)(2,1)}, u32[]{:S(2)}) copy-start(bf16[256,3,192]{0,2,1:T(8,128)(2,1)} %param.11) | copy-start | bytes 884740
  6.5 69.7 %all-gather.5.cloned.1.call-start = ((), (), s32[]{:S(2)}) async-start(), calls=%async_computation.3 | async-start | bytes 6684672 | tf_op jit(solution)/shard_map/all_gather | solution.py:126
  10.9 14.0 %all-to-all-start = ((bf16[16,2,192]{2,1,0:T(2,128)(2,1)}), bf16[16,2,192]{2,1,0:T(2,128)(2,1)S(1)}, u32[]{:S(2)}, u32[]{:S(2)}) async-start(bf16[16,2,192]{2,1,0:T(2,128)(2,1)} %broadcast_in_dim.4), calls=%async_computation | async-start | bytes 32768 | tf_op jit(solution)/shard_map/all_to_all | solution.py:129
  26.7 36.3 %all-to-all-start.1 = ((bf16[8,384,3,128]{1,3,2,0:T(8,128)(2,1)}), bf16[8,384,3,128]{1,3,2,0:T(8,128)(2,1)S(1)}, u32[]{:S(2)}, u32[]{:S(2)}) async-start(bf16[8,384,3,128]{1,3,2,0:T(8,128)(2,1)} %broadcast_in_dim.5), calls=%async_computation.1 | async-start | bytes 4718592 | tf_op jit(solution)/shard_map/all_to_all | solution.py:114
  34.0 79.9 %all-gather.7.cloned.1.call-start = ((), (), s32[]{:S(2)}) async-start(), calls=%async_computation.4 | async-start | bytes 4718592 | tf_op jit(solution)/shard_map/all_gather | solution.py:140
  83.8 99.7 %all-gather.9.cloned.1.call-start = ((), (), s32[]{:S(2)}) async-start(), calls=%async_computation.5 | async-start | bytes 4456448 | tf_op jit(solution)/shard_map/all_gather | solution.py:143
  101.6 81.9 %copy-start.1 = (bf16[1024,192]{0,1:T(8,128)(2,1)S(1)}, bf16[1024,192]{0,1:T(8,128)(2,1)}, u32[]{:S(2)}) copy-start(bf16[1024,192]{0,1:T(8,128)(2,1)} %multiply_add_fusion) | copy-start | bytes 1179652
Sparse Core Ops, SparseCore 0:
  9.5 64.1 all-gather.4
  83.9 29.9 all-gather.6
  133.0 50.4 all-gather.8

commit v19 on v18

--- a/solution.py
+++ b/solution.py
@@ -31,7 +31,7 @@
     scale_col = mod_ref[:, 1:2].astype(jnp.float32)
     normed = (normal * (1.0 + scale_col) + shift_col).astype(jnp.bfloat16)
     qkv_t = jnp.dot(w_ref[...], normed, preferred_element_type=jnp.float32)
-    qkv = jnp.transpose(qkv_t).astype(jnp.bfloat16)
+    qkv = jnp.transpose(qkv_t.astype(jnp.bfloat16))
     q_ref[...] = qkv[:, :DH]
     kv_ref[...] = qkv[:, DH:]
 

time: 195 us -> 195 us (level)
  no operation moved by 1% of the time
where the time goes in v19:
time: 195 us; the launch traced here: 194 us
  waiting for transfers between devices  96.9 us (50%)
  Pallas kernels  26.4 us (14%)
  local copies, waits for them, and re-layouts  18.9 us (10%)
  blocking collectives  16.1 us (8%)
  starting transfers between devices  14.9 us (8%)
  between operations  13.8 us (7%)
  matrix products  4.8 us (2%)
  other arithmetic  2.65 us (1%)
    all_gather x1, waiting for transfers between devices, body(): heads = lax.all_gather(attended, 'wid', axis=0, tiled=False)  50.7 us
    all_to_all x1, waiting for transfers between devices, body(): lax.all_to_all(w_copies, 'tok', split_axis=0, concat_axis=0, tiled=True)  28.6 us
    pallas_call x1, Pallas kernels, attention(): pl.pallas_call(attention_kernel, grid=(rows // block,), in_specs=[pl.Bloc...  18.9 us
    all_to_all x1, blocking collectives, body(): lax.all_to_all(w_late, 'wid', split_axis=1, concat_axis=0, tiled=True)  16.1 us
    all_gather x1, waiting for transfers between devices, body(): key_values = lax.all_gather(key_rows, 'tok', axis=0, tiled=True)  12.3 us
    all_to_all x1, starting transfers between devices, body(): lax.all_to_all(mod_copies, 'wid', split_axis=0, concat_axis=0, tiled=True)  7.57 us
    pallas_call x1, Pallas kernels, project(): pl.pallas_call(project_kernel, grid=(rows // block,), in_specs=[pl.BlockS...  7.43 us
    all_to_all x1, starting transfers between devices, body(): lax.all_to_all(w_copies, 'tok', split_axis=0, concat_axis=0, tiled=True)  7.31 us
  transfers between devices with their start and end apart: 5, of which 4 were waited for; matrix products, arithmetic and copies ran while one was open for 10% of the time, Pallas kernels for 0%

profile of v19, /device:TPU:1, one launch (start us, length us, event | category | flops | bytes accessed | tf_op | source)
XLA Modules:
  0.0 194.4 jit_solution(4885836558046375623)
XLA Ops:
  6.5 0.7 convert_element_type.18
  7.3 1.8 multiply_add_fusion
  9.9 0.3 fusion.7
  10.3 0.6 broadcast_in_dim.4
  10.9 7.6 %all-to-all-start = ((bf16[16,2,192]{2,1,0:T(2,128)(2,1)}), bf16[16,2,192]{2,1,0:T(2,128)(2,1)S(1)}, u32[]{:S(2)}, u32[]{:S(2)}) async-start(bf16[16,2,192]{2,1,0:T(2,128)(2,1)} %broadcast_in_dim.4), calls=%async_computation | async-start | bytes 32768 | tf_op jit(solution)/shard_map/all_to_all | solution.py:129
  18.5 1.2 copy.28
  19.6 5.3 %all-to-all-done = bf16[16,2,192]{2,1,0:T(2,128)(2,1)S(1)} async-done(((bf16[16,2,192]{2,1,0:T(2,128)(2,1)}), bf16[16,2,192]{2,1,0:T(2,128)(2,1)S(1)}, u32[]{:S(2)}, u32[]{:S(2)}) %all-to-all-start) | async-done | bytes 12320 | tf_op jit(solution)/shard_map/all_to_all | solution.py:129
  24.9 1.8 broadcast_in_dim.5
  26.7 7.3 %all-to-all-start.1 = ((bf16[8,384,3,128]{1,3,2,0:T(8,128)(2,1)}), bf16[8,384,3,128]{1,3,2,0:T(8,128)(2,1)S(1)}, u32[]{:S(2)}, u32[]{:S(2)}) async-start(bf16[8,384,3,128]{1,3,2,0:T(8,128)(2,1)} %broadcast_in_dim.5), calls=%async_computation.1 | async-start | bytes 4718592 | tf_op jit(solution)/shard_map/all_to_all | solution.py:114
  34.0 0.4 copy.27
  34.5 28.6 %all-to-all-done.1 = bf16[8,384,3,128]{1,3,2,0:T(8,128)(2,1)S(1)} async-done(((bf16[8,384,3,128]{1,3,2,0:T(8,128)(2,1)}), bf16[8,384,3,128]{1,3,2,0:T(8,128)(2,1)S(1)}, u32[]{:S(2)}, u32[]{:S(2)}) %all-to-all-start.1) | async-done | bytes 2359328 | tf_op jit(solution)/shard_map/all_to_all | solution.py:114
  63.0 3.8 %copy.38 = bf16[8,384,3,128]{3,2,1,0:T(4,128)(2,1)} copy(bf16[8,384,3,128]{1,3,2,0:T(8,128)(2,1)S(1)} %all-to-all-done.1) | data formatting | bytes 4718592 | tf_op jit(solution)/shard_map/reshape;reshape | solution.py:131
  66.9 2.3 %copy.50 = bf16[384,8,3,128]{3,1,2,0:T(8,128)(2,1)S(1)} copy(bf16[384,8,3,128]{3,2,1,0:T(4,128)(2,1)} %bitcast.48) | data formatting | bytes 4718592
  69.2 0.9 slice.22.kv_init
  70.1 0.7 slice.21.q_init
  70.8 2.6 %copy.32 = bf16[8,384,3,128]{3,1,0,2:T(8,128)(2,1)} copy(bf16[8,384,3,128]{1,3,2,0:T(8,128)(2,1)S(1)} %all-to-all-done.1) | data formatting | bytes 4718592 | tf_op jit(solution)/shard_map/all_to_all | solution.py:114
  73.4 2.8 %copy.33 = bf16[3072,3,128]{0,2,1:T(8,128)(2,1)S(1)} copy(bf16[3072,3,128]{2,0,1:T(8,128)(2,1)} %bitcast.49) | data formatting | bytes 4718592 | tf_op jit(solution)/shard_map/optimization_barrier | solution.py:134
  76.2 7.4 %shard_map.73 = (bf16[1024,128]{1,0:T(8,128)(2,1)}, bf16[1024,256]{1,0:T(8,128)(2,1)}) custom-call(bf16[3072,1024]{1,0:T(8,128)(2,1)} %bitcast.50, bf16[3072,2]{1,0:T(8,128)(2,1)S(1)} %bitcast.47, bf16[384,3072]{1,0:T(8,128)(2,1)S(1)} %bitcast.46, bf16[1024,128]{1,0:T(8,128)(2,1)} %slice.21.q_init, ...), custom_call_target="tpu_custom_call", output_to_operand_aliasing={{0}: (3, {}), {1}: (4, {})} | custom-call | flops 2447376384 | bytes 9437184 | tf_op jit(solution)/shard_map/pallas_call | solution.py:42
  83.7 1.5 copy.34
  85.3 16.1 %all_to_all.29 = bf16[128,16,192]{0,2,1:T(8,128)(2,1)S(1)} all-to-all(bf16[128,16,192]{0,2,1:T(8,128)(2,1)S(1)} %bitcast.53), channel_id=1, replica_groups=mesh['tok'=8,'wid'=16] {'wid'}, dimensions={1} | all-to-all | bytes 1572864 | tf_op jit(solution)/shard_map/all_to_all | solution.py:138
  101.5 12.3 %all-gather.7.cloned.1.call-done.kv_ref = bf16[8192,256]{1,0:T(8,128)(2,1)} async-done(((bf16[1024,256]{1,0:T(8,128)(2,1)}), bf16[8192,256]{1,0:T(8,128)(2,1)}) %all-gather.7.cloned.1.call-update) | async-done | bytes 4194320 | tf_op jit(solution)/shard_map/all_gather | solution.py:140
  113.8 18.9 %shard_map.74 = bf16[1024,128]{1,0:T(8,128)(2,1)} custom-call(bf16[1024,128]{1,0:T(8,128)(2,1)} %get-tuple-element.20.q_ref, bf16[8192,256]{1,0:T(8,128)(2,1)} %all-gather.7.cloned.1.call-done.kv_ref), custom_call_target="tpu_custom_call" | custom-call | flops 4294967296 | bytes 4718592 | tf_op jit(solution)/shard_map/pallas_call | solution.py:91
  132.8 50.7 %all-gather.9.cloned.1.call-done = bf16[16384,128]{1,0:T(8,128)(2,1)} async-done(((bf16[1024,128]{1,0:T(8,128)(2,1)}), bf16[16384,128]{1,0:T(8,128)(2,1)}) %all-gather.9.cloned.1.call-update) | async-done | bytes 4194320 | tf_op jit(solution)/shard_map/all_gather | solution.py:143
  183.4 4.5 %fusion.2 = bf16[1024,192]{0,1:T(8,128)(2,1)} fusion(bf16[16,1024,128]{2,1,0:T(8,128)(2,1)} %bitcast.59, bf16[1024,192]{0,1:T(8,128)(2,1)S(1)} %copy-done.1, f32[192]{0:T(256)S(1)} %bitcast.58, bf16[2048,192]{0,1:T(8,128)(2,1)S(1)} %copy_bitcast_fusion.1), kind=kOutput, calls=%fused_computation.4 | convolution fusion | flops 806092800 | bytes 5767936 | tf_op jit(solution)/shard_map/htd,hdc->tc/dot_general | solution.py:144
  (17 shorter events, 0.3 us)
Async XLA Ops:
  6.5 3.3 %copy-start = (bf16[256,3,192]{0,2,1:T(8,128)(2,1)S(1)}, bf16[256,3,192]{0,2,1:T(8,128)(2,1)}, u32[]{:S(2)}) copy-start(bf16[256,3,192]{0,2,1:T(8,128)(2,1)} %param.11) | copy-start | bytes 884740
  6.5 69.7 %all-gather.5.cloned.1.call-start = ((), (), s32[]{:S(2)}) async-start(), calls=%async_computation.3 | async-start | bytes 6684672 | tf_op jit(solution)/shard_map/all_gather | solution.py:126
  10.9 14.0 %all-to-all-start = ((bf16[16,2,192]{2,1,0:T(2,128)(2,1)}), bf16[16,2,192]{2,1,0:T(2,128)(2,1)S(1)}, u32[]{:S(2)}, u32[]{:S(2)}) async-start(bf16[16,2,192]{2,1,0:T(2,128)(2,1)} %broadcast_in_dim.4), calls=%async_computation | async-start | bytes 32768 | tf_op jit(solution)/shard_map/all_to_all | solution.py:129
  26.7 36.3 %all-to-all-start.1 = ((bf16[8,384,3,128]{1,3,2,0:T(8,128)(2,1)}), bf16[8,384,3,128]{1,3,2,0:T(8,128)(2,1)S(1)}, u32[]{:S(2)}, u32[]{:S(2)}) async-start(bf16[8,384,3,128]{1,3,2,0:T(8,128)(2,1)} %broadcast_in_dim.5), calls=%async_computation.1 | async-start | bytes 4718592 | tf_op jit(solution)/shard_map/all_to_all | solution.py:114
  34.0 79.8 %all-gather.7.cloned.1.call-start = ((), (), s32[]{:S(2)}) async-start(), calls=%async_computation.4 | async-start | bytes 4718592 | tf_op jit(solution)/shard_map/all_gather | solution.py:140
  83.7 99.8 %all-gather.9.cloned.1.call-start = ((), (), s32[]{:S(2)}) async-start(), calls=%async_computation.5 | async-start | bytes 4456448 | tf_op jit(solution)/shard_map/all_gather | solution.py:143
  101.5 81.9 %copy-start.1 = (bf16[1024,192]{0,1:T(8,128)(2,1)S(1)}, bf16[1024,192]{0,1:T(8,128)(2,1)}, u32[]{:S(2)}) copy-start(bf16[1024,192]{0,1:T(8,128)(2,1)} %multiply_add_fusion) | copy-start | bytes 1179652
Sparse Core Ops, SparseCore 0:
  9.5 64.1 all-gather.4
  83.8 29.9 all-gather.6
  132.9 50.4 all-gather.8
